TPU v7x, 128 devices: a whole 4x4x4 slice. The times are simulated.
128 devices in a mesh: wide: 32 (over x, y, core), narrow: 4 (over z).
Axes of the slice: x: 4, y: 4, z: 4, core: 2. Of those that a mesh axis runs over, the one named last changes fastest.
Arguments:
- raw_samples: bfloat16 [1024, 32, 16384], P(('wide', 'narrow')), as said below
- filter_taps: float32 [64], replicated, may hold values from -0.75 to 0.75
- tile_pairs: int32 [16, 2], replicated, may hold values from 0 to 127, as said below
- tile_owners: int32 [16], replicated, may hold values from 0 to 3, as said below
Outputs:
- correlation_stacks: float32 [32, 64, 512], P('narrow', 'wide')
Inputs may be any that keep to these rules, and one draw needn't show every extreme that they name: `raw_samples`: noise samples, scaled per channel and per window. `tile_pairs`: each row is (source block, receiver block), and the two blocks differ. `tile_owners`: each owner has at most 8 tiles, and some owner has exactly 8.
All inputs are finite; a program needn't handle non-finite values.
Results may differ from a plain program's by a relative error of at most 0.0074.
Values may be sent and summed in bfloat16 or wider, within the bound.
No kernel may reach another device: no remote copies, remote signals or barrier semaphores. Data moves between devices by JAX's collectives and lax.ppermute only.
A program may use at most 128 MiB of HBM per device.

v0:
```python
import math

import jax
import jax.numpy as jnp
from jax import lax
from jax.experimental import pallas as pl
from jax.experimental.pallas import tpu as pltpu
from jax.sharding import PartitionSpec as P

NFFT = 4096
DECIM = 4
NBINS = 1024
SMOOTH = 63
LAGS = 512
BLK = 8
SLOTS = 8
TAPS = 64

water_level = 0.2
epsilon = 1e-06


def fir_table(filter_taps, block_size):
    taps = filter_taps.astype(jnp.bfloat16)
    span = filter_taps.shape[0] // DECIM
    cols = 2 * block_size
    width = cols + 1
    phase = taps.reshape(span, DECIM)[:, ::-1].T
    padded = jnp.pad(phase, ((0, 0), (0, width - span)))
    shifted = jnp.tile(padded, (1, block_size))[:, : block_size * cols]
    shifted = shifted.reshape(DECIM, block_size, cols)
    return jnp.transpose(shifted, (1, 0, 2)).reshape(DECIM * block_size, cols)


def decimate(samples, filter_taps):
    row_count, row_length = samples.shape
    block_size = min(128, row_length // DECIM)
    table = fir_table(filter_taps, block_size)
    segments = samples.reshape(-1, DECIM * block_size)
    both = jnp.dot(segments, table, preferred_element_type=jnp.float32).reshape(
        row_count, -1, 2 * block_size
    )
    current = both[:, :, :block_size]
    spilled = both[:, :, block_size:]
    spilled = jnp.pad(spilled[:, :-1], ((0, 0), (1, 0), (0, 0)))
    return (current + spilled).reshape(row_count, -1).astype(jnp.bfloat16)


def trig(index, modulus):
    angle = (index % modulus).astype(jnp.float32) * (2.0 * math.pi / modulus)
    return jnp.cos(angle), jnp.sin(angle)


LO = 128


def dft_factors(point_count, bin_count, group):
    hi = jnp.arange(point_count // LO, dtype=jnp.int32)[None, :]
    lo = jnp.arange(LO, dtype=jnp.int32)[None, :]
    frequency = 1 + jnp.arange(bin_count, dtype=jnp.int32)[:, None]
    c1, s1 = trig(frequency * hi * LO, point_count)
    c2, s2 = trig(frequency * lo, point_count)
    slices = bin_count // group

    def rows(real_rows, imag_rows):
        width = real_rows.shape[1]
        real_rows = real_rows.reshape(slices, 1, group, width)
        imag_rows = imag_rows.reshape(slices, 1, group, width)
        return jnp.concatenate([real_rows, imag_rows], axis=1).reshape(2 * bin_count, width)

    return rows(c1, -s1), rows(-s1, -c1), rows(c2, c2), rows(s2, s2)


def dft_kernel(p_ref, q_ref, c_ref, s_ref, dec_ref, out_ref, tab_ref):
    c2 = c_ref[...]
    s2 = s_ref[...]
    p_all = p_ref[...]
    q_all = q_ref[...]
    for hi in range(p_ref.shape[1]):
        value = p_all[:, hi : hi + 1] * c2 + q_all[:, hi : hi + 1] * s2
        tab_ref[:, hi * LO : (hi + 1) * LO] = value.astype(jnp.bfloat16)
    out_ref[...] = lax.dot_general(
        tab_ref[...], dec_ref[...], (((1,), (1,)), ((), ())), preferred_element_type=jnp.float32
    )


def dft_t(decimated, group, block_rows=256):
    rows, points = decimated.shape
    p, q, c, s = dft_factors(points, NBINS, group)
    out_rows = p.shape[0]
    hi_count = p.shape[1]
    return pl.pallas_call(
        dft_kernel,
        grid=(out_rows // block_rows,),
        in_specs=[
            pl.BlockSpec((block_rows, hi_count), lambda i: (i, 0)),
            pl.BlockSpec((block_rows, hi_count), lambda i: (i, 0)),
            pl.BlockSpec((block_rows, LO), lambda i: (i, 0)),
            pl.BlockSpec((block_rows, LO), lambda i: (i, 0)),
            pl.BlockSpec((rows, points), lambda i: (0, 0)),
        ],
        out_specs=pl.BlockSpec((block_rows, rows), lambda i: (i, 0)),
        out_shape=jax.ShapeDtypeStruct((out_rows, rows), jnp.float32),
        scratch_shapes=[pltpu.VMEM((block_rows, points), jnp.bfloat16)],
    )(p, q, c, s, decimated)


def lag_transform(cross, point_count, lag_count, window_count):
    split = 64
    pairs, _, bin_count = cross.shape
    frequency = 1 + jnp.arange(bin_count, dtype=jnp.int32)
    hi = jnp.arange(lag_count // split, dtype=jnp.int32)[:, None]
    lo = jnp.arange(split, dtype=jnp.int32)[None, :]
    ca, sa = trig(frequency[None, :] * (point_count - lag_count // 2 + split * hi), point_count)
    cb, sb = trig(frequency[:, None] * lo, point_count)
    weight = 1.0 / math.sqrt(window_count * bin_count)
    xr = cross[:, 0][:, None, :]
    xi = cross[:, 1][:, None, :]
    u = xr * ca[None] - xi * sa[None]
    v = xr * sa[None] + xi * ca[None]
    uv = jnp.concatenate([u, v], axis=2).reshape(pairs * (lag_count // split), 2 * bin_count)
    table = jnp.concatenate([cb, -sb], axis=0) * weight
    out = jnp.dot(uv, table, precision=lax.Precision.HIGHEST)
    return out.reshape(pairs, lag_count)


def smoother(bin_count, span_width):
    bin_index = jnp.arange(bin_count, dtype=jnp.int32)
    nearby = (jnp.abs(bin_index[:, None] - bin_index[None, :]) <= (span_width - 1) // 2).astype(
        jnp.float32
    )
    return nearby / jnp.sum(nearby, axis=0, keepdims=True)


def whiten_t(decimated, slices, group):
    rows = decimated.shape[0]
    spec = dft_t(decimated, group).reshape(slices, 2, group, rows)
    real_part = spec[:, 0].reshape(NBINS, rows)
    imag_part = spec[:, 1].reshape(NBINS, rows)
    magnitude = jnp.sqrt(real_part * real_part + imag_part * imag_part)
    smooth = lax.dot_general(
        smoother(NBINS, SMOOTH),
        magnitude,
        (((0,), (0,)), ((), ())),
        precision=lax.Precision.HIGHEST,
    )
    floor_level = water_level * jnp.mean(smooth, axis=0, keepdims=True) + epsilon
    factor = (1.0 / (smooth + floor_level)).reshape(slices, 1, group, rows)
    return (spec * factor).astype(jnp.bfloat16).reshape(slices, 2 * group, rows)


def on_device(raw_samples, filter_taps, tile_pairs, tile_owners):
    wide_count = lax.axis_size("wide")
    narrow_count = lax.axis_size("narrow")
    devices = wide_count * narrow_count
    chan_dev, window_total, _ = raw_samples.shape
    assert chan_dev == BLK
    group = NBINS // devices
    rows = chan_dev * window_total

    decimated = decimate(raw_samples.reshape(rows, -1), filter_taps)
    whitened = whiten_t(decimated, devices, group)
    spectra = lax.all_to_all(whitened, ("wide", "narrow"), 0, 0, tiled=True)

    source = jnp.take(spectra, tile_pairs[:, 0], axis=0)
    target = jnp.take(spectra, tile_pairs[:, 1], axis=0)
    tiles = tile_pairs.shape[0]
    source = source.reshape(tiles, 2, group, BLK, window_total)
    target = target.reshape(tiles, 2, group, BLK, window_total)
    src_real, src_imag = source[:, 0], source[:, 1]
    dst_real, dst_imag = target[:, 0], target[:, 1]

    def mm(a, b):
        return jnp.einsum("tbiw,tbjw->tbij", a, b, preferred_element_type=jnp.float32)

    real_sum = mm(src_real, dst_real) + mm(src_imag, dst_imag)
    imag_sum = mm(src_real, dst_imag) - mm(src_imag, dst_real)
    cross = jnp.stack([real_sum, imag_sum], axis=1)
    pair_share = BLK * BLK // wide_count
    cross = cross.reshape(tiles, 2 * group, BLK * BLK // pair_share, pair_share)
    cross = jnp.transpose(cross, (0, 2, 3, 1))

    slot_ids = jnp.arange(SLOTS, dtype=jnp.int32)
    owner_ids = jnp.arange(narrow_count, dtype=jnp.int32)
    owned_all = tile_owners[None, :] == owner_ids[:, None]
    rank_all = jnp.cumsum(owned_all.astype(jnp.int32), axis=1) - 1
    select_all = (owned_all[:, None, :] & (rank_all[:, None, :] == slot_ids[None, :, None])).astype(
        jnp.float32
    )
    send = jnp.einsum("nst,twqv->wnsqv", select_all, cross, precision=lax.Precision.HIGHEST)
    send = send.reshape(devices, SLOTS * pair_share * 2 * group)
    arrived = lax.all_to_all(send, ("wide", "narrow"), 0, 0, tiled=True)
    arrived = arrived.reshape(devices, SLOTS * pair_share, 2, group)
    arrived = jnp.transpose(arrived, (1, 2, 0, 3)).reshape(SLOTS * pair_share, 2, NBINS)
    stacked = lag_transform(arrived, NFFT, LAGS, window_total)
    return stacked.reshape(SLOTS, pair_share, LAGS)


def solution(mesh):
    in_specs = (P(("wide", "narrow"), None, None), P(), P(), P())
    out_specs = P("narrow", "wide", None)
    return jax.shard_map(
        on_device, mesh=mesh, in_specs=in_specs, out_specs=out_specs, check_vma=False
    )
```

profile of v0, /device:TPU:1, one launch (start us, length us, event | category | flops | bytes accessed | tf_op | source)
XLA Modules:
  0.0 137.3 jit_solution(12952334249614056203)
XLA Ops:
  0.0 0.5 fusion.40
  0.9 1.4 %copy.42 = f32[128,2,8,32]{3,2,1,0:T(8,128)} copy(f32[128,2,8,32]{0,3,2,1:T(8,128)S(1)} %get-tuple-element.15) | data formatting | bytes 524288 | tf_op jit(solution)/shard_map/concatenate | solution.py:69
  2.3 1.4 %copy.43 = f32[128,2,8,32]{3,2,1,0:T(8,128)} copy(f32[128,2,8,32]{0,3,2,1:T(8,128)S(1)} %get-tuple-element.14) | data formatting | bytes 524288 | tf_op jit(solution)/shard_map/concatenate | solution.py:69
  3.7 2.1 %fusion.32 = (f32[128,1,8,128]{3,2,1,0:T(8,128)S(1)}, f32[128,1,8,128]{3,2,1,0:T(8,128)S(1)}) fusion(s32[128,8]{1,0:T(8,128)S(1)} %copy.44), kind=kLoop, calls=%fused_computation.67 | loop fusion | flops 1835008 | bytes 1052672 | tf_op jit(solution)/shard_map/sin | solution.py:51
  5.8 13.5 %reshape_reshape.6 = bf16[8192,512]{1,0:T(8,128)(2,1)} reshape(bf16[8,32,16384]{2,1,0:T(8,128)(2,1)} %param.6) | data formatting | bytes 16777216 | tf_op jit(solution)/shard_map/reshape;reshape | solution.py:39
  19.6 0.8 tile.10
  20.6 9.0 %convolution_bitcast_fusion = f32[8192,256]{0,1:T(8,128)} fusion(bf16[512,256]{1,0:T(8,128)(2,1)S(1)} %reshape.391, bf16[8192,512]{1,0:T(8,128)(2,1)} %reshape_reshape.6), kind=kOutput, calls=%fused_computation.2 | convolution fusion | flops 2147483648 | bytes 17039360 | tf_op jit(solution)/shard_map/dot_general | solution.py:40
  29.6 9.0 %copy.47 = f32[8192,256]{1,0:T(8,128)} copy(f32[8192,256]{0,1:T(8,128)} %convolution_bitcast_fusion) | data formatting | bytes 16777216 | tf_op jit(solution)/shard_map/dot_general | solution.py:40
  38.5 2.8 %slice.60 = f32[256,31,128]{2,1,0:T(8,128)S(1)} slice(f32[256,32,256]{2,1,0:T(8,128)} %bitcast.91), slice={[0:256], [0:31], [128:256]} | slice | bytes 8126464 | tf_op jit(solution)/shard_map/slice | solution.py:45
  41.4 1.8 %copy-done = f32[8192,256]{1,0:T(8,128)S(1)} copy-done((f32[8192,256]{1,0:T(8,128)S(1)}, f32[8192,256]{1,0:T(8,128)}, u32[]{:S(2)}) %copy-start) | copy-done | bytes 8388632
  43.2 0.8 fusion
  44.0 2.3 %copy.71 = bf16[32,8,32,128]{3,1,2,0:T(8,128)(2,1)} copy(bf16[32,8,32,128]{3,2,1,0:T(8,128)(2,1)S(1)} %bitcast.93) | data formatting | bytes 4194304
  46.3 1.5 %pad_maximum_fusion = (f32[128,2,8,128]{3,2,1,0:T(8,128)}, f32[128,2,8,128]{3,2,1,0:T(8,128)}) fusion(f32[128,1,8,128]{3,2,1,0:T(8,128)S(1)} %get-tuple-element.17, f32[128,1,8,128]{3,2,1,0:T(8,128)S(1)} %get-tuple-element.16), kind=kLoop, calls=%fused_computation.24 | loop fusion | flops 524288 | bytes 3145728 | tf_op jit(solution)/shard_map/concatenate | solution.py:69
  47.8 23.3 %shard_map.46 = f32[2048,256]{1,0:T(8,128)} custom-call(f32[2048,32]{1,0:T(8,128)} %bitcast.100, f32[2048,32]{1,0:T(8,128)} %bitcast.101, f32[2048,128]{1,0:T(8,128)} %bitcast.98, f32[2048,128]{1,0:T(8,128)} %bitcast.99, bf16[256,4096]{1,0:T(8,128)(2,1)} %bitcast.96), custom_call_target="tpu_custom_call" | custom-call | tf_op jit(solution)/shard_map/pallas_call | solution.py:92
  71.1 8.7 %fusion.55 = (f32[256]{0:T(256)S(1)}, f32[1024,256]{1,0:T(8,128)S(1)}) fusion(f32[128,2,8,256]{3,2,1,0:T(8,128)} %bitcast.94, f32[1024]{0:T(1024)S(1)} %convert_reduce_fusion), kind=kOutput, calls=%fused_computation.113 | convolution fusion | flops 3227516672 | bytes 3150848 | tf_op jit(solution)/shard_map/dot_general | solution.py:141
  80.0 1.4 fusion.2
  81.4 11.5 %all-to-all-start = ((bf16[128,16,256]{2,1,0:T(8,128)(2,1)}), bf16[128,16,256]{2,1,0:T(8,128)(2,1)S(1)}, u32[]{:S(2)}, u32[]{:S(2)}) async-start(bf16[128,16,256]{2,1,0:T(8,128)(2,1)} %fusion.2), calls=%async_computation | async-start | bytes 2097152 | tf_op jit(solution)/shard_map/all_to_all | solution.py:163
  93.2 2.1 %fusion.31 = (f32[1024,64]{1,0:T(8,128)S(1)}, f32[1024,64]{1,0:T(8,128)S(1)}) fusion(s32[1024]{0:T(1024)S(1)} %iota_add_fusion), kind=kLoop, calls=%fused_computation.66 | loop fusion | flops 983040 | bytes 528384 | tf_op jit(solution)/shard_map/cos | solution.py:51
  95.3 17.1 %all-to-all-done = bf16[128,16,256]{2,1,0:T(8,128)(2,1)S(1)} async-done(((bf16[128,16,256]{2,1,0:T(8,128)(2,1)}), bf16[128,16,256]{2,1,0:T(8,128)(2,1)S(1)}, u32[]{:S(2)}, u32[]{:S(2)}) %all-to-all-start) | async-done | bytes 1048608 | tf_op jit(solution)/shard_map/all_to_all | solution.py:163
  112.4 0.6 gather_fusion.1
  113.3 0.6 gather_fusion
  114.8 0.3 fusion.6
  115.5 0.7 copy.52
  116.2 0.3 copy.53
  116.5 0.4 convolution_bitcast_fusion.1
  116.9 1.5 %copy.54 = f32[32,4,8,2,16]{4,3,2,1,0:T(2,128)S(1)} copy(f32[32,4,8,2,16]{0,2,1,4,3:T(8,128)S(1)} %convolution_bitcast_fusion.1) | data formatting | bytes 262144 | tf_op jit(solution)/shard_map/nst,twqv->wnsqv/transpose | solution.py:190
  118.4 2.1 %all_to_all.12 = f32[128,1,256]{2,1,0:T(1,128)} reshape(f32[32,4,8,2,16]{4,3,2,1,0:T(2,128)S(1)} %copy.54) | data formatting | bytes 262144 | tf_op jit(solution)/shard_map/all_to_all | solution.py:192
  120.5 3.9 %all-to-all-start.1 = ((f32[128,1,256]{2,1,0:T(1,128)}), f32[128,1,256]{2,1,0:T(1,128)S(1)}, u32[]{:S(2)}, u32[]{:S(2)}) async-start(f32[128,1,256]{2,1,0:T(1,128)} %all_to_all.12), calls=%async_computation.1 | async-start | bytes 262144 | tf_op jit(solution)/shard_map/all_to_all | solution.py:192
  124.6 9.6 %all-to-all-done.1 = f32[128,1,256]{2,1,0:T(1,128)S(1)} async-done(((f32[128,1,256]{2,1,0:T(1,128)}), f32[128,1,256]{2,1,0:T(1,128)S(1)}, u32[]{:S(2)}, u32[]{:S(2)}) %all-to-all-start.1) | async-done | bytes 131104 | tf_op jit(solution)/shard_map/all_to_all | solution.py:192
  134.4 0.4 copy.57
  135.4 1.2 fusion.11
  136.6 0.7 reshape_reshape.7
  (44 shorter events, 3.7 us)
Async XLA Ops:
  5.8 13.5 %copy-start.4 = (f32[64]{0:T(128)S(1)}, f32[64]{0:T(128)}, u32[]{:S(2)}) copy-start(f32[64]{0:T(128)} %param.7) | copy-start | bytes 772
  38.5 4.6 %copy-start = (f32[8192,256]{1,0:T(8,128)S(1)}, f32[8192,256]{1,0:T(8,128)}, u32[]{:S(2)}) copy-start(f32[8192,256]{1,0:T(8,128)} %copy.47) | copy-start | bytes 25165828
  71.1 8.9 %copy-start.1 = (f32[2048,256]{1,0:T(8,128)S(1)}, f32[2048,256]{1,0:T(8,128)}, u32[]{:S(2)}) copy-start(f32[2048,256]{1,0:T(8,128)} %shard_map.46) | copy-start | bytes 6291460
  79.8 13.1 %copy-start.3 = (s32[16]{0:T(128)S(1)}, s32[16]{0:T(128)}, u32[]{:S(2)}) copy-start(s32[16]{0:T(128)} %param.9) | copy-start | bytes 196
  79.9 13.3 %copy-start.2 = (s32[16,2]{0,1:T(2,128)S(1)}, s32[16,2]{0,1:T(2,128)}, u32[]{:S(2)}) copy-start(s32[16,2]{0,1:T(2,128)} %param.8) | copy-start | bytes 388
  81.4 31.0 %all-to-all-start = ((bf16[128,16,256]{2,1,0:T(8,128)(2,1)}), bf16[128,16,256]{2,1,0:T(8,128)(2,1)S(1)}, u32[]{:S(2)}, u32[]{:S(2)}) async-start(bf16[128,16,256]{2,1,0:T(8,128)(2,1)} %fusion.2), calls=%async_computation | async-start | bytes 2097152 | tf_op jit(solution)/shard_map/all_to_all | solution.py:163
  120.5 13.8 %all-to-all-start.1 = ((f32[128,1,256]{2,1,0:T(1,128)}), f32[128,1,256]{2,1,0:T(1,128)S(1)}, u32[]{:S(2)}, u32[]{:S(2)}) async-start(f32[128,1,256]{2,1,0:T(1,128)} %all_to_all.12), calls=%async_computation.1 | async-start | bytes 262144 | tf_op jit(solution)/shard_map/all_to_all | solution.py:192
where the time goes:
time: 138 us; the launch traced here: 137 us
  local copies, waits for them, and re-layouts  41.4 us (30%)
  waiting for transfers between devices  26.8 us (19%)
  Pallas kernels  23.3 us (17%)
  matrix products  20.4 us (15%)
  starting transfers between devices  15.4 us (11%)
  other arithmetic  9.68 us (7%)
    pallas_call x1, Pallas kernels, dft_t(): pl.pallas_call(dft_kernel, grid=(out_rows // block_rows,), in_specs=[pl.B...  23.3 us
    all_to_all x1, waiting for transfers between devices, on_device(): spectra = lax.all_to_all(whitened, ('wide', 'narrow'), 0, 0, tiled=True)  17.1 us
    another operation x1, local copies, waits for them, and re-layouts, decimate(): segments = samples.reshape(-1, DECIM * block_size)  13.5 us
    all_to_all x1, starting transfers between devices, on_device(): spectra = lax.all_to_all(whitened, ('wide', 'narrow'), 0, 0, tiled=True)  11.5 us
    all_to_all x1, waiting for transfers between devices, on_device(): arrived = lax.all_to_all(send, ('wide', 'narrow'), 0, 0, tiled=True)  9.65 us
    dot_general x1, matrix products, decimate(): jnp.dot(segments, table, preferred_element_type=jnp.float32)  9.01 us
    dot_general x1, local copies, waits for them, and re-layouts, decimate(): jnp.dot(segments, table, preferred_element_type=jnp.float32)  8.97 us
    dot_general x1, matrix products, whiten_t(): lax.dot_general(smoother(NBINS, SMOOTH), magnitude, (((0,), (0,)), ((), (...  8.7 us
  transfers between devices with their start and end apart: 2, of which 2 were waited for; matrix products, arithmetic and copies ran while one was open for 2% of the time, Pallas kernels for 0%

commit v1 on v0

--- a/solution.py
+++ b/solution.py
@@ -32,18 +32,40 @@
     return jnp.transpose(shifted, (1, 0, 2)).reshape(DECIM * block_size, cols)
 
 
-def decimate(samples, filter_taps):
-    row_count, row_length = samples.shape
+def decim_kernel(x_ref, t_ref, o_ref, carry_ref):
+    @pl.when(pl.program_id(0) == 0)
+    def _():
+        carry_ref[...] = jnp.zeros_like(carry_ref)
+
+    table = t_ref[...]
+    channels, windows, width = x_ref.shape
+    segment = table.shape[0]
+    block = table.shape[1] // 2
+    for g in range(width // segment):
+        x = x_ref[:, :, g * segment : (g + 1) * segment].reshape(channels * windows, segment)
+        both = jnp.dot(x, table, preferred_element_type=jnp.float32)
+        o_ref[:, g * block : (g + 1) * block] = (both[:, :block] + carry_ref[...]).astype(
+            jnp.bfloat16
+        )
+        carry_ref[...] = both[:, block:]
+
+
+def decimate(samples, filter_taps, chunk=2048):
+    channels, windows, row_length = samples.shape
     block_size = min(128, row_length // DECIM)
     table = fir_table(filter_taps, block_size)
-    segments = samples.reshape(-1, DECIM * block_size)
-    both = jnp.dot(segments, table, preferred_element_type=jnp.float32).reshape(
-        row_count, -1, 2 * block_size
-    )
-    current = both[:, :, :block_size]
-    spilled = both[:, :, block_size:]
-    spilled = jnp.pad(spilled[:, :-1], ((0, 0), (1, 0), (0, 0)))
-    return (current + spilled).reshape(row_count, -1).astype(jnp.bfloat16)
+    rows = channels * windows
+    return pl.pallas_call(
+        decim_kernel,
+        grid=(row_length // chunk,),
+        in_specs=[
+            pl.BlockSpec((channels, windows, chunk), lambda j: (0, 0, j)),
+            pl.BlockSpec(table.shape, lambda j: (0, 0)),
+        ],
+        out_specs=pl.BlockSpec((rows, chunk // DECIM), lambda j: (0, j)),
+        out_shape=jax.ShapeDtypeStruct((rows, row_length // DECIM), jnp.bfloat16),
+        scratch_shapes=[pltpu.VMEM((rows, block_size), jnp.float32)],
+    )(samples, table)
 
 
 def trig(index, modulus):
@@ -158,7 +180,7 @@
     group = NBINS // devices
     rows = chan_dev * window_total
 
-    decimated = decimate(raw_samples.reshape(rows, -1), filter_taps)
+    decimated = decimate(raw_samples, filter_taps)
     whitened = whiten_t(decimated, devices, group)
     spectra = lax.all_to_all(whitened, ("wide", "narrow"), 0, 0, tiled=True)
 

time: 138 us -> 108 us (0.78)
  local copies, waits for them, and re-layouts: 41.4 us -> 12.7 us
  matrix products: 20.4 us -> 11.4 us
  Pallas kernels: 23.3 us -> 32 us
    another operation x1 -> x0, local copies, waits for them, and re-layouts: 13.5 us -> none  [decimate(): segments = samples.reshape(-1, DECIM * block_size)]
    dot_general x1 -> x0, matrix products: 9.01 us -> none  [decimate(): jnp.dot(segments, table, preferred_element_type=jnp.float32)]
    dot_general x1 -> x0, local copies, waits for them, and re-layouts: 8.97 us -> none  [decimate(): jnp.dot(segments, table, preferred_element_type=jnp.float32)]
    pallas_call x0 -> x1, Pallas kernels: none -> 8.66 us  [decimate(): pl.pallas_call(decim_kernel, grid=(row_length // chunk,), in_specs=[pl.Bl...]
    unnamed x12 -> x9, local copies, waits for them, and re-layouts: 4.27 us -> 0.12 us
    slice x1 -> x0, local copies, waits for them, and re-layouts: 2.8 us -> none  [decimate(): spilled = jnp.pad(spilled[:, :-1], ((0, 0), (1, 0), (0, 0)))]
where the time goes in v1:
time: 108 us; the launch traced here: 107 us
  Pallas kernels  32 us (30%)
  waiting for transfers between devices  26.8 us (25%)
  starting transfers between devices  15.4 us (14%)
  local copies, waits for them, and re-layouts  12.7 us (12%)
  matrix products  11.4 us (11%)
  other arithmetic  8.86 us (8%)
    pallas_call x1, Pallas kernels, dft_t(): pl.pallas_call(dft_kernel, grid=(out_rows // block_rows,), in_specs=[pl.B...  23.3 us
    all_to_all x1, waiting for transfers between devices, on_device(): spectra = lax.all_to_all(whitened, ('wide', 'narrow'), 0, 0, tiled=True)  17.1 us
    all_to_all x1, starting transfers between devices, on_device(): spectra = lax.all_to_all(whitened, ('wide', 'narrow'), 0, 0, tiled=True)  11.5 us
    all_to_all x1, waiting for transfers between devices, on_device(): arrived = lax.all_to_all(send, ('wide', 'narrow'), 0, 0, tiled=True)  9.65 us
    dot_general x1, matrix products, whiten_t(): lax.dot_general(smoother(NBINS, SMOOTH), magnitude, (((0,), (0,)), ((), (...  8.7 us
    pallas_call x1, Pallas kernels, decimate(): pl.pallas_call(decim_kernel, grid=(row_length // chunk,), in_specs=[pl.Bl...  8.66 us
    all_to_all x1, starting transfers between devices, on_device(): arrived = lax.all_to_all(send, ('wide', 'narrow'), 0, 0, tiled=True)  3.9 us
    concatenate x2, local copies, waits for them, and re-layouts, rows(): jnp.concatenate([real_rows, imag_rows], axis=1)  2.75 us
  transfers between devices with their start and end apart: 2, of which 2 were waited for; matrix products, arithmetic and copies ran while one was open for 2% of the time, Pallas kernels for 0%

profile of v1, /device:TPU:1, one launch (start us, length us, event | category | flops | bytes accessed | tf_op | source)
XLA Modules:
  0.0 107.4 jit_solution(1330661559563896443)
XLA Ops:
  0.0 0.5 fusion.39
  0.9 1.4 %copy.38 = f32[128,2,8,32]{3,2,1,0:T(8,128)} copy(f32[128,2,8,32]{0,3,2,1:T(8,128)S(1)} %get-tuple-element.15) | data formatting | bytes 524288 | tf_op jit(solution)/shard_map/concatenate | solution.py:91
  2.3 1.4 %copy.39 = f32[128,2,8,32]{3,2,1,0:T(8,128)} copy(f32[128,2,8,32]{0,3,2,1:T(8,128)S(1)} %get-tuple-element.14) | data formatting | bytes 524288 | tf_op jit(solution)/shard_map/concatenate | solution.py:91
  3.7 2.1 %fusion.31 = (f32[128,1,8,128]{3,2,1,0:T(8,128)S(1)}, f32[128,1,8,128]{3,2,1,0:T(8,128)S(1)}) fusion(s32[128,8]{1,0:T(8,128)S(1)} %copy.40), kind=kLoop, calls=%fused_computation.63 | loop fusion | flops 1835008 | bytes 1052672 | tf_op jit(solution)/shard_map/sin | solution.py:73
  6.1 0.8 tile.10
  7.0 0.8 reshape.386.t_ref
  7.8 1.5 %pad_maximum_fusion = (f32[128,2,8,128]{3,2,1,0:T(8,128)}, f32[128,2,8,128]{3,2,1,0:T(8,128)}) fusion(f32[128,1,8,128]{3,2,1,0:T(8,128)S(1)} %get-tuple-element.17, f32[128,1,8,128]{3,2,1,0:T(8,128)S(1)} %get-tuple-element.16), kind=kLoop, calls=%fused_computation.20 | loop fusion | flops 524288 | bytes 3145728 | tf_op jit(solution)/shard_map/concatenate | solution.py:91
  9.2 8.7 %shard_map.46.dec_ref = bf16[256,4096]{1,0:T(8,128)(2,1)} custom-call(bf16[8,32,16384]{2,1,0:T(8,128)(2,1)} %x_ref.1, bf16[512,256]{1,0:T(8,128)(2,1)} %reshape.386.t_ref), custom_call_target="tpu_custom_call" | custom-call | tf_op jit(solution)/shard_map/pallas_call | solution.py:58
  17.9 23.3 %shard_map.47 = f32[2048,256]{1,0:T(8,128)} custom-call(f32[2048,32]{1,0:T(8,128)} %bitcast.87, f32[2048,32]{1,0:T(8,128)} %bitcast.88, f32[2048,128]{1,0:T(8,128)} %bitcast.85, f32[2048,128]{1,0:T(8,128)} %bitcast.86, bf16[256,4096]{1,0:T(8,128)(2,1)} %shard_map.46.dec_ref), custom_call_target="tpu_custom_call" | custom-call | tf_op jit(solution)/shard_map/pallas_call | solution.py:114
  41.2 8.7 %fusion.54 = (f32[256]{0:T(256)S(1)}, f32[1024,256]{1,0:T(8,128)S(1)}) fusion(f32[128,2,8,256]{3,2,1,0:T(8,128)} %bitcast.82, f32[1024]{0:T(1024)S(1)} %convert_reduce_fusion), kind=kOutput, calls=%fused_computation.109 | convolution fusion | flops 3227516672 | bytes 3150848 | tf_op jit(solution)/shard_map/dot_general | solution.py:163
  50.2 1.4 %fusion.1 = bf16[128,16,256]{2,1,0:T(8,128)(2,1)} fusion(f32[128,16,256]{2,1,0:T(8,128)S(1)} %bitcast.83, f32[128,8,256]{2,1,0:T(8,128)S(1)} %divide_bitcast_fusion), kind=kLoop, calls=%fused_computation.7 | loop fusion | flops 1048576 | bytes 4194304 | tf_op jit(solution)/shard_map/convert_element_type | solution.py:171
  51.5 11.5 %all-to-all-start = ((bf16[128,16,256]{2,1,0:T(8,128)(2,1)}), bf16[128,16,256]{2,1,0:T(8,128)(2,1)S(1)}, u32[]{:S(2)}, u32[]{:S(2)}) async-start(bf16[128,16,256]{2,1,0:T(8,128)(2,1)} %fusion.1), calls=%async_computation | async-start | bytes 2097152 | tf_op jit(solution)/shard_map/all_to_all | solution.py:185
  63.3 2.1 %fusion.30 = (f32[1024,64]{1,0:T(8,128)S(1)}, f32[1024,64]{1,0:T(8,128)S(1)}) fusion(s32[1024]{0:T(1024)S(1)} %iota_add_fusion), kind=kLoop, calls=%fused_computation.62 | loop fusion | flops 983040 | bytes 528384 | tf_op jit(solution)/shard_map/cos | solution.py:73
  65.4 17.1 %all-to-all-done = bf16[128,16,256]{2,1,0:T(8,128)(2,1)S(1)} async-done(((bf16[128,16,256]{2,1,0:T(8,128)(2,1)}), bf16[128,16,256]{2,1,0:T(8,128)(2,1)S(1)}, u32[]{:S(2)}, u32[]{:S(2)}) %all-to-all-start) | async-done | bytes 1048608 | tf_op jit(solution)/shard_map/all_to_all | solution.py:185
  82.5 0.6 gather_fusion.1
  83.2 0.2 reshape.390
  83.4 0.6 gather_fusion
  84.1 0.2 reshape.389
  84.3 0.3 fusion.34
  84.6 0.3 fusion.33
  84.9 0.3 fusion.5
  85.2 0.3 fusion.4
  85.6 0.7 copy.47
  86.3 0.3 copy.48
  86.6 0.4 convolution_bitcast_fusion
  87.0 1.5 %copy.49 = f32[32,4,8,2,16]{4,3,2,1,0:T(2,128)S(1)} copy(f32[32,4,8,2,16]{0,2,1,4,3:T(8,128)S(1)} %convolution_bitcast_fusion) | data formatting | bytes 262144 | tf_op jit(solution)/shard_map/nst,twqv->wnsqv/transpose | solution.py:212
  88.5 2.1 %all_to_all.12 = f32[128,1,256]{2,1,0:T(1,128)} reshape(f32[32,4,8,2,16]{4,3,2,1,0:T(2,128)S(1)} %copy.49) | data formatting | bytes 262144 | tf_op jit(solution)/shard_map/all_to_all | solution.py:214
  90.6 3.9 %all-to-all-start.1 = ((f32[128,1,256]{2,1,0:T(1,128)}), f32[128,1,256]{2,1,0:T(1,128)S(1)}, u32[]{:S(2)}, u32[]{:S(2)}) async-start(f32[128,1,256]{2,1,0:T(1,128)} %all_to_all.12), calls=%async_computation.1 | async-start | bytes 262144 | tf_op jit(solution)/shard_map/all_to_all | solution.py:214
  94.7 9.6 %all-to-all-done.1 = f32[128,1,256]{2,1,0:T(1,128)S(1)} async-done(((f32[128,1,256]{2,1,0:T(1,128)}), f32[128,1,256]{2,1,0:T(1,128)S(1)}, u32[]{:S(2)}, u32[]{:S(2)}) %all-to-all-start.1) | async-done | bytes 131104 | tf_op jit(solution)/shard_map/all_to_all | solution.py:214
  104.5 0.4 copy.52
  105.5 1.2 %fusion.10 = f32[128,64]{1,0:T(8,128)S(1)} fusion(f32[128,1024]{1,0:T(8,128)S(1)} %get-tuple-element.13, f32[128,1024]{1,0:T(8,128)S(1)} %get-tuple-element.12, f32[1024,64]{1,0:T(8,128)S(1)} %get-tuple-element.21, f32[1024,64]{1,0:T(8,128)S(1)} %get-tuple-element.20), kind=kOutput, calls=%fused_computation.23 | convolution fusion | flops 201850880 | bytes 1605632 | tf_op jit(solution)/shard_map/dot_general | solution.py:145
  106.7 0.7 reshape_reshape.3
  (37 shorter events, 2.3 us)
Async XLA Ops:
  0.0 5.8 %copy-start.3 = (f32[64]{0:T(128)S(1)}, f32[64]{0:T(128)}, u32[]{:S(2)}) copy-start(f32[64]{0:T(128)} %param.7) | copy-start | bytes 772
  41.2 8.9 %copy-start = (f32[2048,256]{1,0:T(8,128)S(1)}, f32[2048,256]{1,0:T(8,128)}, u32[]{:S(2)}) copy-start(f32[2048,256]{1,0:T(8,128)} %shard_map.47) | copy-start | bytes 6291460
  50.0 13.1 %copy-start.2 = (s32[16]{0:T(128)S(1)}, s32[16]{0:T(128)}, u32[]{:S(2)}) copy-start(s32[16]{0:T(128)} %param.9) | copy-start | bytes 196
  50.0 13.3 %copy-start.1 = (s32[16,2]{0,1:T(2,128)S(1)}, s32[16,2]{0,1:T(2,128)}, u32[]{:S(2)}) copy-start(s32[16,2]{0,1:T(2,128)} %param.8) | copy-start | bytes 388
  51.5 31.0 %all-to-all-start = ((bf16[128,16,256]{2,1,0:T(8,128)(2,1)}), bf16[128,16,256]{2,1,0:T(8,128)(2,1)S(1)}, u32[]{:S(2)}, u32[]{:S(2)}) async-start(bf16[128,16,256]{2,1,0:T(8,128)(2,1)} %fusion.1), calls=%async_computation | async-start | bytes 2097152 | tf_op jit(solution)/shard_map/all_to_all | solution.py:185
  90.6 13.8 %all-to-all-start.1 = ((f32[128,1,256]{2,1,0:T(1,128)}), f32[128,1,256]{2,1,0:T(1,128)S(1)}, u32[]{:S(2)}, u32[]{:S(2)}) async-start(f32[128,1,256]{2,1,0:T(1,128)} %all_to_all.12), calls=%async_computation.1 | async-start | bytes 262144 | tf_op jit(solution)/shard_map/all_to_all | solution.py:214

commit v2 on v1

--- a/solution.py
+++ b/solution.py
@@ -76,54 +76,46 @@
 LO = 128
 
 
-def dft_factors(point_count, bin_count, group):
-    hi = jnp.arange(point_count // LO, dtype=jnp.int32)[None, :]
-    lo = jnp.arange(LO, dtype=jnp.int32)[None, :]
-    frequency = 1 + jnp.arange(bin_count, dtype=jnp.int32)[:, None]
+def dft_factors(point_count, bin_count):
+    hi = jnp.arange(point_count // LO, dtype=jnp.int32)[:, None]
+    lo = jnp.arange(LO, dtype=jnp.int32)[:, None]
+    frequency = 1 + jnp.arange(bin_count, dtype=jnp.int32)[None, :]
     c1, s1 = trig(frequency * hi * LO, point_count)
     c2, s2 = trig(frequency * lo, point_count)
-    slices = bin_count // group
-
-    def rows(real_rows, imag_rows):
-        width = real_rows.shape[1]
-        real_rows = real_rows.reshape(slices, 1, group, width)
-        imag_rows = imag_rows.reshape(slices, 1, group, width)
-        return jnp.concatenate([real_rows, imag_rows], axis=1).reshape(2 * bin_count, width)
-
-    return rows(c1, -s1), rows(-s1, -c1), rows(c2, c2), rows(s2, s2)
+
+    def cat(real_cols, imag_cols):
+        return jnp.concatenate([real_cols, imag_cols], axis=1)
+
+    return cat(c1, -s1), cat(-s1, -c1), cat(c2, c2), cat(s2, s2)
 
 
 def dft_kernel(p_ref, q_ref, c_ref, s_ref, dec_ref, out_ref, tab_ref):
     c2 = c_ref[...]
     s2 = s_ref[...]
-    p_all = p_ref[...]
-    q_all = q_ref[...]
-    for hi in range(p_ref.shape[1]):
-        value = p_all[:, hi : hi + 1] * c2 + q_all[:, hi : hi + 1] * s2
-        tab_ref[:, hi * LO : (hi + 1) * LO] = value.astype(jnp.bfloat16)
-    out_ref[...] = lax.dot_general(
-        tab_ref[...], dec_ref[...], (((1,), (1,)), ((), ())), preferred_element_type=jnp.float32
-    )
-
-
-def dft_t(decimated, group, block_rows=256):
+    for hi in range(p_ref.shape[0]):
+        value = p_ref[hi : hi + 1, :] * c2 + q_ref[hi : hi + 1, :] * s2
+        tab_ref[hi * LO : (hi + 1) * LO, :] = value.astype(jnp.bfloat16)
+    out_ref[...] = jnp.dot(dec_ref[...], tab_ref[...], preferred_element_type=jnp.float32)
+
+
+def dft(decimated, block_cols=512):
     rows, points = decimated.shape
-    p, q, c, s = dft_factors(points, NBINS, group)
-    out_rows = p.shape[0]
-    hi_count = p.shape[1]
+    p, q, c, s = dft_factors(points, NBINS)
+    cols = p.shape[1]
+    hi_count = p.shape[0]
     return pl.pallas_call(
         dft_kernel,
-        grid=(out_rows // block_rows,),
+        grid=(cols // block_cols,),
         in_specs=[
-            pl.BlockSpec((block_rows, hi_count), lambda i: (i, 0)),
-            pl.BlockSpec((block_rows, hi_count), lambda i: (i, 0)),
-            pl.BlockSpec((block_rows, LO), lambda i: (i, 0)),
-            pl.BlockSpec((block_rows, LO), lambda i: (i, 0)),
+            pl.BlockSpec((hi_count, block_cols), lambda i: (0, i)),
+            pl.BlockSpec((hi_count, block_cols), lambda i: (0, i)),
+            pl.BlockSpec((LO, block_cols), lambda i: (0, i)),
+            pl.BlockSpec((LO, block_cols), lambda i: (0, i)),
             pl.BlockSpec((rows, points), lambda i: (0, 0)),
         ],
-        out_specs=pl.BlockSpec((block_rows, rows), lambda i: (i, 0)),
-        out_shape=jax.ShapeDtypeStruct((out_rows, rows), jnp.float32),
-        scratch_shapes=[pltpu.VMEM((block_rows, points), jnp.bfloat16)],
+        out_specs=pl.BlockSpec((rows, block_cols), lambda i: (0, i)),
+        out_shape=jax.ShapeDtypeStruct((rows, cols), jnp.float32),
+        scratch_shapes=[pltpu.VMEM((points, block_cols), jnp.bfloat16)],
     )(p, q, c, s, decimated)
 
 
@@ -154,21 +146,18 @@
     return nearby / jnp.sum(nearby, axis=0, keepdims=True)
 
 
-def whiten_t(decimated, slices, group):
+def whiten(decimated, slices, group):
     rows = decimated.shape[0]
-    spec = dft_t(decimated, group).reshape(slices, 2, group, rows)
-    real_part = spec[:, 0].reshape(NBINS, rows)
-    imag_part = spec[:, 1].reshape(NBINS, rows)
+    spectrum = dft(decimated)
+    real_part = spectrum[:, :NBINS]
+    imag_part = spectrum[:, NBINS:]
     magnitude = jnp.sqrt(real_part * real_part + imag_part * imag_part)
-    smooth = lax.dot_general(
-        smoother(NBINS, SMOOTH),
-        magnitude,
-        (((0,), (0,)), ((), ())),
-        precision=lax.Precision.HIGHEST,
-    )
-    floor_level = water_level * jnp.mean(smooth, axis=0, keepdims=True) + epsilon
-    factor = (1.0 / (smooth + floor_level)).reshape(slices, 1, group, rows)
-    return (spec * factor).astype(jnp.bfloat16).reshape(slices, 2 * group, rows)
+    smooth = jnp.dot(magnitude, smoother(NBINS, SMOOTH), precision=lax.Precision.HIGHEST)
+    floor_level = water_level * jnp.mean(smooth, axis=1, keepdims=True) + epsilon
+    factor = 1.0 / (smooth + floor_level)
+    whitened = (spectrum * jnp.concatenate([factor, factor], axis=1)).astype(jnp.bfloat16)
+    whitened = jnp.transpose(whitened.reshape(rows, 2, slices, group), (2, 1, 3, 0))
+    return whitened.reshape(slices, 2 * group, rows)
 
 
 def on_device(raw_samples, filter_taps, tile_pairs, tile_owners):
@@ -181,7 +170,7 @@
     rows = chan_dev * window_total
 
     decimated = decimate(raw_samples, filter_taps)
-    whitened = whiten_t(decimated, devices, group)
+    whitened = whiten(decimated, devices, group)
     spectra = lax.all_to_all(whitened, ("wide", "narrow"), 0, 0, tiled=True)
 
     source = jnp.take(spectra, tile_pairs[:, 0], axis=0)

time: 108 us -> 88.7 us (0.82)
  Pallas kernels: 32 us -> 16.9 us
  matrix products: 11.4 us -> 8.21 us
  local copies, waits for them, and re-layouts: 12.7 us -> 11.4 us
    pallas_call x1, Pallas kernels: 23.3 us -> 8.23 us  [dft(): pl.pallas_call(dft_kernel, grid=(cols // block_cols,), in_specs=[pl.Block...]
    dot_general x1, matrix products: 8.7 us -> 5.53 us  [whiten(): jnp.dot(magnitude, smoother(NBINS, SMOOTH), precision=lax.Precision.HIGHEST)]
    concatenate x2 -> x0, local copies, waits for them, and re-layouts: 2.75 us -> none  [rows(): jnp.concatenate([real_rows, imag_rows], axis=1)]
  transfers between devices with their start and end apart: 2 -> 2, of which waited for: 2 -> 2; matrix products, arithmetic and copies ran while one was open for 2% -> 3% of each run, Pallas kernels for 0% -> 0%
where the time goes in v2:
time: 88.7 us; the launch traced here: 88.3 us
  waiting for transfers between devices  26.8 us (30%)
  Pallas kernels  16.9 us (19%)
  starting transfers between devices  15.4 us (17%)
  local copies, waits for them, and re-layouts  11.4 us (13%)
  other arithmetic  9.42 us (11%)
  matrix products  8.21 us (9%)
    all_to_all x1, waiting for transfers between devices, on_device(): spectra = lax.all_to_all(whitened, ('wide', 'narrow'), 0, 0, tiled=True)  17.1 us
    all_to_all x1, starting transfers between devices, on_device(): spectra = lax.all_to_all(whitened, ('wide', 'narrow'), 0, 0, tiled=True)  11.5 us
    all_to_all x1, waiting for transfers between devices, on_device(): arrived = lax.all_to_all(send, ('wide', 'narrow'), 0, 0, tiled=True)  9.65 us
    pallas_call x1, Pallas kernels, decimate(): pl.pallas_call(decim_kernel, grid=(row_length // chunk,), in_specs=[pl.Bl...  8.63 us
    pallas_call x1, Pallas kernels, dft(): pl.pallas_call(dft_kernel, grid=(cols // block_cols,), in_specs=[pl.Block...  8.23 us
    dot_general x1, matrix products, whiten(): jnp.dot(magnitude, smoother(NBINS, SMOOTH), precision=lax.Precision.HIGHEST)  5.53 us
    all_to_all x1, starting transfers between devices, on_device(): arrived = lax.all_to_all(send, ('wide', 'narrow'), 0, 0, tiled=True)  3.91 us
    concatenate x2, other arithmetic, cat(): return jnp.concatenate([real_cols, imag_cols], axis=1)  2.44 us
  transfers between devices with their start and end apart: 2, of which 2 were waited for; matrix products, arithmetic and copies ran while one was open for 3% of the time, Pallas kernels for 0%

profile of v2, /device:TPU:1, one launch (start us, length us, event | category | flops | bytes accessed | tf_op | source)
XLA Modules:
  0.0 88.3 jit_solution(10659559221658809194)
XLA Ops:
  0.0 0.5 fusion.38
  0.5 2.0 %fusion.30 = (f32[128,1024]{1,0:T(8,128)S(1)}, f32[128,1024]{1,0:T(8,128)S(1)}) fusion(s32[1024]{0:T(1024)S(1)} %iota_add_fusion), kind=kLoop, calls=%fused_computation.63 | loop fusion | flops 1835008 | bytes 1052672 | tf_op jit(solution)/shard_map/sin | solution.py:73
  2.8 0.7 convert_element_type.62
  3.8 0.8 tile.10
  4.7 0.8 reshape.192.t_ref
  5.4 1.6 %pad_maximum_fusion = (f32[128,2048]{1,0:T(8,128)}, f32[128,2048]{1,0:T(8,128)}) fusion(f32[128,1024]{1,0:T(8,128)S(1)} %get-tuple-element.21, f32[128,1024]{1,0:T(8,128)S(1)} %get-tuple-element.20), kind=kLoop, calls=%fused_computation.19 | loop fusion | flops 524288 | bytes 3145728 | tf_op jit(solution)/shard_map/concatenate | solution.py:87
  7.0 8.6 %shard_map.46.dec_ref = bf16[256,4096]{1,0:T(8,128)(2,1)} custom-call(bf16[8,32,16384]{2,1,0:T(8,128)(2,1)} %x_ref.1, bf16[512,256]{1,0:T(8,128)(2,1)} %reshape.192.t_ref), custom_call_target="tpu_custom_call" | custom-call | tf_op jit(solution)/shard_map/pallas_call | solution.py:58
  15.6 0.9 pad_maximum_fusion.4
  16.5 8.2 %shard_map.47 = f32[256,2048]{1,0:T(8,128)} custom-call(f32[32,2048]{1,0:T(8,128)} %get-tuple-element.15.p_ref, f32[32,2048]{1,0:T(8,128)} %get-tuple-element.14.q_ref, f32[128,2048]{1,0:T(8,128)} %get-tuple-element.31.c_ref, f32[128,2048]{1,0:T(8,128)} %get-tuple-element.32.s_ref, bf16[256,4096]{1,0:T(8,128)(2,1)} %shard_map.46.dec_ref), custom_call_target="tpu_custom_call" | custom-call | tf_op jit(solution)/shard_map/pallas_call | solution.py:106
  24.7 5.5 %fusion.53 = (f32[256]{0:T(256)S(1)}, f32[256,1024]{1,0:T(8,128)S(1)}) fusion(f32[1024]{0:T(1024)S(1)} %convert_reduce_fusion, f32[256,2048]{1,0:T(8,128)} %shard_map.47), kind=kOutput, calls=%fused_computation.108 | convolution fusion | flops 3227516672 | bytes 3150848 | tf_op jit(solution)/shard_map/dot_general | solution.py:155
  30.5 0.3 fusion.1
  30.9 0.5 copy.41
  31.4 1.1 %copy.65 = bf16[128,2,8,256]{3,2,1,0:T(8,128)(2,1)} copy(bf16[128,2,8,256]{3,2,0,1:T(8,128)(2,1)S(1)} %bitcast.72) | data formatting | bytes 2097152 | tf_op jit(solution)/shard_map/transpose | solution.py:159
  32.5 11.5 %all-to-all-start = ((bf16[128,16,256]{2,1,0:T(8,128)(2,1)}), bf16[128,16,256]{2,1,0:T(8,128)(2,1)S(1)}, u32[]{:S(2)}, u32[]{:S(2)}) async-start(bf16[128,16,256]{2,1,0:T(8,128)(2,1)} %bitcast.70), calls=%async_computation | async-start | bytes 2097152 | tf_op jit(solution)/shard_map/all_to_all | solution.py:174
  44.2 2.1 %fusion.29 = (f32[1024,64]{1,0:T(8,128)S(1)}, f32[1024,64]{1,0:T(8,128)S(1)}) fusion(s32[1024]{0:T(1024)S(1)} %iota_add_fusion), kind=kLoop, calls=%fused_computation.62 | loop fusion | flops 983040 | bytes 528384 | tf_op jit(solution)/shard_map/cos | solution.py:73
  46.4 17.1 %all-to-all-done = bf16[128,16,256]{2,1,0:T(8,128)(2,1)S(1)} async-done(((bf16[128,16,256]{2,1,0:T(8,128)(2,1)}), bf16[128,16,256]{2,1,0:T(8,128)(2,1)S(1)}, u32[]{:S(2)}, u32[]{:S(2)}) %all-to-all-start) | async-done | bytes 1048608 | tf_op jit(solution)/shard_map/all_to_all | solution.py:174
  63.5 0.6 gather_fusion.1
  64.4 0.6 gather_fusion
  65.3 0.3 fusion.33
  65.6 0.3 fusion.32
  65.9 0.3 fusion.5
  66.2 0.3 fusion.4
  66.5 0.7 copy.47
  67.3 0.3 copy.48
  67.6 0.4 convolution_bitcast_fusion
  68.0 1.5 %copy.49 = f32[32,4,8,2,16]{4,3,2,1,0:T(2,128)S(1)} copy(f32[32,4,8,2,16]{0,2,1,4,3:T(8,128)S(1)} %convolution_bitcast_fusion) | data formatting | bytes 262144 | tf_op jit(solution)/shard_map/nst,twqv->wnsqv/transpose | solution.py:201
  69.5 2.1 %all_to_all.12 = f32[128,1,256]{2,1,0:T(1,128)} reshape(f32[32,4,8,2,16]{4,3,2,1,0:T(2,128)S(1)} %copy.49) | data formatting | bytes 262144 | tf_op jit(solution)/shard_map/all_to_all | solution.py:203
  71.6 3.9 %all-to-all-start.1 = ((f32[128,1,256]{2,1,0:T(1,128)}), f32[128,1,256]{2,1,0:T(1,128)S(1)}, u32[]{:S(2)}, u32[]{:S(2)}) async-start(f32[128,1,256]{2,1,0:T(1,128)} %all_to_all.12), calls=%async_computation.1 | async-start | bytes 262144 | tf_op jit(solution)/shard_map/all_to_all | solution.py:203
  75.7 9.6 %all-to-all-done.1 = f32[128,1,256]{2,1,0:T(1,128)S(1)} async-done(((f32[128,1,256]{2,1,0:T(1,128)}), f32[128,1,256]{2,1,0:T(1,128)S(1)}, u32[]{:S(2)}, u32[]{:S(2)}) %all-to-all-start.1) | async-done | bytes 131104 | tf_op jit(solution)/shard_map/all_to_all | solution.py:203
  85.4 0.4 copy.52
  86.4 1.2 %fusion.9 = f32[128,64]{1,0:T(8,128)S(1)} fusion(f32[128,1024]{1,0:T(8,128)S(1)} %get-tuple-element.13, f32[128,1024]{1,0:T(8,128)S(1)} %get-tuple-element.12, f32[1024,64]{1,0:T(8,128)S(1)} %get-tuple-element.19, f32[1024,64]{1,0:T(8,128)S(1)} %get-tuple-element.18), kind=kOutput, calls=%fused_computation.22 | convolution fusion | flops 201850880 | bytes 1605632 | tf_op jit(solution)/shard_map/dot_general | solution.py:137
  87.6 0.7 reshape_reshape.3
  (33 shorter events, 2.7 us)
Async XLA Ops:
  24.7 5.8 %copy-start = (f32[256,2048]{1,0:T(8,128)S(1)}, f32[256,2048]{1,0:T(8,128)}, u32[]{:S(2)}) copy-start(f32[256,2048]{1,0:T(8,128)} %shard_map.47) | copy-start | bytes 6291460
  30.9 13.1 %copy-start.2 = (s32[16]{0:T(128)S(1)}, s32[16]{0:T(128)}, u32[]{:S(2)}) copy-start(s32[16]{0:T(128)} %param.9) | copy-start | bytes 196
  30.9 13.3 %copy-start.1 = (s32[16,2]{0,1:T(2,128)S(1)}, s32[16,2]{0,1:T(2,128)}, u32[]{:S(2)}) copy-start(s32[16,2]{0,1:T(2,128)} %param.8) | copy-start | bytes 388
  32.5 31.0 %all-to-all-start = ((bf16[128,16,256]{2,1,0:T(8,128)(2,1)}), bf16[128,16,256]{2,1,0:T(8,128)(2,1)S(1)}, u32[]{:S(2)}, u32[]{:S(2)}) async-start(bf16[128,16,256]{2,1,0:T(8,128)(2,1)} %bitcast.70), calls=%async_computation | async-start | bytes 2097152 | tf_op jit(solution)/shard_map/all_to_all | solution.py:174
  71.6 13.8 %all-to-all-start.1 = ((f32[128,1,256]{2,1,0:T(1,128)}), f32[128,1,256]{2,1,0:T(1,128)S(1)}, u32[]{:S(2)}, u32[]{:S(2)}) async-start(f32[128,1,256]{2,1,0:T(1,128)} %all_to_all.12), calls=%async_computation.1 | async-start | bytes 262144 | tf_op jit(solution)/shard_map/all_to_all | solution.py:203

commit v3 on v2

--- a/solution.py
+++ b/solution.py
@@ -1,4 +1,7 @@
+import functools
 import math
+
+import numpy as np
 
 import jax
 import jax.numpy as jnp
@@ -77,46 +80,49 @@
 
 
 def dft_factors(point_count, bin_count):
-    hi = jnp.arange(point_count // LO, dtype=jnp.int32)[:, None]
-    lo = jnp.arange(LO, dtype=jnp.int32)[:, None]
-    frequency = 1 + jnp.arange(bin_count, dtype=jnp.int32)[None, :]
-    c1, s1 = trig(frequency * hi * LO, point_count)
-    c2, s2 = trig(frequency * lo, point_count)
-
-    def cat(real_cols, imag_cols):
-        return jnp.concatenate([real_cols, imag_cols], axis=1)
-
-    return cat(c1, -s1), cat(-s1, -c1), cat(c2, c2), cat(s2, s2)
-
-
-def dft_kernel(p_ref, q_ref, c_ref, s_ref, dec_ref, out_ref, tab_ref):
-    c2 = c_ref[...]
-    s2 = s_ref[...]
-    for hi in range(p_ref.shape[0]):
-        value = p_ref[hi : hi + 1, :] * c2 + q_ref[hi : hi + 1, :] * s2
+    frequency = 1 + np.arange(bin_count, dtype=np.int64)[None, :]
+    hi = np.arange(point_count // LO, dtype=np.int64)[:, None]
+    lo = np.arange(LO, dtype=np.int64)[:, None]
+    angle_hi = (frequency * hi * LO % point_count) * (2.0 * np.pi / point_count)
+    angle_lo = (frequency * lo % point_count) * (2.0 * np.pi / point_count)
+    c1, s1 = np.cos(angle_hi), np.sin(angle_hi)
+    c2, s2 = np.cos(angle_lo), np.sin(angle_lo)
+    return [jnp.asarray(t.astype(np.float32)) for t in (c1, s1, c2, s2)]
+
+
+def dft_kernel(c1_ref, s1_ref, c2_ref, s2_ref, dec_ref, out_ref, tab_ref, *, halves):
+    real = pl.program_id(0) < halves
+    c1 = c1_ref[...]
+    s1 = s1_ref[...]
+    p = jnp.where(real, c1, -s1)
+    q = jnp.where(real, -s1, -c1)
+    c2 = c2_ref[...]
+    s2 = s2_ref[...]
+    for hi in range(p.shape[0]):
+        value = p[hi : hi + 1, :] * c2 + q[hi : hi + 1, :] * s2
         tab_ref[hi * LO : (hi + 1) * LO, :] = value.astype(jnp.bfloat16)
     out_ref[...] = jnp.dot(dec_ref[...], tab_ref[...], preferred_element_type=jnp.float32)
 
 
 def dft(decimated, block_cols=512):
     rows, points = decimated.shape
-    p, q, c, s = dft_factors(points, NBINS)
-    cols = p.shape[1]
-    hi_count = p.shape[0]
+    c1, s1, c2, s2 = dft_factors(points, NBINS)
+    hi_count = c1.shape[0]
+    halves = NBINS // block_cols
     return pl.pallas_call(
-        dft_kernel,
-        grid=(cols // block_cols,),
+        functools.partial(dft_kernel, halves=halves),
+        grid=(2 * halves,),
         in_specs=[
-            pl.BlockSpec((hi_count, block_cols), lambda i: (0, i)),
-            pl.BlockSpec((hi_count, block_cols), lambda i: (0, i)),
-            pl.BlockSpec((LO, block_cols), lambda i: (0, i)),
-            pl.BlockSpec((LO, block_cols), lambda i: (0, i)),
+            pl.BlockSpec((hi_count, block_cols), lambda i: (0, i % halves)),
+            pl.BlockSpec((hi_count, block_cols), lambda i: (0, i % halves)),
+            pl.BlockSpec((LO, block_cols), lambda i: (0, i % halves)),
+            pl.BlockSpec((LO, block_cols), lambda i: (0, i % halves)),
             pl.BlockSpec((rows, points), lambda i: (0, 0)),
         ],
         out_specs=pl.BlockSpec((rows, block_cols), lambda i: (0, i)),
-        out_shape=jax.ShapeDtypeStruct((rows, cols), jnp.float32),
+        out_shape=jax.ShapeDtypeStruct((rows, 2 * NBINS), jnp.float32),
         scratch_shapes=[pltpu.VMEM((points, block_cols), jnp.bfloat16)],
-    )(p, q, c, s, decimated)
+    )(c1, s1, c2, s2, decimated)
 
 
 def lag_transform(cross, point_count, lag_count, window_count):
@@ -152,7 +158,7 @@
     real_part = spectrum[:, :NBINS]
     imag_part = spectrum[:, NBINS:]
     magnitude = jnp.sqrt(real_part * real_part + imag_part * imag_part)
-    smooth = jnp.dot(magnitude, smoother(NBINS, SMOOTH), precision=lax.Precision.HIGHEST)
+    smooth = jnp.dot(magnitude, smoother(NBINS, SMOOTH), precision=lax.Precision.HIGH)
     floor_level = water_level * jnp.mean(smooth, axis=1, keepdims=True) + epsilon
     factor = 1.0 / (smooth + floor_level)
     whitened = (spectrum * jnp.concatenate([factor, factor], axis=1)).astype(jnp.bfloat16)
@@ -186,10 +192,7 @@
 
     real_sum = mm(src_real, dst_real) + mm(src_imag, dst_imag)
     imag_sum = mm(src_real, dst_imag) - mm(src_imag, dst_real)
-    cross = jnp.stack([real_sum, imag_sum], axis=1)
-    pair_share = BLK * BLK // wide_count
-    cross = cross.reshape(tiles, 2 * group, BLK * BLK // pair_share, pair_share)
-    cross = jnp.transpose(cross, (0, 2, 3, 1))
+    cross = jnp.stack([real_sum, imag_sum], axis=1).reshape(tiles, -1)
 
     slot_ids = jnp.arange(SLOTS, dtype=jnp.int32)
     owner_ids = jnp.arange(narrow_count, dtype=jnp.int32)
@@ -198,11 +201,18 @@
     select_all = (owned_all[:, None, :] & (rank_all[:, None, :] == slot_ids[None, :, None])).astype(
         jnp.float32
     )
-    send = jnp.einsum("nst,twqv->wnsqv", select_all, cross, precision=lax.Precision.HIGHEST)
-    send = send.reshape(devices, SLOTS * pair_share * 2 * group)
+    slotted = jnp.dot(
+        select_all.reshape(narrow_count * SLOTS, tiles), cross, precision=lax.Precision.HIGHEST
+    )
+    pair_share = BLK * BLK // wide_count
+    slotted = slotted.reshape(
+        narrow_count, SLOTS, 2, group, BLK, BLK // pair_share, pair_share
+    )
+    send = jnp.transpose(slotted, (4, 5, 0, 1, 2, 3, 6))
+    send = send.reshape(devices, SLOTS * 2 * group * pair_share)
     arrived = lax.all_to_all(send, ("wide", "narrow"), 0, 0, tiled=True)
-    arrived = arrived.reshape(devices, SLOTS * pair_share, 2, group)
-    arrived = jnp.transpose(arrived, (1, 2, 0, 3)).reshape(SLOTS * pair_share, 2, NBINS)
+    arrived = arrived.reshape(devices, SLOTS, 2, group, pair_share)
+    arrived = jnp.transpose(arrived, (1, 4, 2, 0, 3)).reshape(SLOTS * pair_share, 2, NBINS)
     stacked = lag_transform(arrived, NFFT, LAGS, window_total)
     return stacked.reshape(SLOTS, pair_share, LAGS)
 

time: 88.7 us -> 97 us (1.094)
  local copies, waits for them, and re-layouts: 11.4 us -> 22.5 us
  other arithmetic: 9.42 us -> 5.33 us
  matrix products: 8.21 us -> 10.3 us
  waiting for transfers between devices: 26.8 us -> 25.7 us
    transpose x2, local copies, waits for them, and re-layouts: 1.91 us -> 7.98 us  [the longest x1 7.37 us: on_device(): send = jnp.transpose(slotted, (4, 5, 0, 1, 2, 3, 6))]
    all_to_all x2 -> x3, local copies, waits for them, and re-layouts: 2.19 us -> 6.99 us  [on_device(): arrived = lax.all_to_all(send, ('wide', 'narrow'), 0, 0, tiled=True)]
    concatenate x2 -> x0, other arithmetic: 2.44 us -> none  [cat(): return jnp.concatenate([real_cols, imag_cols], axis=1)]
    dot_general x2, matrix products: 5.89 us -> 7.95 us  [the longest x1 4.17 us: on_device(): jnp.dot(select_all.reshape(narrow_count * SLOTS, tiles), cross, precision...]
    sin x1 -> x0, other arithmetic: 2.04 us -> none  [trig(): return (jnp.cos(angle), jnp.sin(angle))]
    all_to_all x1, waiting for transfers between devices: 17.1 us -> 16.1 us  [on_device(): spectra = lax.all_to_all(whitened, ('wide', 'narrow'), 0, 0, tiled=True)]
    cos x2, other arithmetic: 2.34 us -> 3.37 us  [trig(): return (jnp.cos(angle), jnp.sin(angle))]
  transfers between devices with their start and end apart: 2 -> 2, of which waited for: 2 -> 2; matrix products, arithmetic and copies ran while one was open for 3% -> 4% of each run, Pallas kernels for 0% -> 0%
where the time goes in v3:
time: 97 us; the launch traced here: 96.6 us
  waiting for transfers between devices  25.7 us (26%)
  local copies, waits for them, and re-layouts  22.5 us (23%)
  Pallas kernels  17 us (18%)
  starting transfers between devices  15.4 us (16%)
  matrix products  10.3 us (11%)
  other arithmetic  5.33 us (5%)
    all_to_all x1, waiting for transfers between devices, on_device(): spectra = lax.all_to_all(whitened, ('wide', 'narrow'), 0, 0, tiled=True)  16.1 us
    all_to_all x1, starting transfers between devices, on_device(): spectra = lax.all_to_all(whitened, ('wide', 'narrow'), 0, 0, tiled=True)  11.5 us
    all_to_all x1, waiting for transfers between devices, on_device(): arrived = lax.all_to_all(send, ('wide', 'narrow'), 0, 0, tiled=True)  9.64 us
    pallas_call x1, Pallas kernels, decimate(): pl.pallas_call(decim_kernel, grid=(row_length // chunk,), in_specs=[pl.Bl...  8.68 us
    pallas_call x1, Pallas kernels, dft(): pl.pallas_call(functools.partial(dft_kernel, halves=halves), grid=(2 * ha...  8.35 us
    transpose x1, local copies, waits for them, and re-layouts, on_device(): send = jnp.transpose(slotted, (4, 5, 0, 1, 2, 3, 6))  7.37 us
    all_to_all x3, local copies, waits for them, and re-layouts, on_device(): arrived = lax.all_to_all(send, ('wide', 'narrow'), 0, 0, tiled=True)  6.99 us
    dot_general x1, matrix products, on_device(): jnp.dot(select_all.reshape(narrow_count * SLOTS, tiles), cross, precision...  4.17 us
  transfers between devices with their start and end apart: 2, of which 2 were waited for; matrix products, arithmetic and copies ran while one was open for 4% of the time, Pallas kernels for 0%

profile of v3, /device:TPU:1, one launch (start us, length us, event | category | flops | bytes accessed | tf_op | source)
XLA Modules:
  0.0 96.6 jit_solution(14883695381389263435)
XLA Ops:
  0.2 0.7 convert_element_type.43
  1.2 0.8 tile.10
  2.1 0.8 reshape.217.t_ref
  2.8 8.7 %shard_map.82.dec_ref = bf16[256,4096]{1,0:T(8,128)(2,1)} custom-call(bf16[8,32,16384]{2,1,0:T(8,128)(2,1)} %x_ref.1, bf16[512,256]{1,0:T(8,128)(2,1)} %reshape.217.t_ref), custom_call_target="tpu_custom_call" | custom-call | tf_op jit(solution)/shard_map/pallas_call | solution.py:61
  11.5 8.4 %shard_map.83 = f32[256,2048]{1,0:T(8,128)} custom-call(f32[32,1024]{1,0:T(8,128)} %constant.74.clone.c1_ref, f32[32,1024]{1,0:T(8,128)} %constant.75.clone.s1_ref, f32[128,1024]{1,0:T(8,128)} %constant.76.clone.c2_ref, f32[128,1024]{1,0:T(8,128)} %constant.77.clone.s2_ref, bf16[256,4096]{1,0:T(8,128)(2,1)} %shard_map.82.dec_ref), custom_call_target="tpu_custom_call" | custom-call | tf_op jit(solution)/shard_map/pallas_call | solution.py:112
  19.9 3.8 %fusion.41 = (f32[256]{0:T(256)S(1)}, f32[256,1024]{1,0:T(8,128)S(1)}) fusion(f32[1024]{0:T(1024)S(1)} %convert_reduce_fusion, f32[256,2048]{1,0:T(8,128)} %shard_map.83), kind=kOutput, calls=%fused_computation.85 | convolution fusion | flops 1616903936 | bytes 3150848 | tf_op jit(solution)/shard_map/dot_general | solution.py:161
  23.6 0.2 add_divide_fusion
  23.9 0.3 fusion.1
  24.3 0.5 copy.40
  24.8 1.0 %copy.65 = bf16[128,2,8,256]{3,2,1,0:T(8,128)(2,1)} copy(bf16[128,2,8,256]{3,2,0,1:T(8,128)(2,1)S(1)} %bitcast.78) | data formatting | bytes 2097152 | tf_op jit(solution)/shard_map/transpose | solution.py:165
  25.8 11.5 %all-to-all-start = ((bf16[128,16,256]{2,1,0:T(8,128)(2,1)}), bf16[128,16,256]{2,1,0:T(8,128)(2,1)S(1)}, u32[]{:S(2)}, u32[]{:S(2)}) async-start(bf16[128,16,256]{2,1,0:T(8,128)(2,1)} %bitcast.77), calls=%async_computation | async-start | bytes 2097152 | tf_op jit(solution)/shard_map/all_to_all | solution.py:180
  37.6 3.1 %fusion.24 = (f32[1024,64]{1,0:T(8,128)S(1)}, f32[1024,64]{1,0:T(8,128)}) fusion(s32[1024]{0:T(1024)S(1)} %iota_add_fusion), kind=kLoop, calls=%fused_computation.48 | loop fusion | flops 983040 | bytes 528384 | tf_op jit(solution)/shard_map/cos | solution.py:76
  40.8 16.1 %all-to-all-done = bf16[128,16,256]{2,1,0:T(8,128)(2,1)S(1)} async-done(((bf16[128,16,256]{2,1,0:T(8,128)(2,1)}), bf16[128,16,256]{2,1,0:T(8,128)(2,1)S(1)}, u32[]{:S(2)}, u32[]{:S(2)}) %all-to-all-start) | async-done | bytes 1048608 | tf_op jit(solution)/shard_map/all_to_all | solution.py:180
  56.9 0.6 gather_fusion
  57.4 0.6 gather_fusion.1
  58.1 0.2 reshape.220
  58.4 0.2 reshape.221
  58.6 0.3 fusion.26
  58.9 0.3 fusion.25
  59.2 0.3 fusion.5
  59.5 0.3 fusion.4
  59.8 0.5 copy.46
  60.3 4.2 %convolution_bitcast_fusion = f32[8,4,4,8,2,8,2]{0,3,6,1,5,4,2:T(8,128)S(1)} fusion(f32[2,8,8,4,2,16]{5,4,3,2,1,0:T(2,128)S(1)} %bitcast.79, s32[4,16]{1,0:T(4,128)S(1)} %broadcast_add_fusion, pred[4,16]{1,0:T(4,128)(4,1)S(1)} %get-tuple-element.20), kind=kOutput, calls=%fused_computation.10 | convolution fusion | flops 6292480 | bytes 196928 | tf_op jit(solution)/shard_map/dot_general | solution.py:204
  64.5 7.4 %copy.48 = f32[8,4,4,8,2,8,2]{2,1,0,6,5,4,3:T(4,128)} copy(f32[8,4,4,8,2,8,2]{0,3,6,1,5,4,2:T(8,128)S(1)} %convolution_bitcast_fusion) | data formatting | bytes 262144 | tf_op jit(solution)/shard_map/transpose | solution.py:211
  71.9 6.1 %all_to_all.10 = f32[128,1,256]{0,2,1:T(8,128)S(1)} reshape(f32[8,4,4,8,2,8,2]{2,1,0,6,5,4,3:T(4,128)} %copy.48) | data formatting | bytes 262144 | tf_op jit(solution)/shard_map/all_to_all | solution.py:213
  78.1 0.8 copy.49
  78.8 3.9 %all-to-all-start.1 = ((f32[128,1,256]{2,1,0:T(1,128)}), f32[128,1,256]{2,1,0:T(1,128)S(1)}, u32[]{:S(2)}, u32[]{:S(2)}) async-start(f32[128,1,256]{2,1,0:T(1,128)} %copy.49), calls=%async_computation.1 | async-start | bytes 262144 | tf_op jit(solution)/shard_map/all_to_all | solution.py:213
  82.9 9.6 %all-to-all-done.1 = f32[128,1,256]{2,1,0:T(1,128)S(1)} async-done(((f32[128,1,256]{2,1,0:T(1,128)}), f32[128,1,256]{2,1,0:T(1,128)S(1)}, u32[]{:S(2)}, u32[]{:S(2)}) %all-to-all-start.1) | async-done | bytes 131104 | tf_op jit(solution)/shard_map/all_to_all | solution.py:213
  92.7 0.6 copy.51
  93.3 1.2 %reshape.224 = f32[16,2,1024]{2,0,1:T(8,128)S(1)} reshape(f32[8,2,2,128,8]{4,3,1,0,2:T(8,128)S(1)} %copy.51) | data formatting | bytes 262144 | tf_op jit(solution)/shard_map/reshape | solution.py:215
  94.7 1.2 %fusion.9 = f32[128,64]{1,0:T(8,128)S(1)} fusion(f32[128,1024]{1,0:T(8,128)S(1)} %get-tuple-element.11, f32[128,1024]{1,0:T(8,128)S(1)} %get-tuple-element.10, f32[1024,64]{1,0:T(8,128)S(1)} %copy-done.1, f32[1024,64]{1,0:T(8,128)S(1)} %get-tuple-element.16), kind=kOutput, calls=%fused_computation.20 | convolution fusion | flops 201850880 | bytes 1605632 | tf_op jit(solution)/shard_map/dot_general | solution.py:143
  95.9 0.7 reshape_reshape.3
  (30 shorter events, 1.5 us)
Async XLA Ops:
  19.9 4.0 %copy-start = (f32[256,2048]{1,0:T(8,128)S(1)}, f32[256,2048]{1,0:T(8,128)}, u32[]{:S(2)}) copy-start(f32[256,2048]{1,0:T(8,128)} %shard_map.83) | copy-start | bytes 6291460
  24.2 13.1 %copy-start.3 = (s32[16]{0:T(128)S(1)}, s32[16]{0:T(128)}, u32[]{:S(2)}) copy-start(s32[16]{0:T(128)} %param.13) | copy-start | bytes 196
  24.3 13.3 %copy-start.2 = (s32[16,2]{0,1:T(2,128)S(1)}, s32[16,2]{0,1:T(2,128)}, u32[]{:S(2)}) copy-start(s32[16,2]{0,1:T(2,128)} %param.12) | copy-start | bytes 388
  25.8 31.0 %all-to-all-start = ((bf16[128,16,256]{2,1,0:T(8,128)(2,1)}), bf16[128,16,256]{2,1,0:T(8,128)(2,1)S(1)}, u32[]{:S(2)}, u32[]{:S(2)}) async-start(bf16[128,16,256]{2,1,0:T(8,128)(2,1)} %bitcast.77), calls=%async_computation | async-start | bytes 2097152 | tf_op jit(solution)/shard_map/all_to_all | solution.py:180
  78.0 16.6 %copy-start.1 = (f32[1024,64]{1,0:T(8,128)S(1)}, f32[1024,64]{1,0:T(8,128)}, u32[]{:S(2)}) copy-start(f32[1024,64]{1,0:T(8,128)} %get-tuple-element.17) | copy-start | bytes 786436
  78.8 13.8 %all-to-all-start.1 = ((f32[128,1,256]{2,1,0:T(1,128)}), f32[128,1,256]{2,1,0:T(1,128)S(1)}, u32[]{:S(2)}, u32[]{:S(2)}) async-start(f32[128,1,256]{2,1,0:T(1,128)} %copy.49), calls=%async_computation.1 | async-start | bytes 262144 | tf_op jit(solution)/shard_map/all_to_all | solution.py:213

commit v4 on v3

--- a/solution.py
+++ b/solution.py
@@ -192,7 +192,10 @@
 
     real_sum = mm(src_real, dst_real) + mm(src_imag, dst_imag)
     imag_sum = mm(src_real, dst_imag) - mm(src_imag, dst_real)
-    cross = jnp.stack([real_sum, imag_sum], axis=1).reshape(tiles, -1)
+    cross = jnp.stack([real_sum, imag_sum], axis=1)
+    pair_share = BLK * BLK // wide_count
+    cross = cross.reshape(tiles, 2 * group, BLK * BLK // pair_share, pair_share)
+    cross = jnp.transpose(cross, (0, 2, 3, 1))
 
     slot_ids = jnp.arange(SLOTS, dtype=jnp.int32)
     owner_ids = jnp.arange(narrow_count, dtype=jnp.int32)
@@ -201,18 +204,11 @@
     select_all = (owned_all[:, None, :] & (rank_all[:, None, :] == slot_ids[None, :, None])).astype(
         jnp.float32
     )
-    slotted = jnp.dot(
-        select_all.reshape(narrow_count * SLOTS, tiles), cross, precision=lax.Precision.HIGHEST
-    )
-    pair_share = BLK * BLK // wide_count
-    slotted = slotted.reshape(
-        narrow_count, SLOTS, 2, group, BLK, BLK // pair_share, pair_share
-    )
-    send = jnp.transpose(slotted, (4, 5, 0, 1, 2, 3, 6))
-    send = send.reshape(devices, SLOTS * 2 * group * pair_share)
+    send = jnp.einsum("nst,twqv->wnsqv", select_all, cross, precision=lax.Precision.HIGHEST)
+    send = send.reshape(devices, SLOTS * pair_share * 2 * group)
     arrived = lax.all_to_all(send, ("wide", "narrow"), 0, 0, tiled=True)
-    arrived = arrived.reshape(devices, SLOTS, 2, group, pair_share)
-    arrived = jnp.transpose(arrived, (1, 4, 2, 0, 3)).reshape(SLOTS * pair_share, 2, NBINS)
+    arrived = arrived.reshape(devices, SLOTS * pair_share, 2, group)
+    arrived = jnp.transpose(arrived, (1, 2, 0, 3)).reshape(SLOTS * pair_share, 2, NBINS)
     stacked = lag_transform(arrived, NFFT, LAGS, window_total)
     return stacked.reshape(SLOTS, pair_share, LAGS)
 

time: 97 us -> 82 us (0.85)
  local copies, waits for them, and re-layouts: 22.5 us -> 11.4 us
  matrix products: 10.3 us -> 6.46 us
  waiting for transfers between devices: 25.7 us -> 26.8 us
  other arithmetic: 5.33 us -> 4.32 us
    transpose x2, local copies, waits for them, and re-layouts: 7.98 us -> 1.91 us  [the longest x1 1.5 us: on_device(): jnp.einsum('nst,twqv->wnsqv', select_all, cross, precision=lax.Precision....]
    all_to_all x3 -> x2, local copies, waits for them, and re-layouts: 6.99 us -> 2.2 us  [on_device(): arrived = lax.all_to_all(send, ('wide', 'narrow'), 0, 0, tiled=True)]
    dot_general x1, matrix products: 4.17 us -> 0.36 us  [on_device(): jnp.einsum('nst,twqv->wnsqv', select_all, cross, precision=lax.Precision....]
    cos x2, other arithmetic: 3.37 us -> 2.34 us  [trig(): return (jnp.cos(angle), jnp.sin(angle))]
    all_to_all x1, waiting for transfers between devices: 16.1 us -> 17.1 us  [on_device(): spectra = lax.all_to_all(whitened, ('wide', 'narrow'), 0, 0, tiled=True)]
  transfers between devices with their start and end apart: 2 -> 2, of which waited for: 2 -> 2; matrix products, arithmetic and copies ran while one was open for 4% -> 3% of each run, Pallas kernels for 0% -> 0%
where the time goes in v4:
time: 82 us; the launch traced here: 81.6 us
  waiting for transfers between devices  26.8 us (33%)
  Pallas kernels  17 us (21%)
  starting transfers between devices  15.4 us (19%)
  local copies, waits for them, and re-layouts  11.4 us (14%)
  matrix products  6.46 us (8%)
  other arithmetic  4.32 us (5%)
    all_to_all x1, waiting for transfers between devices, on_device(): spectra = lax.all_to_all(whitened, ('wide', 'narrow'), 0, 0, tiled=True)  17.1 us
    all_to_all x1, starting transfers between devices, on_device(): spectra = lax.all_to_all(whitened, ('wide', 'narrow'), 0, 0, tiled=True)  11.5 us
    all_to_all x1, waiting for transfers between devices, on_device(): arrived = lax.all_to_all(send, ('wide', 'narrow'), 0, 0, tiled=True)  9.65 us
    pallas_call x1, Pallas kernels, decimate(): pl.pallas_call(decim_kernel, grid=(row_length // chunk,), in_specs=[pl.Bl...  8.62 us
    pallas_call x1, Pallas kernels, dft(): pl.pallas_call(functools.partial(dft_kernel, halves=halves), grid=(2 * ha...  8.34 us
    all_to_all x1, starting transfers between devices, on_device(): arrived = lax.all_to_all(send, ('wide', 'narrow'), 0, 0, tiled=True)  3.9 us
    dot_general x1, matrix products, whiten(): jnp.dot(magnitude, smoother(NBINS, SMOOTH), precision=lax.Precision.HIGH)  3.78 us
    cos x2, other arithmetic, trig(): return (jnp.cos(angle), jnp.sin(angle))  2.34 us
  transfers between devices with their start and end apart: 2, of which 2 were waited for; matrix products, arithmetic and copies ran while one was open for 3% of the time, Pallas kernels for 0%

profile of v4, /device:TPU:1, one launch (start us, length us, event | category | flops | bytes accessed | tf_op | source)
XLA Modules:
  0.0 81.6 jit_solution(6435019703008076671)
XLA Ops:
  0.2 0.7 convert_element_type.42
  1.2 0.8 tile.10
  2.1 0.8 reshape.190.t_ref
  2.8 8.6 %shard_map.82.dec_ref = bf16[256,4096]{1,0:T(8,128)(2,1)} custom-call(bf16[8,32,16384]{2,1,0:T(8,128)(2,1)} %x_ref.1, bf16[512,256]{1,0:T(8,128)(2,1)} %reshape.190.t_ref), custom_call_target="tpu_custom_call" | custom-call | tf_op jit(solution)/shard_map/pallas_call | solution.py:61
  11.4 8.3 %shard_map.83 = f32[256,2048]{1,0:T(8,128)} custom-call(f32[32,1024]{1,0:T(8,128)} %constant.74.clone.c1_ref, f32[32,1024]{1,0:T(8,128)} %constant.75.clone.s1_ref, f32[128,1024]{1,0:T(8,128)} %constant.76.clone.c2_ref, f32[128,1024]{1,0:T(8,128)} %constant.77.clone.s2_ref, bf16[256,4096]{1,0:T(8,128)(2,1)} %shard_map.82.dec_ref), custom_call_target="tpu_custom_call" | custom-call | tf_op jit(solution)/shard_map/pallas_call | solution.py:112
  19.8 3.8 %fusion.40 = (f32[256]{0:T(256)S(1)}, f32[256,1024]{1,0:T(8,128)S(1)}) fusion(f32[1024]{0:T(1024)S(1)} %convert_reduce_fusion, f32[256,2048]{1,0:T(8,128)} %shard_map.83), kind=kOutput, calls=%fused_computation.84 | convolution fusion | flops 1616903936 | bytes 3150848 | tf_op jit(solution)/shard_map/dot_general | solution.py:161
  23.6 0.2 add_divide_fusion
  23.8 0.3 fusion.1
  24.2 0.5 copy.45
  24.7 1.1 %copy.69 = bf16[128,2,8,256]{3,2,1,0:T(8,128)(2,1)} copy(bf16[128,2,8,256]{3,2,0,1:T(8,128)(2,1)S(1)} %bitcast.72) | data formatting | bytes 2097152 | tf_op jit(solution)/shard_map/transpose | solution.py:165
  25.8 11.5 %all-to-all-start = ((bf16[128,16,256]{2,1,0:T(8,128)(2,1)}), bf16[128,16,256]{2,1,0:T(8,128)(2,1)S(1)}, u32[]{:S(2)}, u32[]{:S(2)}) async-start(bf16[128,16,256]{2,1,0:T(8,128)(2,1)} %bitcast.70), calls=%async_computation | async-start | bytes 2097152 | tf_op jit(solution)/shard_map/all_to_all | solution.py:180
  37.6 2.1 %fusion.23 = (f32[1024,64]{1,0:T(8,128)S(1)}, f32[1024,64]{1,0:T(8,128)S(1)}) fusion(s32[1024]{0:T(1024)S(1)} %iota_add_fusion), kind=kLoop, calls=%fused_computation.49 | loop fusion | flops 983040 | bytes 528384 | tf_op jit(solution)/shard_map/cos | solution.py:76
  39.7 17.1 %all-to-all-done = bf16[128,16,256]{2,1,0:T(8,128)(2,1)S(1)} async-done(((bf16[128,16,256]{2,1,0:T(8,128)(2,1)}), bf16[128,16,256]{2,1,0:T(8,128)(2,1)S(1)}, u32[]{:S(2)}, u32[]{:S(2)}) %all-to-all-start) | async-done | bytes 1048608 | tf_op jit(solution)/shard_map/all_to_all | solution.py:180
  56.8 0.6 gather_fusion
  57.4 0.6 gather_fusion.1
  58.0 0.2 reshape.193
  58.3 0.2 reshape.194
  58.5 0.3 fusion.25
  58.8 0.3 fusion.24
  59.1 0.3 fusion.5
  59.4 0.3 fusion.4
  59.8 0.7 copy.51
  60.5 0.3 copy.52
  60.8 0.4 convolution_bitcast_fusion
  61.2 1.5 %copy.53 = f32[32,4,8,2,16]{4,3,2,1,0:T(2,128)S(1)} copy(f32[32,4,8,2,16]{0,2,1,4,3:T(8,128)S(1)} %convolution_bitcast_fusion) | data formatting | bytes 262144 | tf_op jit(solution)/shard_map/nst,twqv->wnsqv/transpose | solution.py:207
  62.7 2.1 %all_to_all.12 = f32[128,1,256]{2,1,0:T(1,128)} reshape(f32[32,4,8,2,16]{4,3,2,1,0:T(2,128)S(1)} %copy.53) | data formatting | bytes 262144 | tf_op jit(solution)/shard_map/all_to_all | solution.py:209
  64.8 3.9 %all-to-all-start.1 = ((f32[128,1,256]{2,1,0:T(1,128)}), f32[128,1,256]{2,1,0:T(1,128)S(1)}, u32[]{:S(2)}, u32[]{:S(2)}) async-start(f32[128,1,256]{2,1,0:T(1,128)} %all_to_all.12), calls=%async_computation.1 | async-start | bytes 262144 | tf_op jit(solution)/shard_map/all_to_all | solution.py:209
  68.7 0.2 fusion.30
  68.9 9.7 %all-to-all-done.1 = f32[128,1,256]{2,1,0:T(1,128)S(1)} async-done(((f32[128,1,256]{2,1,0:T(1,128)}), f32[128,1,256]{2,1,0:T(1,128)S(1)}, u32[]{:S(2)}, u32[]{:S(2)}) %all-to-all-start.1) | async-done | bytes 131104 | tf_op jit(solution)/shard_map/all_to_all | solution.py:209
  78.7 0.4 copy.56
  79.7 1.2 %fusion.9 = f32[128,64]{1,0:T(8,128)S(1)} fusion(f32[128,1024]{1,0:T(8,128)S(1)} %get-tuple-element.13, f32[128,1024]{1,0:T(8,128)S(1)} %get-tuple-element.12, f32[1024,64]{1,0:T(8,128)S(1)} %get-tuple-element.17, f32[1024,64]{1,0:T(8,128)S(1)} %get-tuple-element.16), kind=kOutput, calls=%fused_computation.20 | convolution fusion | flops 201850880 | bytes 1605632 | tf_op jit(solution)/shard_map/dot_general | solution.py:143
  80.9 0.7 reshape_reshape.3
  (29 shorter events, 1.7 us)
Async XLA Ops:
  19.8 4.0 %copy-start = (f32[256,2048]{1,0:T(8,128)S(1)}, f32[256,2048]{1,0:T(8,128)}, u32[]{:S(2)}) copy-start(f32[256,2048]{1,0:T(8,128)} %shard_map.83) | copy-start | bytes 6291460
  24.2 13.1 %copy-start.2 = (s32[16]{0:T(128)S(1)}, s32[16]{0:T(128)}, u32[]{:S(2)}) copy-start(s32[16]{0:T(128)} %param.13) | copy-start | bytes 196
  24.2 13.3 %copy-start.1 = (s32[16,2]{0,1:T(2,128)S(1)}, s32[16,2]{0,1:T(2,128)}, u32[]{:S(2)}) copy-start(s32[16,2]{0,1:T(2,128)} %param.12) | copy-start | bytes 388
  25.8 31.0 %all-to-all-start = ((bf16[128,16,256]{2,1,0:T(8,128)(2,1)}), bf16[128,16,256]{2,1,0:T(8,128)(2,1)S(1)}, u32[]{:S(2)}, u32[]{:S(2)}) async-start(bf16[128,16,256]{2,1,0:T(8,128)(2,1)} %bitcast.70), calls=%async_computation | async-start | bytes 2097152 | tf_op jit(solution)/shard_map/all_to_all | solution.py:180
  64.8 13.8 %all-to-all-start.1 = ((f32[128,1,256]{2,1,0:T(1,128)}), f32[128,1,256]{2,1,0:T(1,128)S(1)}, u32[]{:S(2)}, u32[]{:S(2)}) async-start(f32[128,1,256]{2,1,0:T(1,128)} %all_to_all.12), calls=%async_computation.1 | async-start | bytes 262144 | tf_op jit(solution)/shard_map/all_to_all | solution.py:209

commit v5 on v4

--- a/solution.py
+++ b/solution.py
@@ -53,7 +53,7 @@
         carry_ref[...] = both[:, block:]
 
 
-def decimate(samples, filter_taps, chunk=2048):
+def decimate(samples, filter_taps, chunk=8192):
     channels, windows, row_length = samples.shape
     block_size = min(128, row_length // DECIM)
     table = fir_table(filter_taps, block_size)

time: 82 us -> 79 us (0.963)
  Pallas kernels: 17 us -> 14.2 us
    pallas_call x1, Pallas kernels: 8.62 us -> 5.85 us  [decimate(): pl.pallas_call(decim_kernel, grid=(row_length // chunk,), in_specs=[pl.Bl...]
where the time goes in v5:
time: 79 us; the launch traced here: 78.8 us
  waiting for transfers between devices  26.8 us (34%)
  starting transfers between devices  15.4 us (19%)
  Pallas kernels  14.2 us (18%)
  local copies, waits for them, and re-layouts  11.4 us (14%)
  matrix products  6.46 us (8%)
  other arithmetic  4.32 us (5%)
    all_to_all x1, waiting for transfers between devices, on_device(): spectra = lax.all_to_all(whitened, ('wide', 'narrow'), 0, 0, tiled=True)  17.1 us
    all_to_all x1, starting transfers between devices, on_device(): spectra = lax.all_to_all(whitened, ('wide', 'narrow'), 0, 0, tiled=True)  11.5 us
    all_to_all x1, waiting for transfers between devices, on_device(): arrived = lax.all_to_all(send, ('wide', 'narrow'), 0, 0, tiled=True)  9.65 us
    pallas_call x1, Pallas kernels, dft(): pl.pallas_call(functools.partial(dft_kernel, halves=halves), grid=(2 * ha...  8.34 us
    pallas_call x1, Pallas kernels, decimate(): pl.pallas_call(decim_kernel, grid=(row_length // chunk,), in_specs=[pl.Bl...  5.85 us
    all_to_all x1, starting transfers between devices, on_device(): arrived = lax.all_to_all(send, ('wide', 'narrow'), 0, 0, tiled=True)  3.9 us
    dot_general x1, matrix products, whiten(): jnp.dot(magnitude, smoother(NBINS, SMOOTH), precision=lax.Precision.HIGH)  3.78 us
    cos x2, other arithmetic, trig(): return (jnp.cos(angle), jnp.sin(angle))  2.34 us
  transfers between devices with their start and end apart: 2, of which 2 were waited for; matrix products, arithmetic and copies ran while one was open for 3% of the time, Pallas kernels for 0%

profile of v5, /device:TPU:1, one launch (start us, length us, event | category | flops | bytes accessed | tf_op | source)
XLA Modules:
  0.0 78.8 jit_solution(16624727123260282000)
XLA Ops:
  0.2 0.7 convert_element_type.42
  1.2 0.8 tile.10
  2.1 0.8 reshape.190.t_ref
  2.8 5.8 %shard_map.82.dec_ref = bf16[256,4096]{1,0:T(8,128)(2,1)} custom-call(bf16[8,32,16384]{2,1,0:T(8,128)(2,1)} %x_ref.1, bf16[512,256]{1,0:T(8,128)(2,1)} %reshape.190.t_ref), custom_call_target="tpu_custom_call" | custom-call | tf_op jit(solution)/shard_map/pallas_call | solution.py:61
  8.7 8.3 %shard_map.83 = f32[256,2048]{1,0:T(8,128)} custom-call(f32[32,1024]{1,0:T(8,128)} %constant.74.clone.c1_ref, f32[32,1024]{1,0:T(8,128)} %constant.75.clone.s1_ref, f32[128,1024]{1,0:T(8,128)} %constant.76.clone.c2_ref, f32[128,1024]{1,0:T(8,128)} %constant.77.clone.s2_ref, bf16[256,4096]{1,0:T(8,128)(2,1)} %shard_map.82.dec_ref), custom_call_target="tpu_custom_call" | custom-call | tf_op jit(solution)/shard_map/pallas_call | solution.py:112
  17.0 3.8 %fusion.40 = (f32[256]{0:T(256)S(1)}, f32[256,1024]{1,0:T(8,128)S(1)}) fusion(f32[1024]{0:T(1024)S(1)} %convert_reduce_fusion, f32[256,2048]{1,0:T(8,128)} %shard_map.83), kind=kOutput, calls=%fused_computation.84 | convolution fusion | flops 1616903936 | bytes 3150848 | tf_op jit(solution)/shard_map/dot_general | solution.py:161
  20.8 0.2 add_divide_fusion
  21.1 0.3 fusion.1
  21.4 0.5 copy.45
  22.0 1.1 %copy.69 = bf16[128,2,8,256]{3,2,1,0:T(8,128)(2,1)} copy(bf16[128,2,8,256]{3,2,0,1:T(8,128)(2,1)S(1)} %bitcast.72) | data formatting | bytes 2097152 | tf_op jit(solution)/shard_map/transpose | solution.py:165
  23.0 11.5 %all-to-all-start = ((bf16[128,16,256]{2,1,0:T(8,128)(2,1)}), bf16[128,16,256]{2,1,0:T(8,128)(2,1)S(1)}, u32[]{:S(2)}, u32[]{:S(2)}) async-start(bf16[128,16,256]{2,1,0:T(8,128)(2,1)} %bitcast.70), calls=%async_computation | async-start | bytes 2097152 | tf_op jit(solution)/shard_map/all_to_all | solution.py:180
  34.8 2.1 %fusion.23 = (f32[1024,64]{1,0:T(8,128)S(1)}, f32[1024,64]{1,0:T(8,128)S(1)}) fusion(s32[1024]{0:T(1024)S(1)} %iota_add_fusion), kind=kLoop, calls=%fused_computation.49 | loop fusion | flops 983040 | bytes 528384 | tf_op jit(solution)/shard_map/cos | solution.py:76
  36.9 17.1 %all-to-all-done = bf16[128,16,256]{2,1,0:T(8,128)(2,1)S(1)} async-done(((bf16[128,16,256]{2,1,0:T(8,128)(2,1)}), bf16[128,16,256]{2,1,0:T(8,128)(2,1)S(1)}, u32[]{:S(2)}, u32[]{:S(2)}) %all-to-all-start) | async-done | bytes 1048608 | tf_op jit(solution)/shard_map/all_to_all | solution.py:180
  54.0 0.6 gather_fusion
  54.6 0.6 gather_fusion.1
  55.3 0.2 reshape.193
  55.5 0.2 reshape.194
  55.8 0.3 fusion.25
  56.0 0.3 fusion.24
  56.3 0.3 fusion.5
  56.6 0.3 fusion.4
  57.0 0.7 copy.51
  57.7 0.3 copy.52
  58.0 0.4 convolution_bitcast_fusion
  58.4 1.5 %copy.53 = f32[32,4,8,2,16]{4,3,2,1,0:T(2,128)S(1)} copy(f32[32,4,8,2,16]{0,2,1,4,3:T(8,128)S(1)} %convolution_bitcast_fusion) | data formatting | bytes 262144 | tf_op jit(solution)/shard_map/nst,twqv->wnsqv/transpose | solution.py:207
  59.9 2.1 %all_to_all.12 = f32[128,1,256]{2,1,0:T(1,128)} reshape(f32[32,4,8,2,16]{4,3,2,1,0:T(2,128)S(1)} %copy.53) | data formatting | bytes 262144 | tf_op jit(solution)/shard_map/all_to_all | solution.py:209
  62.0 3.9 %all-to-all-start.1 = ((f32[128,1,256]{2,1,0:T(1,128)}), f32[128,1,256]{2,1,0:T(1,128)S(1)}, u32[]{:S(2)}, u32[]{:S(2)}) async-start(f32[128,1,256]{2,1,0:T(1,128)} %all_to_all.12), calls=%async_computation.1 | async-start | bytes 262144 | tf_op jit(solution)/shard_map/all_to_all | solution.py:209
  65.9 0.2 fusion.30
  66.1 9.7 %all-to-all-done.1 = f32[128,1,256]{2,1,0:T(1,128)S(1)} async-done(((f32[128,1,256]{2,1,0:T(1,128)}), f32[128,1,256]{2,1,0:T(1,128)S(1)}, u32[]{:S(2)}, u32[]{:S(2)}) %all-to-all-start.1) | async-done | bytes 131104 | tf_op jit(solution)/shard_map/all_to_all | solution.py:209
  75.9 0.4 copy.56
  76.9 1.2 %fusion.9 = f32[128,64]{1,0:T(8,128)S(1)} fusion(f32[128,1024]{1,0:T(8,128)S(1)} %get-tuple-element.13, f32[128,1024]{1,0:T(8,128)S(1)} %get-tuple-element.12, f32[1024,64]{1,0:T(8,128)S(1)} %get-tuple-element.17, f32[1024,64]{1,0:T(8,128)S(1)} %get-tuple-element.16), kind=kOutput, calls=%fused_computation.20 | convolution fusion | flops 201850880 | bytes 1605632 | tf_op jit(solution)/shard_map/dot_general | solution.py:143
  78.1 0.7 reshape_reshape.3
  (29 shorter events, 1.7 us)
Async XLA Ops:
  17.0 4.0 %copy-start = (f32[256,2048]{1,0:T(8,128)S(1)}, f32[256,2048]{1,0:T(8,128)}, u32[]{:S(2)}) copy-start(f32[256,2048]{1,0:T(8,128)} %shard_map.83) | copy-start | bytes 6291460
  21.4 13.1 %copy-start.2 = (s32[16]{0:T(128)S(1)}, s32[16]{0:T(128)}, u32[]{:S(2)}) copy-start(s32[16]{0:T(128)} %param.13) | copy-start | bytes 196
  21.4 13.3 %copy-start.1 = (s32[16,2]{0,1:T(2,128)S(1)}, s32[16,2]{0,1:T(2,128)}, u32[]{:S(2)}) copy-start(s32[16,2]{0,1:T(2,128)} %param.12) | copy-start | bytes 388
  23.0 31.0 %all-to-all-start = ((bf16[128,16,256]{2,1,0:T(8,128)(2,1)}), bf16[128,16,256]{2,1,0:T(8,128)(2,1)S(1)}, u32[]{:S(2)}, u32[]{:S(2)}) async-start(bf16[128,16,256]{2,1,0:T(8,128)(2,1)} %bitcast.70), calls=%async_computation | async-start | bytes 2097152 | tf_op jit(solution)/shard_map/all_to_all | solution.py:180
  62.0 13.8 %all-to-all-start.1 = ((f32[128,1,256]{2,1,0:T(1,128)}), f32[128,1,256]{2,1,0:T(1,128)S(1)}, u32[]{:S(2)}, u32[]{:S(2)}) async-start(f32[128,1,256]{2,1,0:T(1,128)} %all_to_all.12), calls=%async_computation.1 | async-start | bytes 262144 | tf_op jit(solution)/shard_map/all_to_all | solution.py:209

commit v6 on v5

--- a/solution.py
+++ b/solution.py
@@ -179,36 +179,32 @@
     whitened = whiten(decimated, devices, group)
     spectra = lax.all_to_all(whitened, ("wide", "narrow"), 0, 0, tiled=True)
 
-    source = jnp.take(spectra, tile_pairs[:, 0], axis=0)
-    target = jnp.take(spectra, tile_pairs[:, 1], axis=0)
     tiles = tile_pairs.shape[0]
-    source = source.reshape(tiles, 2, group, BLK, window_total)
-    target = target.reshape(tiles, 2, group, BLK, window_total)
-    src_real, src_imag = source[:, 0], source[:, 1]
-    dst_real, dst_imag = target[:, 0], target[:, 1]
-
-    def mm(a, b):
-        return jnp.einsum("tbiw,tbjw->tbij", a, b, preferred_element_type=jnp.float32)
-
-    real_sum = mm(src_real, dst_real) + mm(src_imag, dst_imag)
-    imag_sum = mm(src_real, dst_imag) - mm(src_imag, dst_real)
-    cross = jnp.stack([real_sum, imag_sum], axis=1)
-    pair_share = BLK * BLK // wide_count
-    cross = cross.reshape(tiles, 2 * group, BLK * BLK // pair_share, pair_share)
-    cross = jnp.transpose(cross, (0, 2, 3, 1))
-
     slot_ids = jnp.arange(SLOTS, dtype=jnp.int32)
     owner_ids = jnp.arange(narrow_count, dtype=jnp.int32)
     owned_all = tile_owners[None, :] == owner_ids[:, None]
     rank_all = jnp.cumsum(owned_all.astype(jnp.int32), axis=1) - 1
-    select_all = (owned_all[:, None, :] & (rank_all[:, None, :] == slot_ids[None, :, None])).astype(
-        jnp.float32
-    )
-    send = jnp.einsum("nst,twqv->wnsqv", select_all, cross, precision=lax.Precision.HIGHEST)
-    send = send.reshape(devices, SLOTS * pair_share * 2 * group)
-    arrived = lax.all_to_all(send, ("wide", "narrow"), 0, 0, tiled=True)
-    arrived = arrived.reshape(devices, SLOTS * pair_share, 2, group)
-    arrived = jnp.transpose(arrived, (1, 2, 0, 3)).reshape(SLOTS * pair_share, 2, NBINS)
+    select_all = owned_all[:, None, :] & (rank_all[:, None, :] == slot_ids[None, :, None])
+    slot_tile = jnp.sum(select_all * jnp.arange(tiles, dtype=jnp.int32), axis=2).reshape(-1)
+    live = jnp.any(select_all, axis=2).astype(jnp.float32)
+    slot_pairs = jnp.take(tile_pairs, slot_tile, axis=0)
+    shape = (narrow_count, SLOTS, 2, group, BLK, window_total)
+    source = jnp.take(spectra, slot_pairs[:, 0], axis=0).reshape(shape)
+    target = jnp.take(spectra, slot_pairs[:, 1], axis=0).reshape(shape)
+    src_real, src_imag = source[:, :, 0], source[:, :, 1]
+    dst_real, dst_imag = target[:, :, 0], target[:, :, 1]
+
+    def mm(a, b):
+        return jnp.einsum("nsbiw,nsbjw->nijsb", a, b, preferred_element_type=jnp.float32)
+
+    real_sum = mm(src_real, dst_real) + mm(src_imag, dst_imag)
+    imag_sum = mm(src_real, dst_imag) - mm(src_imag, dst_real)
+    cross = jnp.stack([real_sum, imag_sum], axis=4) * live[:, None, None, :, None, None]
+    pair_share = BLK * BLK // wide_count
+    send = cross.reshape(devices, pair_share * SLOTS * 2 * group)
+    arrived = lax.all_to_all(send, ("narrow", "wide"), 0, 0, tiled=True)
+    arrived = arrived.reshape(narrow_count, wide_count, pair_share, SLOTS, 2, group)
+    arrived = jnp.transpose(arrived, (3, 2, 4, 1, 0, 5)).reshape(SLOTS * pair_share, 2, NBINS)
     stacked = lag_transform(arrived, NFFT, LAGS, window_total)
     return stacked.reshape(SLOTS, pair_share, LAGS)
 

time: 79 us -> 87.4 us (1.11)
  local copies, waits for them, and re-layouts: 11.4 us -> 20.3 us
  waiting for transfers between devices: 26.8 us -> 24.4 us
  other arithmetic: 4.32 us -> 6 us
    mul x0 -> x2, local copies, waits for them, and re-layouts: none -> 7.88 us  [on_device(): jnp.stack([real_sum, imag_sum], axis=4) * live[:, None, None, :, None, None]]
    reshape x3 -> x6, local copies, waits for them, and re-layouts: 0.79 us -> 3.81 us  [the longest x1 2.51 us: on_device(): jnp.transpose(arrived, (3, 2, 4, 1, 0, 5))]
    all_to_all x1, waiting for transfers between devices: 17.1 us -> 14.6 us  [on_device(): spectra = lax.all_to_all(whitened, ('wide', 'narrow'), 0, 0, tiled=True)]
    all_to_all x2 -> x1, local copies, waits for them, and re-layouts: 2.2 us -> 0.09 us  [on_device(): arrived = lax.all_to_all(send, ('narrow', 'wide'), 0, 0, tiled=True)]
    unnamed x7 -> x10, local copies, waits for them, and re-layouts: 0.11 us -> 1.53 us
    cos x2, other arithmetic: 2.34 us -> 3.37 us  [trig(): return (jnp.cos(angle), jnp.sin(angle))]
    transpose x2 -> x1, local copies, waits for them, and re-layouts: 1.91 us -> 0.91 us  [on_device(): jnp.transpose(arrived, (3, 2, 4, 1, 0, 5))]
  transfers between devices with their start and end apart: 2 -> 2, of which waited for: 2 -> 2; matrix products, arithmetic and copies ran while one was open for 3% -> 6% of each run, Pallas kernels for 0% -> 0%
where the time goes in v6:
time: 87.4 us; the launch traced here: 87.1 us
  waiting for transfers between devices  24.4 us (28%)
  local copies, waits for them, and re-layouts  20.3 us (23%)
  starting transfers between devices  15.4 us (18%)
  Pallas kernels  14.2 us (16%)
  matrix products  6.49 us (7%)
  other arithmetic  6 us (7%)
    all_to_all x1, waiting for transfers between devices, on_device(): spectra = lax.all_to_all(whitened, ('wide', 'narrow'), 0, 0, tiled=True)  14.6 us
    all_to_all x1, starting transfers between devices, on_device(): spectra = lax.all_to_all(whitened, ('wide', 'narrow'), 0, 0, tiled=True)  11.5 us
    all_to_all x1, waiting for transfers between devices, on_device(): arrived = lax.all_to_all(send, ('narrow', 'wide'), 0, 0, tiled=True)  9.79 us
    pallas_call x1, Pallas kernels, dft(): pl.pallas_call(functools.partial(dft_kernel, halves=halves), grid=(2 * ha...  8.36 us
    mul x2, local copies, waits for them, and re-layouts, on_device(): jnp.stack([real_sum, imag_sum], axis=4) * live[:, None, None, :, None, None]  7.88 us
    pallas_call x1, Pallas kernels, decimate(): pl.pallas_call(decim_kernel, grid=(row_length // chunk,), in_specs=[pl.Bl...  5.8 us
    all_to_all x1, starting transfers between devices, on_device(): arrived = lax.all_to_all(send, ('narrow', 'wide'), 0, 0, tiled=True)  3.91 us
    dot_general x1, matrix products, whiten(): jnp.dot(magnitude, smoother(NBINS, SMOOTH), precision=lax.Precision.HIGH)  3.63 us
  transfers between devices with their start and end apart: 2, of which 2 were waited for; matrix products, arithmetic and copies ran while one was open for 6% of the time, Pallas kernels for 0%

profile of v6, /device:TPU:1, one launch (start us, length us, event | category | flops | bytes accessed | tf_op | source)
XLA Modules:
  0.0 87.1 jit_solution(8723851014166240141)
XLA Ops:
  0.2 0.7 convert_element_type.49
  1.2 0.8 tile.10
  2.1 0.8 reshape.248.t_ref
  2.8 5.8 %shard_map.82.dec_ref = bf16[256,4096]{1,0:T(8,128)(2,1)} custom-call(bf16[8,32,16384]{2,1,0:T(8,128)(2,1)} %x_ref.1, bf16[512,256]{1,0:T(8,128)(2,1)} %reshape.248.t_ref), custom_call_target="tpu_custom_call" | custom-call | tf_op jit(solution)/shard_map/pallas_call | solution.py:61
  8.6 8.4 %shard_map.83 = f32[256,2048]{1,0:T(8,128)} custom-call(f32[32,1024]{1,0:T(8,128)} %constant.92.clone.c1_ref, f32[32,1024]{1,0:T(8,128)} %constant.93.clone.s1_ref, f32[128,1024]{1,0:T(8,128)} %constant.94.clone.c2_ref, f32[128,1024]{1,0:T(8,128)} %constant.95.clone.s2_ref, bf16[256,4096]{1,0:T(8,128)(2,1)} %shard_map.82.dec_ref), custom_call_target="tpu_custom_call" | custom-call | tf_op jit(solution)/shard_map/pallas_call | solution.py:112
  17.0 3.6 %fusion.37 = (f32[256]{0:T(256)S(1)}, f32[256,1024]{1,0:T(8,128)S(1)}) fusion(f32[1024]{0:T(1024)S(1)} %convert_reduce_fusion, f32[256,2048]{1,0:T(8,128)} %shard_map.83), kind=kOutput, calls=%fused_computation.90 | convolution fusion | flops 1616903936 | bytes 3150848 | tf_op jit(solution)/shard_map/dot_general | solution.py:161
  20.9 1.3 %copy-done = f32[256,2048]{1,0:T(8,128)S(1)} copy-done((f32[256,2048]{1,0:T(8,128)S(1)}, f32[256,2048]{1,0:T(8,128)}, u32[]{:S(2)}) %copy-start) | copy-done | bytes 2097176
  22.2 0.3 fusion.1
  22.6 0.5 copy.41
  23.1 1.1 %copy.59 = bf16[128,2,8,256]{3,2,1,0:T(8,128)(2,1)} copy(bf16[128,2,8,256]{3,2,0,1:T(8,128)(2,1)S(1)} %bitcast.57) | data formatting | bytes 2097152 | tf_op jit(solution)/shard_map/transpose | solution.py:165
  24.2 11.5 %all-to-all-start = ((bf16[128,16,256]{2,1,0:T(8,128)(2,1)}), bf16[128,16,256]{2,1,0:T(8,128)(2,1)S(1)}, u32[]{:S(2)}, u32[]{:S(2)}) async-start(bf16[128,16,256]{2,1,0:T(8,128)(2,1)} %bitcast.56), calls=%async_computation | async-start | bytes 2097152 | tf_op jit(solution)/shard_map/all_to_all | solution.py:180
  36.5 0.6 gather_fusion
  37.4 3.1 %fusion.24 = (f32[1024,64]{1,0:T(8,128)S(1)}, f32[1024,64]{1,0:T(8,128)}) fusion(s32[1024]{0:T(1024)S(1)} %iota_add_fusion), kind=kLoop, calls=%fused_computation.48 | loop fusion | flops 983040 | bytes 528384 | tf_op jit(solution)/shard_map/cos | solution.py:76
  40.6 14.6 %all-to-all-done = bf16[128,16,256]{2,1,0:T(8,128)(2,1)S(1)} async-done(((bf16[128,16,256]{2,1,0:T(8,128)(2,1)}), bf16[128,16,256]{2,1,0:T(8,128)(2,1)S(1)}, u32[]{:S(2)}, u32[]{:S(2)}) %all-to-all-start) | async-done | bytes 1048608 | tf_op jit(solution)/shard_map/all_to_all | solution.py:180
  55.2 0.6 gather_fusion.1
  55.9 0.4 reshape.253
  56.3 0.6 gather_fusion.2
  57.0 0.4 reshape.254
  57.5 0.4 fusion.22
  57.9 0.4 fusion.23
  58.3 0.4 fusion.5
  58.7 0.4 fusion.4
  59.2 0.2 maximum_multiply_fusion.1
  59.4 2.8 %copy.47 = f32[4,8,8,8,2,8]{5,4,3,2,1,0:T(2,128)} copy(f32[4,8,8,8,2,8]{1,2,5,3,0,4:T(8,128)S(1)} %maximum_multiply_fusion.1) | data formatting | bytes 262144 | tf_op jit(solution)/shard_map/mul | solution.py:202
  62.2 5.0 %mul.244 = f32[128,1,256]{2,1,0:T(1,128)} reshape(f32[4,8,8,8,2,8]{5,4,3,2,1,0:T(2,128)} %copy.47) | data formatting | bytes 262144 | tf_op jit(solution)/shard_map/mul | solution.py:202
  67.3 3.9 %all-to-all-start.1 = ((f32[128,1,256]{2,1,0:T(1,128)}), f32[128,1,256]{2,1,0:T(1,128)S(1)}, u32[]{:S(2)}, u32[]{:S(2)}) async-start(f32[128,1,256]{2,1,0:T(1,128)} %mul.244), calls=%async_computation.1 | async-start | bytes 262144 | tf_op jit(solution)/shard_map/all_to_all | solution.py:205
  71.4 9.8 %all-to-all-done.1 = f32[128,1,256]{2,1,0:T(1,128)S(1)} async-done(((f32[128,1,256]{2,1,0:T(1,128)}), f32[128,1,256]{2,1,0:T(1,128)S(1)}, u32[]{:S(2)}, u32[]{:S(2)}) %all-to-all-start.1) | async-done | bytes 131104 | tf_op jit(solution)/shard_map/all_to_all | solution.py:205
  81.3 0.3 reshape.255
  81.6 0.9 %copy.50 = f32[8,2,2,32,4,8]{5,4,3,1,0,2:T(4,128)S(1)} copy(f32[8,2,2,32,4,8]{3,4,5,2,0,1:T(4,128)S(1)} %bitcast.58) | data formatting | bytes 262144 | tf_op jit(solution)/shard_map/transpose | solution.py:207
  82.5 2.5 %reshape.256 = f32[16,2,1024]{2,0,1:T(8,128)S(1)} reshape(f32[8,2,2,32,4,8]{5,4,3,1,0,2:T(4,128)S(1)} %copy.50) | data formatting | bytes 262144 | tf_op jit(solution)/shard_map/reshape | solution.py:207
  85.2 1.2 %fusion.9 = f32[128,64]{1,0:T(8,128)S(1)} fusion(f32[128,1024]{1,0:T(8,128)S(1)} %get-tuple-element.9, f32[128,1024]{1,0:T(8,128)S(1)} %get-tuple-element.8, f32[1024,64]{1,0:T(8,128)S(1)} %copy-done.1, f32[1024,64]{1,0:T(8,128)S(1)} %get-tuple-element.14), kind=kOutput, calls=%fused_computation.20 | convolution fusion | flops 201850880 | bytes 1605632 | tf_op jit(solution)/shard_map/dot_general | solution.py:143
  86.4 0.7 reshape_reshape.3
  (42 shorter events, 2.6 us)
Async XLA Ops:
  20.6 1.6 %copy-start = (f32[256,2048]{1,0:T(8,128)S(1)}, f32[256,2048]{1,0:T(8,128)}, u32[]{:S(2)}) copy-start(f32[256,2048]{1,0:T(8,128)} %shard_map.83) | copy-start | bytes 6291460
  23.1 12.6 %copy-start.3 = (s32[16]{0:T(128)S(1)}, s32[16]{0:T(128)}, u32[]{:S(2)}) copy-start(s32[16]{0:T(128)} %param.13) | copy-start | bytes 196
  23.1 13.3 %copy-start.2 = (s32[16,2]{0,1:T(2,128)S(1)}, s32[16,2]{0,1:T(2,128)}, u32[]{:S(2)}) copy-start(s32[16,2]{0,1:T(2,128)} %param.12) | copy-start | bytes 388
  24.2 31.0 %all-to-all-start = ((bf16[128,16,256]{2,1,0:T(8,128)(2,1)}), bf16[128,16,256]{2,1,0:T(8,128)(2,1)S(1)}, u32[]{:S(2)}, u32[]{:S(2)}) async-start(bf16[128,16,256]{2,1,0:T(8,128)(2,1)} %bitcast.56), calls=%async_computation | async-start | bytes 2097152 | tf_op jit(solution)/shard_map/all_to_all | solution.py:180
  67.3 13.9 %all-to-all-start.1 = ((f32[128,1,256]{2,1,0:T(1,128)}), f32[128,1,256]{2,1,0:T(1,128)S(1)}, u32[]{:S(2)}, u32[]{:S(2)}) async-start(f32[128,1,256]{2,1,0:T(1,128)} %mul.244), calls=%async_computation.1 | async-start | bytes 262144 | tf_op jit(solution)/shard_map/all_to_all | solution.py:205
  82.5 2.7 %copy-start.1 = (f32[1024,64]{1,0:T(8,128)S(1)}, f32[1024,64]{1,0:T(8,128)}, u32[]{:S(2)}) copy-start(f32[1024,64]{1,0:T(8,128)} %get-tuple-element.15) | copy-start | bytes 786436

commit v7 on v5

--- a/solution.py
+++ b/solution.py
@@ -152,9 +152,86 @@
     return nearby / jnp.sum(nearby, axis=0, keepdims=True)
 
 
-def whiten(decimated, slices, group):
-    rows = decimated.shape[0]
-    spectrum = dft(decimated)
+def fused_kernel(x_ref, t_ref, c1_ref, s1_ref, c2_ref, s2_ref, out_ref, carry_ref, dec_ref, tab_ref,
+                 *, dec_steps, halves):
+    i = pl.program_id(0)
+
+    @pl.when(i == 0)
+    def _():
+        carry_ref[...] = jnp.zeros_like(carry_ref)
+
+    @pl.when(i < dec_steps)
+    def _():
+        table = t_ref[...]
+        channels, windows, width = x_ref.shape
+        segment = table.shape[0]
+        block = table.shape[1] // 2
+        per_step = width // segment
+        for g in range(per_step):
+            x = x_ref[:, :, g * segment : (g + 1) * segment].reshape(channels * windows, segment)
+            both = jnp.dot(x, table, preferred_element_type=jnp.float32)
+            col = pl.multiple_of((i * per_step + g) * block, block)
+            dec_ref[:, pl.ds(col, block)] = (both[:, :block] + carry_ref[...]).astype(jnp.bfloat16)
+            carry_ref[...] = both[:, block:]
+
+    @pl.when(i >= dec_steps)
+    def _():
+        real = i - dec_steps < halves
+        c1 = c1_ref[...]
+        s1 = s1_ref[...]
+        p = jnp.where(real, c1, -s1)
+        q = jnp.where(real, -s1, -c1)
+        c2 = c2_ref[...]
+        s2 = s2_ref[...]
+        for hi in range(p.shape[0]):
+            value = p[hi : hi + 1, :] * c2 + q[hi : hi + 1, :] * s2
+            tab_ref[hi * LO : (hi + 1) * LO, :] = value.astype(jnp.bfloat16)
+        out_ref[...] = jnp.dot(dec_ref[...], tab_ref[...], preferred_element_type=jnp.float32)
+
+
+def decimate_dft(samples, filter_taps, chunk=8192, block_cols=512):
+    channels, windows, row_length = samples.shape
+    block_size = min(128, row_length // DECIM)
+    table = fir_table(filter_taps, block_size)
+    rows = channels * windows
+    points = row_length // DECIM
+    c1, s1, c2, s2 = dft_factors(points, NBINS)
+    hi_count = c1.shape[0]
+    halves = NBINS // block_cols
+    dec_steps = row_length // chunk
+
+    def raw_map(i):
+        return (0, 0, jnp.minimum(i, dec_steps - 1))
+
+    def factor_map(i):
+        return (0, jnp.maximum(i - dec_steps, 0) % halves)
+
+    def out_map(i):
+        return (0, jnp.maximum(i - dec_steps, 0))
+
+    return pl.pallas_call(
+        functools.partial(fused_kernel, dec_steps=dec_steps, halves=halves),
+        grid=(dec_steps + 2 * halves,),
+        in_specs=[
+            pl.BlockSpec((channels, windows, chunk), raw_map),
+            pl.BlockSpec(table.shape, lambda i: (0, 0)),
+            pl.BlockSpec((hi_count, block_cols), factor_map),
+            pl.BlockSpec((hi_count, block_cols), factor_map),
+            pl.BlockSpec((LO, block_cols), factor_map),
+            pl.BlockSpec((LO, block_cols), factor_map),
+        ],
+        out_specs=pl.BlockSpec((rows, block_cols), out_map),
+        out_shape=jax.ShapeDtypeStruct((rows, 2 * NBINS), jnp.float32),
+        scratch_shapes=[
+            pltpu.VMEM((rows, block_size), jnp.float32),
+            pltpu.VMEM((rows, points), jnp.bfloat16),
+            pltpu.VMEM((points, block_cols), jnp.bfloat16),
+        ],
+    )(samples, table, c1, s1, c2, s2)
+
+
+def whiten(spectrum, slices, group):
+    rows = spectrum.shape[0]
     real_part = spectrum[:, :NBINS]
     imag_part = spectrum[:, NBINS:]
     magnitude = jnp.sqrt(real_part * real_part + imag_part * imag_part)
@@ -175,8 +252,7 @@
     group = NBINS // devices
     rows = chan_dev * window_total
 
-    decimated = decimate(raw_samples, filter_taps)
-    whitened = whiten(decimated, devices, group)
+    whitened = whiten(decimate_dft(raw_samples, filter_taps), devices, group)
     spectra = lax.all_to_all(whitened, ("wide", "narrow"), 0, 0, tiled=True)
 
     source = jnp.take(spectra, tile_pairs[:, 0], axis=0)

time: 79 us -> 76.7 us (0.971)
  Pallas kernels: 14.2 us -> 11.9 us
    pallas_call x2 -> x1, Pallas kernels: 14.2 us -> 11.9 us  [decimate_dft(): pl.pallas_call(functools.partial(fused_kernel, dec_steps=dec_steps, halve...]
where the time goes in v7:
time: 76.7 us; the launch traced here: 76.5 us
  waiting for transfers between devices  26.8 us (35%)
  starting transfers between devices  15.4 us (20%)
  Pallas kernels  11.9 us (16%)
  local copies, waits for them, and re-layouts  11.4 us (15%)
  matrix products  6.46 us (8%)
  other arithmetic  4.32 us (6%)
    all_to_all x1, waiting for transfers between devices, on_device(): spectra = lax.all_to_all(whitened, ('wide', 'narrow'), 0, 0, tiled=True)  17.1 us
    pallas_call x1, Pallas kernels, decimate_dft(): pl.pallas_call(functools.partial(fused_kernel, dec_steps=dec_steps, halve...  11.9 us
    all_to_all x1, starting transfers between devices, on_device(): spectra = lax.all_to_all(whitened, ('wide', 'narrow'), 0, 0, tiled=True)  11.5 us
    all_to_all x1, waiting for transfers between devices, on_device(): arrived = lax.all_to_all(send, ('wide', 'narrow'), 0, 0, tiled=True)  9.65 us
    all_to_all x1, starting transfers between devices, on_device(): arrived = lax.all_to_all(send, ('wide', 'narrow'), 0, 0, tiled=True)  3.9 us
    dot_general x1, matrix products, whiten(): jnp.dot(magnitude, smoother(NBINS, SMOOTH), precision=lax.Precision.HIGH)  3.78 us
    cos x2, other arithmetic, trig(): return (jnp.cos(angle), jnp.sin(angle))  2.34 us
    all_to_all x2, local copies, waits for them, and re-layouts, on_device(): arrived = lax.all_to_all(send, ('wide', 'narrow'), 0, 0, tiled=True)  2.2 us
  transfers between devices with their start and end apart: 2, of which 2 were waited for; matrix products, arithmetic and copies ran while one was open for 3% of the time, Pallas kernels for 0%

profile of v7, /device:TPU:1, one launch (start us, length us, event | category | flops | bytes accessed | tf_op | source)
XLA Modules:
  0.0 76.5 jit_solution(10823586720390712269)
XLA Ops:
  0.2 0.7 convert_element_type.42
  1.2 0.8 tile.10
  2.1 0.8 reshape.190.t_ref
  2.8 11.9 %shard_map.82 = f32[256,2048]{1,0:T(8,128)} custom-call(bf16[8,32,16384]{2,1,0:T(8,128)(2,1)} %x_ref.1, bf16[512,256]{1,0:T(8,128)(2,1)} %reshape.190.t_ref, f32[32,1024]{1,0:T(8,128)} %constant.74.clone.c1_ref, f32[32,1024]{1,0:T(8,128)} %constant.75.clone.s1_ref, f32[128,1024]{1,0:T(8,128)} %constant.76.clone.c2_ref, f32[128,1024]{1,0:T(8,128)} %constant.77.clone.s2_ref), custom_call_target="tpu_custom_call" | custom-call | tf_op jit(solution)/shard_map/pallas_call | solution.py:212
  14.8 3.8 %fusion.40 = (f32[256]{0:T(256)S(1)}, f32[256,1024]{1,0:T(8,128)S(1)}) fusion(f32[1024]{0:T(1024)S(1)} %convert_reduce_fusion, f32[256,2048]{1,0:T(8,128)} %shard_map.82), kind=kOutput, calls=%fused_computation.84 | convolution fusion | flops 1616903936 | bytes 3150848 | tf_op jit(solution)/shard_map/dot_general | solution.py:238
  18.6 0.2 add_divide_fusion
  18.8 0.3 fusion.1
  19.2 0.5 copy.45
  19.7 1.1 %copy.69 = bf16[128,2,8,256]{3,2,1,0:T(8,128)(2,1)} copy(bf16[128,2,8,256]{3,2,0,1:T(8,128)(2,1)S(1)} %bitcast.72) | data formatting | bytes 2097152 | tf_op jit(solution)/shard_map/transpose | solution.py:242
  20.8 11.5 %all-to-all-start = ((bf16[128,16,256]{2,1,0:T(8,128)(2,1)}), bf16[128,16,256]{2,1,0:T(8,128)(2,1)S(1)}, u32[]{:S(2)}, u32[]{:S(2)}) async-start(bf16[128,16,256]{2,1,0:T(8,128)(2,1)} %bitcast.70), calls=%async_computation | async-start | bytes 2097152 | tf_op jit(solution)/shard_map/all_to_all | solution.py:256
  32.3 0.2 reduce_window_sum.11
  32.5 2.1 %fusion.23 = (f32[1024,64]{1,0:T(8,128)S(1)}, f32[1024,64]{1,0:T(8,128)S(1)}) fusion(s32[1024]{0:T(1024)S(1)} %iota_add_fusion), kind=kLoop, calls=%fused_computation.49 | loop fusion | flops 983040 | bytes 528384 | tf_op jit(solution)/shard_map/cos | solution.py:76
  34.7 17.1 %all-to-all-done = bf16[128,16,256]{2,1,0:T(8,128)(2,1)S(1)} async-done(((bf16[128,16,256]{2,1,0:T(8,128)(2,1)}), bf16[128,16,256]{2,1,0:T(8,128)(2,1)S(1)}, u32[]{:S(2)}, u32[]{:S(2)}) %all-to-all-start) | async-done | bytes 1048608 | tf_op jit(solution)/shard_map/all_to_all | solution.py:256
  51.8 0.6 gather_fusion
  52.3 0.6 gather_fusion.1
  53.0 0.2 reshape.193
  53.3 0.2 reshape.194
  53.5 0.3 fusion.25
  53.8 0.3 fusion.24
  54.1 0.3 fusion.5
  54.4 0.3 fusion.4
  54.7 0.7 copy.51
  55.5 0.3 copy.52
  55.8 0.4 convolution_bitcast_fusion
  56.1 1.5 %copy.53 = f32[32,4,8,2,16]{4,3,2,1,0:T(2,128)S(1)} copy(f32[32,4,8,2,16]{0,2,1,4,3:T(8,128)S(1)} %convolution_bitcast_fusion) | data formatting | bytes 262144 | tf_op jit(solution)/shard_map/nst,twqv->wnsqv/transpose | solution.py:283
  57.7 2.1 %all_to_all.12 = f32[128,1,256]{2,1,0:T(1,128)} reshape(f32[32,4,8,2,16]{4,3,2,1,0:T(2,128)S(1)} %copy.53) | data formatting | bytes 262144 | tf_op jit(solution)/shard_map/all_to_all | solution.py:285
  59.8 3.9 %all-to-all-start.1 = ((f32[128,1,256]{2,1,0:T(1,128)}), f32[128,1,256]{2,1,0:T(1,128)S(1)}, u32[]{:S(2)}, u32[]{:S(2)}) async-start(f32[128,1,256]{2,1,0:T(1,128)} %all_to_all.12), calls=%async_computation.1 | async-start | bytes 262144 | tf_op jit(solution)/shard_map/all_to_all | solution.py:285
  63.7 0.2 fusion.30
  63.9 9.7 %all-to-all-done.1 = f32[128,1,256]{2,1,0:T(1,128)S(1)} async-done(((f32[128,1,256]{2,1,0:T(1,128)}), f32[128,1,256]{2,1,0:T(1,128)S(1)}, u32[]{:S(2)}, u32[]{:S(2)}) %all-to-all-start.1) | async-done | bytes 131104 | tf_op jit(solution)/shard_map/all_to_all | solution.py:285
  73.6 0.4 copy.56
  74.6 1.2 %fusion.9 = f32[128,64]{1,0:T(8,128)S(1)} fusion(f32[128,1024]{1,0:T(8,128)S(1)} %get-tuple-element.13, f32[128,1024]{1,0:T(8,128)S(1)} %get-tuple-element.12, f32[1024,64]{1,0:T(8,128)S(1)} %get-tuple-element.17, f32[1024,64]{1,0:T(8,128)S(1)} %get-tuple-element.16), kind=kOutput, calls=%fused_computation.20 | convolution fusion | flops 201850880 | bytes 1605632 | tf_op jit(solution)/shard_map/dot_general | solution.py:143
  75.8 0.7 reshape_reshape.3
  (28 shorter events, 1.5 us)
Async XLA Ops:
  14.8 4.0 %copy-start = (f32[256,2048]{1,0:T(8,128)S(1)}, f32[256,2048]{1,0:T(8,128)}, u32[]{:S(2)}) copy-start(f32[256,2048]{1,0:T(8,128)} %shard_map.82) | copy-start | bytes 6291460
  19.1 13.1 %copy-start.2 = (s32[16]{0:T(128)S(1)}, s32[16]{0:T(128)}, u32[]{:S(2)}) copy-start(s32[16]{0:T(128)} %param.13) | copy-start | bytes 196
  19.2 13.3 %copy-start.1 = (s32[16,2]{0,1:T(2,128)S(1)}, s32[16,2]{0,1:T(2,128)}, u32[]{:S(2)}) copy-start(s32[16,2]{0,1:T(2,128)} %param.12) | copy-start | bytes 388
  20.8 31.0 %all-to-all-start = ((bf16[128,16,256]{2,1,0:T(8,128)(2,1)}), bf16[128,16,256]{2,1,0:T(8,128)(2,1)S(1)}, u32[]{:S(2)}, u32[]{:S(2)}) async-start(bf16[128,16,256]{2,1,0:T(8,128)(2,1)} %bitcast.70), calls=%async_computation | async-start | bytes 2097152 | tf_op jit(solution)/shard_map/all_to_all | solution.py:256
  59.8 13.8 %all-to-all-start.1 = ((f32[128,1,256]{2,1,0:T(1,128)}), f32[128,1,256]{2,1,0:T(1,128)S(1)}, u32[]{:S(2)}, u32[]{:S(2)}) async-start(f32[128,1,256]{2,1,0:T(1,128)} %all_to_all.12), calls=%async_computation.1 | async-start | bytes 262144 | tf_op jit(solution)/shard_map/all_to_all | solution.py:285

commit v8 on v7

--- a/solution.py
+++ b/solution.py
@@ -152,17 +152,28 @@
     return nearby / jnp.sum(nearby, axis=0, keepdims=True)
 
 
-def fused_kernel(x_ref, t_ref, c1_ref, s1_ref, c2_ref, s2_ref, out_ref, carry_ref, dec_ref, tab_ref,
-                 *, dec_steps, halves):
+def fused_kernel(taps_ref, x_ref, c1_ref, s1_ref, c2_ref, s2_ref, out_ref, carry_ref, fir_ref, dec_ref,
+                 tab_ref, *, dec_steps, halves):
     i = pl.program_id(0)
 
     @pl.when(i == 0)
     def _():
         carry_ref[...] = jnp.zeros_like(carry_ref)
+        shape = fir_ref.shape
+        row = lax.broadcasted_iota(jnp.int32, shape, 0)
+        phase = row % DECIM
+        offset = lax.broadcasted_iota(jnp.int32, shape, 1) - row // DECIM
+        table = jnp.zeros(shape, jnp.float32)
+        for m in range(taps_ref.shape[0] // DECIM):
+            value = jnp.full(shape, taps_ref[DECIM * m], jnp.float32)
+            for b in range(DECIM - 1):
+                value = jnp.where(phase == b, taps_ref[DECIM * m + DECIM - 1 - b], value)
+            table = jnp.where(offset == m, value, table)
+        fir_ref[...] = table.astype(jnp.bfloat16)
 
     @pl.when(i < dec_steps)
     def _():
-        table = t_ref[...]
+        table = fir_ref[...]
         channels, windows, width = x_ref.shape
         segment = table.shape[0]
         block = table.shape[1] // 2
@@ -192,7 +203,6 @@
 def decimate_dft(samples, filter_taps, chunk=8192, block_cols=512):
     channels, windows, row_length = samples.shape
     block_size = min(128, row_length // DECIM)
-    table = fir_table(filter_taps, block_size)
     rows = channels * windows
     points = row_length // DECIM
     c1, s1, c2, s2 = dft_factors(points, NBINS)
@@ -213,8 +223,8 @@
         functools.partial(fused_kernel, dec_steps=dec_steps, halves=halves),
         grid=(dec_steps + 2 * halves,),
         in_specs=[
+            pl.BlockSpec(memory_space=pltpu.SMEM),
             pl.BlockSpec((channels, windows, chunk), raw_map),
-            pl.BlockSpec(table.shape, lambda i: (0, 0)),
             pl.BlockSpec((hi_count, block_cols), factor_map),
             pl.BlockSpec((hi_count, block_cols), factor_map),
             pl.BlockSpec((LO, block_cols), factor_map),
@@ -224,10 +234,11 @@
         out_shape=jax.ShapeDtypeStruct((rows, 2 * NBINS), jnp.float32),
         scratch_shapes=[
             pltpu.VMEM((rows, block_size), jnp.float32),
+            pltpu.VMEM((DECIM * block_size, 2 * block_size), jnp.bfloat16),
             pltpu.VMEM((rows, points), jnp.bfloat16),
             pltpu.VMEM((points, block_cols), jnp.bfloat16),
         ],
-    )(samples, table, c1, s1, c2, s2)
+    )(filter_taps, samples, c1, s1, c2, s2)
 
 
 def whiten(spectrum, slices, group):

time: 76.7 us -> 74.9 us (0.977)
  local copies, waits for them, and re-layouts: 11.4 us -> 9.44 us
  Pallas kernels: 11.9 us -> 12.7 us
    reshape x2 -> x0, local copies, waits for them, and re-layouts: 0.85 us -> none  [the longest x1 0.76 us: fir_table(): return jnp.transpose(shifted, (1, 0, 2)).reshape(DECIM * block_size, cols)]
    another operation x2 -> x0, local copies, waits for them, and re-layouts: 0.81 us -> none  [fir_table(): shifted = jnp.tile(padded, (1, block_size))[:, :block_size * cols]]
    pallas_call x1, Pallas kernels: 11.9 us -> 12.7 us  [decimate_dft(): pl.pallas_call(functools.partial(fused_kernel, dec_steps=dec_steps, halve...]
where the time goes in v8:
time: 74.9 us; the launch traced here: 74.7 us
  waiting for transfers between devices  26.8 us (36%)
  starting transfers between devices  15.4 us (21%)
  Pallas kernels  12.7 us (17%)
  local copies, waits for them, and re-layouts  9.44 us (13%)
  matrix products  6.46 us (9%)
  other arithmetic  3.67 us (5%)
    all_to_all x1, waiting for transfers between devices, on_device(): spectra = lax.all_to_all(whitened, ('wide', 'narrow'), 0, 0, tiled=True)  17.1 us
    pallas_call x1, Pallas kernels, decimate_dft(): pl.pallas_call(functools.partial(fused_kernel, dec_steps=dec_steps, halve...  12.7 us
    all_to_all x1, starting transfers between devices, on_device(): spectra = lax.all_to_all(whitened, ('wide', 'narrow'), 0, 0, tiled=True)  11.5 us
    all_to_all x1, waiting for transfers between devices, on_device(): arrived = lax.all_to_all(send, ('wide', 'narrow'), 0, 0, tiled=True)  9.65 us
    all_to_all x1, starting transfers between devices, on_device(): arrived = lax.all_to_all(send, ('wide', 'narrow'), 0, 0, tiled=True)  3.9 us
    dot_general x1, matrix products, whiten(): jnp.dot(magnitude, smoother(NBINS, SMOOTH), precision=lax.Precision.HIGH)  3.78 us
    cos x2, other arithmetic, trig(): return (jnp.cos(angle), jnp.sin(angle))  2.34 us
    all_to_all x2, local copies, waits for them, and re-layouts, on_device(): arrived = lax.all_to_all(send, ('wide', 'narrow'), 0, 0, tiled=True)  2.2 us
  transfers between devices with their start and end apart: 2, of which 2 were waited for; matrix products, arithmetic and copies ran while one was open for 3% of the time, Pallas kernels for 0%

profile of v8, /device:TPU:1, one launch (start us, length us, event | category | flops | bytes accessed | tf_op | source)
XLA Modules:
  0.0 74.7 jit_solution(11132435742084835755)
XLA Ops:
  0.0 0.2 convert_reduce_fusion
  0.2 12.7 %shard_map.82 = f32[256,2048]{1,0:T(8,128)} custom-call(f32[64]{0:T(128)} %taps_ref.1, bf16[8,32,16384]{2,1,0:T(8,128)(2,1)} %x_ref.1, f32[32,1024]{1,0:T(8,128)} %constant.71.clone.c1_ref, f32[32,1024]{1,0:T(8,128)} %constant.72.clone.s1_ref, f32[128,1024]{1,0:T(8,128)} %constant.73.clone.c2_ref, f32[128,1024]{1,0:T(8,128)} %constant.74.clone.s2_ref), custom_call_target="tpu_custom_call" | custom-call | tf_op jit(solution)/shard_map/pallas_call | solution.py:222
  12.9 3.8 %fusion.40 = (f32[256]{0:T(256)S(1)}, f32[256,1024]{1,0:T(8,128)S(1)}) fusion(f32[1024]{0:T(1024)S(1)} %convert_reduce_fusion, f32[256,2048]{1,0:T(8,128)} %shard_map.82), kind=kOutput, calls=%fused_computation.84 | convolution fusion | flops 1616903936 | bytes 3150848 | tf_op jit(solution)/shard_map/dot_general | solution.py:249
  16.7 0.2 add_divide_fusion
  17.0 0.3 fusion.1
  17.3 0.5 copy.38
  17.9 1.1 %copy.61 = bf16[128,2,8,256]{3,2,1,0:T(8,128)(2,1)} copy(bf16[128,2,8,256]{3,2,0,1:T(8,128)(2,1)S(1)} %bitcast.68) | data formatting | bytes 2097152 | tf_op jit(solution)/shard_map/transpose | solution.py:253
  18.9 11.5 %all-to-all-start = ((bf16[128,16,256]{2,1,0:T(8,128)(2,1)}), bf16[128,16,256]{2,1,0:T(8,128)(2,1)S(1)}, u32[]{:S(2)}, u32[]{:S(2)}) async-start(bf16[128,16,256]{2,1,0:T(8,128)(2,1)} %bitcast.66), calls=%async_computation | async-start | bytes 2097152 | tf_op jit(solution)/shard_map/all_to_all | solution.py:267
  30.5 0.2 reduce_window_sum.11
  30.7 2.1 %fusion.23 = (f32[1024,64]{1,0:T(8,128)S(1)}, f32[1024,64]{1,0:T(8,128)S(1)}) fusion(s32[1024]{0:T(1024)S(1)} %iota_add_fusion), kind=kLoop, calls=%fused_computation.49 | loop fusion | flops 983040 | bytes 528384 | tf_op jit(solution)/shard_map/cos | solution.py:76
  32.8 17.1 %all-to-all-done = bf16[128,16,256]{2,1,0:T(8,128)(2,1)S(1)} async-done(((bf16[128,16,256]{2,1,0:T(8,128)(2,1)}), bf16[128,16,256]{2,1,0:T(8,128)(2,1)S(1)}, u32[]{:S(2)}, u32[]{:S(2)}) %all-to-all-start) | async-done | bytes 1048608 | tf_op jit(solution)/shard_map/all_to_all | solution.py:267
  49.9 0.6 gather_fusion
  50.5 0.6 gather_fusion.1
  51.2 0.2 reshape.177
  51.4 0.2 reshape.178
  51.7 0.3 fusion.25
  51.9 0.3 fusion.24
  52.2 0.3 fusion.5
  52.5 0.3 fusion.4
  52.9 0.7 copy.44
  53.6 0.3 copy.45
  53.9 0.4 convolution_bitcast_fusion
  54.3 1.5 %copy.46 = f32[32,4,8,2,16]{4,3,2,1,0:T(2,128)S(1)} copy(f32[32,4,8,2,16]{0,2,1,4,3:T(8,128)S(1)} %convolution_bitcast_fusion) | data formatting | bytes 262144 | tf_op jit(solution)/shard_map/nst,twqv->wnsqv/transpose | solution.py:294
  55.8 2.1 %all_to_all.12 = f32[128,1,256]{2,1,0:T(1,128)} reshape(f32[32,4,8,2,16]{4,3,2,1,0:T(2,128)S(1)} %copy.46) | data formatting | bytes 262144 | tf_op jit(solution)/shard_map/all_to_all | solution.py:296
  57.9 3.9 %all-to-all-start.1 = ((f32[128,1,256]{2,1,0:T(1,128)}), f32[128,1,256]{2,1,0:T(1,128)S(1)}, u32[]{:S(2)}, u32[]{:S(2)}) async-start(f32[128,1,256]{2,1,0:T(1,128)} %all_to_all.12), calls=%async_computation.1 | async-start | bytes 262144 | tf_op jit(solution)/shard_map/all_to_all | solution.py:296
  61.8 0.2 fusion.30
  62.1 9.7 %all-to-all-done.1 = f32[128,1,256]{2,1,0:T(1,128)S(1)} async-done(((f32[128,1,256]{2,1,0:T(1,128)}), f32[128,1,256]{2,1,0:T(1,128)S(1)}, u32[]{:S(2)}, u32[]{:S(2)}) %all-to-all-start.1) | async-done | bytes 131104 | tf_op jit(solution)/shard_map/all_to_all | solution.py:296
  71.8 0.4 copy.49
  72.3 0.2 copy.50
  72.5 0.2 copy.51
  72.8 1.2 %fusion.9 = f32[128,64]{1,0:T(8,128)S(1)} fusion(f32[128,1024]{1,0:T(8,128)S(1)} %get-tuple-element.13, f32[128,1024]{1,0:T(8,128)S(1)} %get-tuple-element.12, f32[1024,64]{1,0:T(8,128)S(1)} %get-tuple-element.17, f32[1024,64]{1,0:T(8,128)S(1)} %get-tuple-element.16), kind=kOutput, calls=%fused_computation.20 | convolution fusion | flops 201850880 | bytes 1605632 | tf_op jit(solution)/shard_map/dot_general | solution.py:143
  74.0 0.7 reshape_reshape.3
  (19 shorter events, 0.6 us)
Async XLA Ops:
  12.9 4.0 %copy-start = (f32[256,2048]{1,0:T(8,128)S(1)}, f32[256,2048]{1,0:T(8,128)}, u32[]{:S(2)}) copy-start(f32[256,2048]{1,0:T(8,128)} %shard_map.82) | copy-start | bytes 6291460
  17.3 13.1 %copy-start.2 = (s32[16]{0:T(128)S(1)}, s32[16]{0:T(128)}, u32[]{:S(2)}) copy-start(s32[16]{0:T(128)} %param.13) | copy-start | bytes 196
  17.3 13.3 %copy-start.1 = (s32[16,2]{0,1:T(2,128)S(1)}, s32[16,2]{0,1:T(2,128)}, u32[]{:S(2)}) copy-start(s32[16,2]{0,1:T(2,128)} %param.12) | copy-start | bytes 388
  18.9 31.0 %all-to-all-start = ((bf16[128,16,256]{2,1,0:T(8,128)(2,1)}), bf16[128,16,256]{2,1,0:T(8,128)(2,1)S(1)}, u32[]{:S(2)}, u32[]{:S(2)}) async-start(bf16[128,16,256]{2,1,0:T(8,128)(2,1)} %bitcast.66), calls=%async_computation | async-start | bytes 2097152 | tf_op jit(solution)/shard_map/all_to_all | solution.py:267
  57.9 13.8 %all-to-all-start.1 = ((f32[128,1,256]{2,1,0:T(1,128)}), f32[128,1,256]{2,1,0:T(1,128)S(1)}, u32[]{:S(2)}, u32[]{:S(2)}) async-start(f32[128,1,256]{2,1,0:T(1,128)} %all_to_all.12), calls=%async_computation.1 | async-start | bytes 262144 | tf_op jit(solution)/shard_map/all_to_all | solution.py:296

commit v9 on v8

--- a/solution.py
+++ b/solution.py
@@ -142,6 +142,13 @@
     table = jnp.concatenate([cb, -sb], axis=0) * weight
     out = jnp.dot(uv, table, precision=lax.Precision.HIGHEST)
     return out.reshape(pairs, lag_count)
+
+
+def window_sums(bin_count, span_width):
+    bin_index = jnp.arange(bin_count, dtype=jnp.int32)
+    nearby = jnp.abs(bin_index[:, None] - bin_index[None, :]) <= (span_width - 1) // 2
+    count = jnp.sum(nearby.astype(jnp.float32), axis=0, keepdims=True)
+    return nearby.astype(jnp.bfloat16), count
 
 
 def smoother(bin_count, span_width):
@@ -246,7 +253,13 @@
     real_part = spectrum[:, :NBINS]
     imag_part = spectrum[:, NBINS:]
     magnitude = jnp.sqrt(real_part * real_part + imag_part * imag_part)
-    smooth = jnp.dot(magnitude, smoother(NBINS, SMOOTH), precision=lax.Precision.HIGH)
+    nearby, count = window_sums(NBINS, SMOOTH)
+    mag_hi = magnitude.astype(jnp.bfloat16)
+    mag_lo = (magnitude - mag_hi.astype(jnp.float32)).astype(jnp.bfloat16)
+    summed = jnp.dot(mag_hi, nearby, preferred_element_type=jnp.float32) + jnp.dot(
+        mag_lo, nearby, preferred_element_type=jnp.float32
+    )
+    smooth = summed / count
     floor_level = water_level * jnp.mean(smooth, axis=1, keepdims=True) + epsilon
     factor = 1.0 / (smooth + floor_level)
     whitened = (spectrum * jnp.concatenate([factor, factor], axis=1)).astype(jnp.bfloat16)

time: 74.9 us -> 74.7 us (level)
    dot_general x1 -> x2, matrix products: 3.78 us -> 3.6 us  [the longest x1 2.61 us: whiten(): jnp.dot(mag_lo, nearby, preferred_element_type=jnp.float32)]
where the time goes in v9:
time: 74.7 us; the launch traced here: 74.5 us
  waiting for transfers between devices  26.8 us (36%)
  starting transfers between devices  15.4 us (21%)
  Pallas kernels  12.7 us (17%)
  local copies, waits for them, and re-layouts  9.44 us (13%)
  matrix products  6.28 us (8%)
  other arithmetic  3.67 us (5%)
    all_to_all x1, waiting for transfers between devices, on_device(): spectra = lax.all_to_all(whitened, ('wide', 'narrow'), 0, 0, tiled=True)  17.1 us
    pallas_call x1, Pallas kernels, decimate_dft(): pl.pallas_call(functools.partial(fused_kernel, dec_steps=dec_steps, halve...  12.7 us
    all_to_all x1, starting transfers between devices, on_device(): spectra = lax.all_to_all(whitened, ('wide', 'narrow'), 0, 0, tiled=True)  11.5 us
    all_to_all x1, waiting for transfers between devices, on_device(): arrived = lax.all_to_all(send, ('wide', 'narrow'), 0, 0, tiled=True)  9.65 us
    all_to_all x1, starting transfers between devices, on_device(): arrived = lax.all_to_all(send, ('wide', 'narrow'), 0, 0, tiled=True)  3.9 us
    dot_general x1, matrix products, whiten(): jnp.dot(mag_lo, nearby, preferred_element_type=jnp.float32)  2.61 us
    cos x2, other arithmetic, trig(): return (jnp.cos(angle), jnp.sin(angle))  2.34 us
    all_to_all x2, local copies, waits for them, and re-layouts, on_device(): arrived = lax.all_to_all(send, ('wide', 'narrow'), 0, 0, tiled=True)  2.2 us
  transfers between devices with their start and end apart: 2, of which 2 were waited for; matrix products, arithmetic and copies ran while one was open for 3% of the time, Pallas kernels for 0%

profile of v9, /device:TPU:1, one launch (start us, length us, event | category | flops | bytes accessed | tf_op | source)
XLA Modules:
  0.0 74.5 jit_solution(16232006171825920130)
XLA Ops:
  0.0 0.2 convert_reduce_fusion
  0.2 12.7 %shard_map.82 = f32[256,2048]{1,0:T(8,128)} custom-call(f32[64]{0:T(128)} %taps_ref.1, bf16[8,32,16384]{2,1,0:T(8,128)(2,1)} %x_ref.1, f32[32,1024]{1,0:T(8,128)} %constant.71.clone.c1_ref, f32[32,1024]{1,0:T(8,128)} %constant.72.clone.s1_ref, f32[128,1024]{1,0:T(8,128)} %constant.73.clone.c2_ref, f32[128,1024]{1,0:T(8,128)} %constant.74.clone.s2_ref), custom_call_target="tpu_custom_call" | custom-call | tf_op jit(solution)/shard_map/pallas_call | solution.py:229
  12.9 2.6 %fusion = f32[256,1024]{1,0:T(8,128)S(1)} fusion(f32[256,2048]{1,0:T(8,128)} %shard_map.82), kind=kOutput, calls=%fused_computation.4 | convolution fusion | flops 541851648 | bytes 3145728 | tf_op jit(solution)/shard_map/dot_general | solution.py:259
  15.6 1.0 %fusion.47 = (f32[256]{0:T(256)S(1)}, f32[256,1024]{1,0:T(8,128)S(1)}) fusion(f32[1024]{0:T(1024)S(1)} %convert_reduce_fusion, f32[256,1024]{1,0:T(8,128)S(1)} %fusion, f32[256,2048]{1,0:T(8,128)S(1)} %copy-done), kind=kOutput, calls=%fused_computation.90 | convolution fusion | flops 541851392 | bytes 4199424 | tf_op jit(solution)/shard_map/dot_general | solution.py:259
  16.5 0.2 add_divide_fusion
  16.8 0.3 fusion.2
  17.2 0.5 copy.38
  17.7 1.1 %copy.61 = bf16[128,2,8,256]{3,2,1,0:T(8,128)(2,1)} copy(bf16[128,2,8,256]{3,2,0,1:T(8,128)(2,1)S(1)} %bitcast.68) | data formatting | bytes 2097152 | tf_op jit(solution)/shard_map/transpose | solution.py:266
  18.7 11.5 %all-to-all-start = ((bf16[128,16,256]{2,1,0:T(8,128)(2,1)}), bf16[128,16,256]{2,1,0:T(8,128)(2,1)S(1)}, u32[]{:S(2)}, u32[]{:S(2)}) async-start(bf16[128,16,256]{2,1,0:T(8,128)(2,1)} %bitcast.66), calls=%async_computation | async-start | bytes 2097152 | tf_op jit(solution)/shard_map/all_to_all | solution.py:280
  30.3 0.2 reduce_window_sum.11
  30.5 2.1 %fusion.25 = (f32[1024,64]{1,0:T(8,128)S(1)}, f32[1024,64]{1,0:T(8,128)S(1)}) fusion(s32[1024]{0:T(1024)S(1)} %iota_add_fusion), kind=kLoop, calls=%fused_computation.52 | loop fusion | flops 983040 | bytes 528384 | tf_op jit(solution)/shard_map/cos | solution.py:76
  32.7 17.1 %all-to-all-done = bf16[128,16,256]{2,1,0:T(8,128)(2,1)S(1)} async-done(((bf16[128,16,256]{2,1,0:T(8,128)(2,1)}), bf16[128,16,256]{2,1,0:T(8,128)(2,1)S(1)}, u32[]{:S(2)}, u32[]{:S(2)}) %all-to-all-start) | async-done | bytes 1048608 | tf_op jit(solution)/shard_map/all_to_all | solution.py:280
  49.8 0.6 gather_fusion
  50.3 0.6 gather_fusion.1
  51.0 0.2 reshape.177
  51.2 0.2 reshape.178
  51.5 0.3 fusion.29
  51.8 0.3 fusion.28
  52.1 0.3 fusion.7
  52.3 0.3 fusion.6
  52.7 0.7 copy.44
  53.4 0.3 copy.45
  53.8 0.4 convolution_bitcast_fusion
  54.1 1.5 %copy.46 = f32[32,4,8,2,16]{4,3,2,1,0:T(2,128)S(1)} copy(f32[32,4,8,2,16]{0,2,1,4,3:T(8,128)S(1)} %convolution_bitcast_fusion) | data formatting | bytes 262144 | tf_op jit(solution)/shard_map/nst,twqv->wnsqv/transpose | solution.py:307
  55.6 2.1 %all_to_all.12 = f32[128,1,256]{2,1,0:T(1,128)} reshape(f32[32,4,8,2,16]{4,3,2,1,0:T(2,128)S(1)} %copy.46) | data formatting | bytes 262144 | tf_op jit(solution)/shard_map/all_to_all | solution.py:309
  57.8 3.9 %all-to-all-start.1 = ((f32[128,1,256]{2,1,0:T(1,128)}), f32[128,1,256]{2,1,0:T(1,128)S(1)}, u32[]{:S(2)}, u32[]{:S(2)}) async-start(f32[128,1,256]{2,1,0:T(1,128)} %all_to_all.12), calls=%async_computation.1 | async-start | bytes 262144 | tf_op jit(solution)/shard_map/all_to_all | solution.py:309
  61.7 0.2 fusion.36
  61.9 9.7 %all-to-all-done.1 = f32[128,1,256]{2,1,0:T(1,128)S(1)} async-done(((f32[128,1,256]{2,1,0:T(1,128)}), f32[128,1,256]{2,1,0:T(1,128)S(1)}, u32[]{:S(2)}, u32[]{:S(2)}) %all-to-all-start.1) | async-done | bytes 131104 | tf_op jit(solution)/shard_map/all_to_all | solution.py:309
  71.6 0.4 copy.49
  72.3 0.2 copy.51
  72.6 1.2 %fusion.10 = f32[128,64]{1,0:T(8,128)S(1)} fusion(f32[128,1024]{1,0:T(8,128)S(1)} %get-tuple-element.13, f32[128,1024]{1,0:T(8,128)S(1)} %get-tuple-element.12, f32[1024,64]{1,0:T(8,128)S(1)} %get-tuple-element.17, f32[1024,64]{1,0:T(8,128)S(1)} %get-tuple-element.16), kind=kOutput, calls=%fused_computation.21 | convolution fusion | flops 201850880 | bytes 1605632 | tf_op jit(solution)/shard_map/dot_general | solution.py:143
  73.8 0.7 reshape_reshape.3
  (20 shorter events, 0.7 us)
Async XLA Ops:
  12.9 2.6 %copy-start = (f32[256,2048]{1,0:T(8,128)S(1)}, f32[256,2048]{1,0:T(8,128)}, u32[]{:S(2)}) copy-start(f32[256,2048]{1,0:T(8,128)} %shard_map.82) | copy-start | bytes 6291460
  17.1 13.1 %copy-start.2 = (s32[16]{0:T(128)S(1)}, s32[16]{0:T(128)}, u32[]{:S(2)}) copy-start(s32[16]{0:T(128)} %param.13) | copy-start | bytes 196
  17.1 13.3 %copy-start.1 = (s32[16,2]{0,1:T(2,128)S(1)}, s32[16,2]{0,1:T(2,128)}, u32[]{:S(2)}) copy-start(s32[16,2]{0,1:T(2,128)} %param.12) | copy-start | bytes 388
  18.7 31.0 %all-to-all-start = ((bf16[128,16,256]{2,1,0:T(8,128)(2,1)}), bf16[128,16,256]{2,1,0:T(8,128)(2,1)S(1)}, u32[]{:S(2)}, u32[]{:S(2)}) async-start(bf16[128,16,256]{2,1,0:T(8,128)(2,1)} %bitcast.66), calls=%async_computation | async-start | bytes 2097152 | tf_op jit(solution)/shard_map/all_to_all | solution.py:280
  57.8 13.8 %all-to-all-start.1 = ((f32[128,1,256]{2,1,0:T(1,128)}), f32[128,1,256]{2,1,0:T(1,128)S(1)}, u32[]{:S(2)}, u32[]{:S(2)}) async-start(f32[128,1,256]{2,1,0:T(1,128)} %all_to_all.12), calls=%async_computation.1 | async-start | bytes 262144 | tf_op jit(solution)/shard_map/all_to_all | solution.py:309

commit v10 on v8

--- a/solution.py
+++ b/solution.py
@@ -153,7 +153,7 @@
 
 
 def fused_kernel(taps_ref, x_ref, c1_ref, s1_ref, c2_ref, s2_ref, out_ref, carry_ref, fir_ref, dec_ref,
-                 tab_ref, *, dec_steps, halves):
+                 tab_ref, *, dec_steps, halves, sub_cols):
     i = pl.program_id(0)
 
     @pl.when(i == 0)
@@ -188,16 +188,20 @@
     @pl.when(i >= dec_steps)
     def _():
         real = i - dec_steps < halves
-        c1 = c1_ref[...]
-        s1 = s1_ref[...]
-        p = jnp.where(real, c1, -s1)
-        q = jnp.where(real, -s1, -c1)
-        c2 = c2_ref[...]
-        s2 = s2_ref[...]
-        for hi in range(p.shape[0]):
-            value = p[hi : hi + 1, :] * c2 + q[hi : hi + 1, :] * s2
-            tab_ref[hi * LO : (hi + 1) * LO, :] = value.astype(jnp.bfloat16)
-        out_ref[...] = jnp.dot(dec_ref[...], tab_ref[...], preferred_element_type=jnp.float32)
+        for start in range(0, tab_ref.shape[1], sub_cols):
+            cols = slice(start, start + sub_cols)
+            c1 = c1_ref[:, cols]
+            s1 = s1_ref[:, cols]
+            p = jnp.where(real, c1, -s1)
+            q = jnp.where(real, -s1, -c1)
+            c2 = c2_ref[:, cols]
+            s2 = s2_ref[:, cols]
+            for hi in range(p.shape[0]):
+                value = p[hi : hi + 1, :] * c2 + q[hi : hi + 1, :] * s2
+                tab_ref[hi * LO : (hi + 1) * LO, cols] = value.astype(jnp.bfloat16)
+            out_ref[:, cols] = jnp.dot(
+                dec_ref[...], tab_ref[:, cols], preferred_element_type=jnp.float32
+            )
 
 
 def decimate_dft(samples, filter_taps, chunk=8192, block_cols=512):
@@ -220,7 +224,7 @@
         return (0, jnp.maximum(i - dec_steps, 0))
 
     return pl.pallas_call(
-        functools.partial(fused_kernel, dec_steps=dec_steps, halves=halves),
+        functools.partial(fused_kernel, dec_steps=dec_steps, halves=halves, sub_cols=256),
         grid=(dec_steps + 2 * halves,),
         in_specs=[
             pl.BlockSpec(memory_space=pltpu.SMEM),

time: 74.9 us -> 74.9 us (level)
  no operation moved by 1% of the time
where the time goes in v10:
time: 74.9 us; the launch traced here: 74.7 us
  waiting for transfers between devices  26.8 us (36%)
  starting transfers between devices  15.4 us (21%)
  Pallas kernels  12.7 us (17%)
  local copies, waits for them, and re-layouts  9.44 us (13%)
  matrix products  6.46 us (9%)
  other arithmetic  3.67 us (5%)
    all_to_all x1, waiting for transfers between devices, on_device(): spectra = lax.all_to_all(whitened, ('wide', 'narrow'), 0, 0, tiled=True)  17.1 us
    pallas_call x1, Pallas kernels, decimate_dft(): pl.pallas_call(functools.partial(fused_kernel, dec_steps=dec_steps, halve...  12.7 us
    all_to_all x1, starting transfers between devices, on_device(): spectra = lax.all_to_all(whitened, ('wide', 'narrow'), 0, 0, tiled=True)  11.5 us
    all_to_all x1, waiting for transfers between devices, on_device(): arrived = lax.all_to_all(send, ('wide', 'narrow'), 0, 0, tiled=True)  9.65 us
    all_to_all x1, starting transfers between devices, on_device(): arrived = lax.all_to_all(send, ('wide', 'narrow'), 0, 0, tiled=True)  3.9 us
    dot_general x1, matrix products, whiten(): jnp.dot(magnitude, smoother(NBINS, SMOOTH), precision=lax.Precision.HIGH)  3.78 us
    cos x2, other arithmetic, trig(): return (jnp.cos(angle), jnp.sin(angle))  2.34 us
    all_to_all x2, local copies, waits for them, and re-layouts, on_device(): arrived = lax.all_to_all(send, ('wide', 'narrow'), 0, 0, tiled=True)  2.2 us
  transfers between devices with their start and end apart: 2, of which 2 were waited for; matrix products, arithmetic and copies ran while one was open for 3% of the time, Pallas kernels for 0%

profile of v10, /device:TPU:1, one launch (start us, length us, event | category | flops | bytes accessed | tf_op | source)
XLA Modules:
  0.0 74.7 jit_solution(11132435742084835755)
XLA Ops:
  0.0 0.2 convert_reduce_fusion
  0.2 12.7 %shard_map.82 = f32[256,2048]{1,0:T(8,128)} custom-call(f32[64]{0:T(128)} %taps_ref.1, bf16[8,32,16384]{2,1,0:T(8,128)(2,1)} %x_ref.1, f32[32,1024]{1,0:T(8,128)} %constant.71.clone.c1_ref, f32[32,1024]{1,0:T(8,128)} %constant.72.clone.s1_ref, f32[128,1024]{1,0:T(8,128)} %constant.73.clone.c2_ref, f32[128,1024]{1,0:T(8,128)} %constant.74.clone.s2_ref), custom_call_target="tpu_custom_call" | custom-call | tf_op jit(solution)/shard_map/pallas_call | solution.py:226
  12.9 3.8 %fusion.40 = (f32[256]{0:T(256)S(1)}, f32[256,1024]{1,0:T(8,128)S(1)}) fusion(f32[1024]{0:T(1024)S(1)} %convert_reduce_fusion, f32[256,2048]{1,0:T(8,128)} %shard_map.82), kind=kOutput, calls=%fused_computation.84 | convolution fusion | flops 1616903936 | bytes 3150848 | tf_op jit(solution)/shard_map/dot_general | solution.py:253
  16.7 0.2 add_divide_fusion
  17.0 0.3 fusion.1
  17.3 0.5 copy.38
  17.9 1.1 %copy.61 = bf16[128,2,8,256]{3,2,1,0:T(8,128)(2,1)} copy(bf16[128,2,8,256]{3,2,0,1:T(8,128)(2,1)S(1)} %bitcast.68) | data formatting | bytes 2097152 | tf_op jit(solution)/shard_map/transpose | solution.py:257
  18.9 11.5 %all-to-all-start = ((bf16[128,16,256]{2,1,0:T(8,128)(2,1)}), bf16[128,16,256]{2,1,0:T(8,128)(2,1)S(1)}, u32[]{:S(2)}, u32[]{:S(2)}) async-start(bf16[128,16,256]{2,1,0:T(8,128)(2,1)} %bitcast.66), calls=%async_computation | async-start | bytes 2097152 | tf_op jit(solution)/shard_map/all_to_all | solution.py:271
  30.5 0.2 reduce_window_sum.11
  30.7 2.1 %fusion.23 = (f32[1024,64]{1,0:T(8,128)S(1)}, f32[1024,64]{1,0:T(8,128)S(1)}) fusion(s32[1024]{0:T(1024)S(1)} %iota_add_fusion), kind=kLoop, calls=%fused_computation.49 | loop fusion | flops 983040 | bytes 528384 | tf_op jit(solution)/shard_map/cos | solution.py:76
  32.8 17.1 %all-to-all-done = bf16[128,16,256]{2,1,0:T(8,128)(2,1)S(1)} async-done(((bf16[128,16,256]{2,1,0:T(8,128)(2,1)}), bf16[128,16,256]{2,1,0:T(8,128)(2,1)S(1)}, u32[]{:S(2)}, u32[]{:S(2)}) %all-to-all-start) | async-done | bytes 1048608 | tf_op jit(solution)/shard_map/all_to_all | solution.py:271
  49.9 0.6 gather_fusion
  50.5 0.6 gather_fusion.1
  51.2 0.2 reshape.177
  51.4 0.2 reshape.178
  51.7 0.3 fusion.25
  51.9 0.3 fusion.24
  52.2 0.3 fusion.5
  52.5 0.3 fusion.4
  52.9 0.7 copy.44
  53.6 0.3 copy.45
  53.9 0.4 convolution_bitcast_fusion
  54.3 1.5 %copy.46 = f32[32,4,8,2,16]{4,3,2,1,0:T(2,128)S(1)} copy(f32[32,4,8,2,16]{0,2,1,4,3:T(8,128)S(1)} %convolution_bitcast_fusion) | data formatting | bytes 262144 | tf_op jit(solution)/shard_map/nst,twqv->wnsqv/transpose | solution.py:298
  55.8 2.1 %all_to_all.12 = f32[128,1,256]{2,1,0:T(1,128)} reshape(f32[32,4,8,2,16]{4,3,2,1,0:T(2,128)S(1)} %copy.46) | data formatting | bytes 262144 | tf_op jit(solution)/shard_map/all_to_all | solution.py:300
  57.9 3.9 %all-to-all-start.1 = ((f32[128,1,256]{2,1,0:T(1,128)}), f32[128,1,256]{2,1,0:T(1,128)S(1)}, u32[]{:S(2)}, u32[]{:S(2)}) async-start(f32[128,1,256]{2,1,0:T(1,128)} %all_to_all.12), calls=%async_computation.1 | async-start | bytes 262144 | tf_op jit(solution)/shard_map/all_to_all | solution.py:300
  61.8 0.2 fusion.30
  62.1 9.7 %all-to-all-done.1 = f32[128,1,256]{2,1,0:T(1,128)S(1)} async-done(((f32[128,1,256]{2,1,0:T(1,128)}), f32[128,1,256]{2,1,0:T(1,128)S(1)}, u32[]{:S(2)}, u32[]{:S(2)}) %all-to-all-start.1) | async-done | bytes 131104 | tf_op jit(solution)/shard_map/all_to_all | solution.py:300
  71.8 0.4 copy.49
  72.3 0.2 copy.50
  72.5 0.2 copy.51
  72.8 1.2 %fusion.9 = f32[128,64]{1,0:T(8,128)S(1)} fusion(f32[128,1024]{1,0:T(8,128)S(1)} %get-tuple-element.13, f32[128,1024]{1,0:T(8,128)S(1)} %get-tuple-element.12, f32[1024,64]{1,0:T(8,128)S(1)} %get-tuple-element.17, f32[1024,64]{1,0:T(8,128)S(1)} %get-tuple-element.16), kind=kOutput, calls=%fused_computation.20 | convolution fusion | flops 201850880 | bytes 1605632 | tf_op jit(solution)/shard_map/dot_general | solution.py:143
  74.0 0.7 reshape_reshape.3
  (19 shorter events, 0.6 us)
Async XLA Ops:
  12.9 4.0 %copy-start = (f32[256,2048]{1,0:T(8,128)S(1)}, f32[256,2048]{1,0:T(8,128)}, u32[]{:S(2)}) copy-start(f32[256,2048]{1,0:T(8,128)} %shard_map.82) | copy-start | bytes 6291460
  17.3 13.1 %copy-start.2 = (s32[16]{0:T(128)S(1)}, s32[16]{0:T(128)}, u32[]{:S(2)}) copy-start(s32[16]{0:T(128)} %param.13) | copy-start | bytes 196
  17.3 13.3 %copy-start.1 = (s32[16,2]{0,1:T(2,128)S(1)}, s32[16,2]{0,1:T(2,128)}, u32[]{:S(2)}) copy-start(s32[16,2]{0,1:T(2,128)} %param.12) | copy-start | bytes 388
  18.9 31.0 %all-to-all-start = ((bf16[128,16,256]{2,1,0:T(8,128)(2,1)}), bf16[128,16,256]{2,1,0:T(8,128)(2,1)S(1)}, u32[]{:S(2)}, u32[]{:S(2)}) async-start(bf16[128,16,256]{2,1,0:T(8,128)(2,1)} %bitcast.66), calls=%async_computation | async-start | bytes 2097152 | tf_op jit(solution)/shard_map/all_to_all | solution.py:271
  57.9 13.8 %all-to-all-start.1 = ((f32[128,1,256]{2,1,0:T(1,128)}), f32[128,1,256]{2,1,0:T(1,128)S(1)}, u32[]{:S(2)}, u32[]{:S(2)}) async-start(f32[128,1,256]{2,1,0:T(1,128)} %all_to_all.12), calls=%async_computation.1 | async-start | bytes 262144 | tf_op jit(solution)/shard_map/all_to_all | solution.py:300

commit v11 on v10

--- a/solution.py
+++ b/solution.py
@@ -204,7 +204,7 @@
             )
 
 
-def decimate_dft(samples, filter_taps, chunk=8192, block_cols=512):
+def decimate_dft(samples, filter_taps, chunk=8192, block_cols=1024):
     channels, windows, row_length = samples.shape
     block_size = min(128, row_length // DECIM)
     rows = channels * windows

time: 74.9 us -> 74.6 us (level)
  no operation moved by 1% of the time
where the time goes in v11:
time: 74.6 us; the launch traced here: 74.4 us
  waiting for transfers between devices  26.8 us (36%)
  starting transfers between devices  15.4 us (21%)
  Pallas kernels  12.5 us (17%)
  local copies, waits for them, and re-layouts  9.44 us (13%)
  matrix products  6.46 us (9%)
  other arithmetic  3.67 us (5%)
    all_to_all x1, waiting for transfers between devices, on_device(): spectra = lax.all_to_all(whitened, ('wide', 'narrow'), 0, 0, tiled=True)  17.1 us
    pallas_call x1, Pallas kernels, decimate_dft(): pl.pallas_call(functools.partial(fused_kernel, dec_steps=dec_steps, halve...  12.5 us
    all_to_all x1, starting transfers between devices, on_device(): spectra = lax.all_to_all(whitened, ('wide', 'narrow'), 0, 0, tiled=True)  11.5 us
    all_to_all x1, waiting for transfers between devices, on_device(): arrived = lax.all_to_all(send, ('wide', 'narrow'), 0, 0, tiled=True)  9.65 us
    all_to_all x1, starting transfers between devices, on_device(): arrived = lax.all_to_all(send, ('wide', 'narrow'), 0, 0, tiled=True)  3.91 us
    dot_general x1, matrix products, whiten(): jnp.dot(magnitude, smoother(NBINS, SMOOTH), precision=lax.Precision.HIGH)  3.78 us
    cos x2, other arithmetic, trig(): return (jnp.cos(angle), jnp.sin(angle))  2.34 us
    all_to_all x2, local copies, waits for them, and re-layouts, on_device(): arrived = lax.all_to_all(send, ('wide', 'narrow'), 0, 0, tiled=True)  2.2 us
  transfers between devices with their start and end apart: 2, of which 2 were waited for; matrix products, arithmetic and copies ran while one was open for 3% of the time, Pallas kernels for 0%

profile of v11, /device:TPU:1, one launch (start us, length us, event | category | flops | bytes accessed | tf_op | source)
XLA Modules:
  0.0 74.4 jit_solution(5833956566636571531)
XLA Ops:
  0.0 0.2 convert_reduce_fusion
  0.2 12.5 %shard_map.82 = f32[256,2048]{1,0:T(8,128)} custom-call(f32[64]{0:T(128)} %taps_ref.1, bf16[8,32,16384]{2,1,0:T(8,128)(2,1)} %x_ref.1, f32[32,1024]{1,0:T(8,128)} %constant.71.clone.c1_ref, f32[32,1024]{1,0:T(8,128)} %constant.72.clone.s1_ref, f32[128,1024]{1,0:T(8,128)} %constant.73.clone.c2_ref, f32[128,1024]{1,0:T(8,128)} %constant.74.clone.s2_ref), custom_call_target="tpu_custom_call" | custom-call | tf_op jit(solution)/shard_map/pallas_call | solution.py:226
  12.6 3.8 %fusion.40 = (f32[256]{0:T(256)S(1)}, f32[256,1024]{1,0:T(8,128)S(1)}) fusion(f32[1024]{0:T(1024)S(1)} %convert_reduce_fusion, f32[256,2048]{1,0:T(8,128)} %shard_map.82), kind=kOutput, calls=%fused_computation.84 | convolution fusion | flops 1616903936 | bytes 3150848 | tf_op jit(solution)/shard_map/dot_general | solution.py:253
  16.4 0.2 add_divide_fusion
  16.7 0.3 fusion.1
  17.1 0.5 copy.38
  17.6 1.1 %copy.61 = bf16[128,2,8,256]{3,2,1,0:T(8,128)(2,1)} copy(bf16[128,2,8,256]{3,2,0,1:T(8,128)(2,1)S(1)} %bitcast.68) | data formatting | bytes 2097152 | tf_op jit(solution)/shard_map/transpose | solution.py:257
  18.6 11.5 %all-to-all-start = ((bf16[128,16,256]{2,1,0:T(8,128)(2,1)}), bf16[128,16,256]{2,1,0:T(8,128)(2,1)S(1)}, u32[]{:S(2)}, u32[]{:S(2)}) async-start(bf16[128,16,256]{2,1,0:T(8,128)(2,1)} %bitcast.66), calls=%async_computation | async-start | bytes 2097152 | tf_op jit(solution)/shard_map/all_to_all | solution.py:271
  30.2 0.2 reduce_window_sum.11
  30.4 2.1 %fusion.23 = (f32[1024,64]{1,0:T(8,128)S(1)}, f32[1024,64]{1,0:T(8,128)S(1)}) fusion(s32[1024]{0:T(1024)S(1)} %iota_add_fusion), kind=kLoop, calls=%fused_computation.49 | loop fusion | flops 983040 | bytes 528384 | tf_op jit(solution)/shard_map/cos | solution.py:76
  32.6 17.1 %all-to-all-done = bf16[128,16,256]{2,1,0:T(8,128)(2,1)S(1)} async-done(((bf16[128,16,256]{2,1,0:T(8,128)(2,1)}), bf16[128,16,256]{2,1,0:T(8,128)(2,1)S(1)}, u32[]{:S(2)}, u32[]{:S(2)}) %all-to-all-start) | async-done | bytes 1048608 | tf_op jit(solution)/shard_map/all_to_all | solution.py:271
  49.7 0.6 gather_fusion
  50.2 0.6 gather_fusion.1
  50.9 0.2 reshape.177
  51.1 0.2 reshape.178
  51.4 0.3 fusion.25
  51.7 0.3 fusion.24
  52.0 0.3 fusion.5
  52.2 0.3 fusion.4
  52.6 0.7 copy.44
  53.3 0.3 copy.45
  53.7 0.4 convolution_bitcast_fusion
  54.0 1.5 %copy.46 = f32[32,4,8,2,16]{4,3,2,1,0:T(2,128)S(1)} copy(f32[32,4,8,2,16]{0,2,1,4,3:T(8,128)S(1)} %convolution_bitcast_fusion) | data formatting | bytes 262144 | tf_op jit(solution)/shard_map/nst,twqv->wnsqv/transpose | solution.py:298
  55.5 2.1 %all_to_all.12 = f32[128,1,256]{2,1,0:T(1,128)} reshape(f32[32,4,8,2,16]{4,3,2,1,0:T(2,128)S(1)} %copy.46) | data formatting | bytes 262144 | tf_op jit(solution)/shard_map/all_to_all | solution.py:300
  57.6 3.9 %all-to-all-start.1 = ((f32[128,1,256]{2,1,0:T(1,128)}), f32[128,1,256]{2,1,0:T(1,128)S(1)}, u32[]{:S(2)}, u32[]{:S(2)}) async-start(f32[128,1,256]{2,1,0:T(1,128)} %all_to_all.12), calls=%async_computation.1 | async-start | bytes 262144 | tf_op jit(solution)/shard_map/all_to_all | solution.py:300
  61.6 0.2 fusion.30
  61.8 9.6 %all-to-all-done.1 = f32[128,1,256]{2,1,0:T(1,128)S(1)} async-done(((f32[128,1,256]{2,1,0:T(1,128)}), f32[128,1,256]{2,1,0:T(1,128)S(1)}, u32[]{:S(2)}, u32[]{:S(2)}) %all-to-all-start.1) | async-done | bytes 131104 | tf_op jit(solution)/shard_map/all_to_all | solution.py:300
  71.5 0.4 copy.49
  72.0 0.2 copy.50
  72.2 0.2 copy.51
  72.5 1.2 %fusion.9 = f32[128,64]{1,0:T(8,128)S(1)} fusion(f32[128,1024]{1,0:T(8,128)S(1)} %get-tuple-element.13, f32[128,1024]{1,0:T(8,128)S(1)} %get-tuple-element.12, f32[1024,64]{1,0:T(8,128)S(1)} %get-tuple-element.17, f32[1024,64]{1,0:T(8,128)S(1)} %get-tuple-element.16), kind=kOutput, calls=%fused_computation.20 | convolution fusion | flops 201850880 | bytes 1605632 | tf_op jit(solution)/shard_map/dot_general | solution.py:143
  73.7 0.7 reshape_reshape.3
  (19 shorter events, 0.6 us)
Async XLA Ops:
  12.6 4.0 %copy-start = (f32[256,2048]{1,0:T(8,128)S(1)}, f32[256,2048]{1,0:T(8,128)}, u32[]{:S(2)}) copy-start(f32[256,2048]{1,0:T(8,128)} %shard_map.82) | copy-start | bytes 6291460
  17.0 13.1 %copy-start.2 = (s32[16]{0:T(128)S(1)}, s32[16]{0:T(128)}, u32[]{:S(2)}) copy-start(s32[16]{0:T(128)} %param.13) | copy-start | bytes 196
  17.0 13.3 %copy-start.1 = (s32[16,2]{0,1:T(2,128)S(1)}, s32[16,2]{0,1:T(2,128)}, u32[]{:S(2)}) copy-start(s32[16,2]{0,1:T(2,128)} %param.12) | copy-start | bytes 388
  18.6 31.0 %all-to-all-start = ((bf16[128,16,256]{2,1,0:T(8,128)(2,1)}), bf16[128,16,256]{2,1,0:T(8,128)(2,1)S(1)}, u32[]{:S(2)}, u32[]{:S(2)}) async-start(bf16[128,16,256]{2,1,0:T(8,128)(2,1)} %bitcast.66), calls=%async_computation | async-start | bytes 2097152 | tf_op jit(solution)/shard_map/all_to_all | solution.py:271
  57.6 13.8 %all-to-all-start.1 = ((f32[128,1,256]{2,1,0:T(1,128)}), f32[128,1,256]{2,1,0:T(1,128)S(1)}, u32[]{:S(2)}, u32[]{:S(2)}) async-start(f32[128,1,256]{2,1,0:T(1,128)} %all_to_all.12), calls=%async_computation.1 | async-start | bytes 262144 | tf_op jit(solution)/shard_map/all_to_all | solution.py:300

commit v12 on v8

--- a/solution.py
+++ b/solution.py
@@ -266,19 +266,19 @@
     whitened = whiten(decimate_dft(raw_samples, filter_taps), devices, group)
     spectra = lax.all_to_all(whitened, ("wide", "narrow"), 0, 0, tiled=True)
 
-    source = jnp.take(spectra, tile_pairs[:, 0], axis=0)
-    target = jnp.take(spectra, tile_pairs[:, 1], axis=0)
     tiles = tile_pairs.shape[0]
-    source = source.reshape(tiles, 2, group, BLK, window_total)
-    target = target.reshape(tiles, 2, group, BLK, window_total)
-    src_real, src_imag = source[:, 0], source[:, 1]
-    dst_real, dst_imag = target[:, 0], target[:, 1]
+    blocks = jnp.take(spectra, jnp.transpose(tile_pairs).reshape(-1), axis=0)
+    blocks = blocks.reshape(2, tiles, 2, group, BLK, window_total)
+    source, target = blocks[0], blocks[1]
+    src_both = jnp.concatenate([source[:, 0], source[:, 1]], axis=-1)
+    dst_real_imag = jnp.concatenate([target[:, 0], target[:, 1]], axis=-1)
+    dst_imag_real = jnp.concatenate([target[:, 1], -target[:, 0]], axis=-1)
 
     def mm(a, b):
         return jnp.einsum("tbiw,tbjw->tbij", a, b, preferred_element_type=jnp.float32)
 
-    real_sum = mm(src_real, dst_real) + mm(src_imag, dst_imag)
-    imag_sum = mm(src_real, dst_imag) - mm(src_imag, dst_real)
+    real_sum = mm(src_both, dst_real_imag)
+    imag_sum = mm(src_both, dst_imag_real)
     cross = jnp.stack([real_sum, imag_sum], axis=1)
     pair_share = BLK * BLK // wide_count
     cross = cross.reshape(tiles, 2 * group, BLK * BLK // pair_share, pair_share)

time: 74.9 us -> 74.1 us (0.989)
  transfers between devices with their start and end apart: 2 -> 2, of which waited for: 2 -> 2; matrix products, arithmetic and copies ran while one was open for 3% -> 4% of each run, Pallas kernels for 0% -> 0%
where the time goes in v12:
time: 74.1 us; the launch traced here: 73.9 us
  waiting for transfers between devices  26.6 us (36%)
  starting transfers between devices  15.4 us (21%)
  Pallas kernels  12.7 us (17%)
  local copies, waits for them, and re-layouts  9.16 us (12%)
  matrix products  6.09 us (8%)
  other arithmetic  3.71 us (5%)
    all_to_all x1, waiting for transfers between devices, on_device(): spectra = lax.all_to_all(whitened, ('wide', 'narrow'), 0, 0, tiled=True)  16.9 us
    pallas_call x1, Pallas kernels, decimate_dft(): pl.pallas_call(functools.partial(fused_kernel, dec_steps=dec_steps, halve...  12.7 us
    all_to_all x1, starting transfers between devices, on_device(): spectra = lax.all_to_all(whitened, ('wide', 'narrow'), 0, 0, tiled=True)  11.5 us
    all_to_all x1, waiting for transfers between devices, on_device(): arrived = lax.all_to_all(send, ('wide', 'narrow'), 0, 0, tiled=True)  9.65 us
    all_to_all x1, starting transfers between devices, on_device(): arrived = lax.all_to_all(send, ('wide', 'narrow'), 0, 0, tiled=True)  3.9 us
    dot_general x1, matrix products, whiten(): jnp.dot(magnitude, smoother(NBINS, SMOOTH), precision=lax.Precision.HIGH)  3.78 us
    cos x2, other arithmetic, trig(): return (jnp.cos(angle), jnp.sin(angle))  2.34 us
    all_to_all x2, local copies, waits for them, and re-layouts, on_device(): arrived = lax.all_to_all(send, ('wide', 'narrow'), 0, 0, tiled=True)  2.2 us
  transfers between devices with their start and end apart: 2, of which 2 were waited for; matrix products, arithmetic and copies ran while one was open for 4% of the time, Pallas kernels for 0%

profile of v12, /device:TPU:1, one launch (start us, length us, event | category | flops | bytes accessed | tf_op | source)
XLA Modules:
  0.0 73.9 jit_solution(18052573002071745370)
XLA Ops:
  0.0 0.2 convert_reduce_fusion
  0.2 12.7 %shard_map.82 = f32[256,2048]{1,0:T(8,128)} custom-call(f32[64]{0:T(128)} %taps_ref.1, bf16[8,32,16384]{2,1,0:T(8,128)(2,1)} %x_ref.1, f32[32,1024]{1,0:T(8,128)} %constant.76.clone.c1_ref, f32[32,1024]{1,0:T(8,128)} %constant.77.clone.s1_ref, f32[128,1024]{1,0:T(8,128)} %constant.78.clone.c2_ref, f32[128,1024]{1,0:T(8,128)} %constant.79.clone.s2_ref), custom_call_target="tpu_custom_call" | custom-call | tf_op jit(solution)/shard_map/pallas_call | solution.py:222
  12.9 3.8 %fusion.47 = (f32[256]{0:T(256)S(1)}, f32[256,1024]{1,0:T(8,128)S(1)}) fusion(f32[1024]{0:T(1024)S(1)} %convert_reduce_fusion, f32[256,2048]{1,0:T(8,128)} %shard_map.82), kind=kOutput, calls=%fused_computation.88 | convolution fusion | flops 1616903936 | bytes 3150848 | tf_op jit(solution)/shard_map/dot_general | solution.py:249
  16.7 0.2 add_divide_fusion
  17.0 0.3 fusion.1
  17.3 0.5 copy.38
  17.9 1.1 %copy.61 = bf16[128,2,8,256]{3,2,1,0:T(8,128)(2,1)} copy(bf16[128,2,8,256]{3,2,0,1:T(8,128)(2,1)S(1)} %bitcast.59) | data formatting | bytes 2097152 | tf_op jit(solution)/shard_map/transpose | solution.py:253
  18.9 11.5 %all-to-all-start = ((bf16[128,16,256]{2,1,0:T(8,128)(2,1)}), bf16[128,16,256]{2,1,0:T(8,128)(2,1)S(1)}, u32[]{:S(2)}, u32[]{:S(2)}) async-start(bf16[128,16,256]{2,1,0:T(8,128)(2,1)} %bitcast.57), calls=%async_computation | async-start | bytes 2097152 | tf_op jit(solution)/shard_map/all_to_all | solution.py:267
  30.6 0.2 reduce_window_sum.11
  30.9 2.1 %fusion.27 = (f32[1024,64]{1,0:T(8,128)S(1)}, f32[1024,64]{1,0:T(8,128)S(1)}) fusion(s32[1024]{0:T(1024)S(1)} %iota_add_fusion), kind=kLoop, calls=%fused_computation.53 | loop fusion | flops 983040 | bytes 528384 | tf_op jit(solution)/shard_map/cos | solution.py:76
  33.0 16.9 %all-to-all-done = bf16[128,16,256]{2,1,0:T(8,128)(2,1)S(1)} async-done(((bf16[128,16,256]{2,1,0:T(8,128)(2,1)}), bf16[128,16,256]{2,1,0:T(8,128)(2,1)S(1)}, u32[]{:S(2)}, u32[]{:S(2)}) %all-to-all-start) | async-done | bytes 1048608 | tf_op jit(solution)/shard_map/all_to_all | solution.py:267
  49.9 0.6 gather_fusion
  50.5 0.1 broadcast_select_fusion
  50.6 0.2 squeeze.23
  50.9 0.2 squeeze.20
  51.3 0.4 convolution_bitcast_fusion.2
  51.6 0.4 convolution_bitcast_fusion.1
  52.1 0.7 copy.44
  52.9 0.3 copy.45
  53.2 0.4 convolution_bitcast_fusion
  53.5 1.5 %copy.46 = f32[32,4,8,2,16]{4,3,2,1,0:T(2,128)S(1)} copy(f32[32,4,8,2,16]{0,2,1,4,3:T(8,128)S(1)} %convolution_bitcast_fusion) | data formatting | bytes 262144 | tf_op jit(solution)/shard_map/nst,twqv->wnsqv/transpose | solution.py:294
  55.1 2.1 %all_to_all.12 = f32[128,1,256]{2,1,0:T(1,128)} reshape(f32[32,4,8,2,16]{4,3,2,1,0:T(2,128)S(1)} %copy.46) | data formatting | bytes 262144 | tf_op jit(solution)/shard_map/all_to_all | solution.py:296
  57.2 3.9 %all-to-all-start.1 = ((f32[128,1,256]{2,1,0:T(1,128)}), f32[128,1,256]{2,1,0:T(1,128)S(1)}, u32[]{:S(2)}, u32[]{:S(2)}) async-start(f32[128,1,256]{2,1,0:T(1,128)} %all_to_all.12), calls=%async_computation.1 | async-start | bytes 262144 | tf_op jit(solution)/shard_map/all_to_all | solution.py:296
  61.1 0.2 fusion.32
  61.3 9.7 %all-to-all-done.1 = f32[128,1,256]{2,1,0:T(1,128)S(1)} async-done(((f32[128,1,256]{2,1,0:T(1,128)}), f32[128,1,256]{2,1,0:T(1,128)S(1)}, u32[]{:S(2)}, u32[]{:S(2)}) %all-to-all-start.1) | async-done | bytes 131104 | tf_op jit(solution)/shard_map/all_to_all | solution.py:296
  70.9 0.1 copy.48
  71.0 0.4 copy.49
  71.5 0.2 copy.50
  71.7 0.2 copy.51
  71.9 0.2 subtract_bitcast_fusion
  72.0 1.2 %fusion.7 = f32[128,64]{1,0:T(8,128)S(1)} fusion(f32[128,1024]{1,0:T(8,128)S(1)} %get-tuple-element.14, f32[128,1024]{1,0:T(8,128)S(1)} %get-tuple-element.13, f32[1024,64]{1,0:T(8,128)S(1)} %get-tuple-element.18, f32[1024,64]{1,0:T(8,128)S(1)} %get-tuple-element.17), kind=kOutput, calls=%fused_computation.17 | convolution fusion | flops 201850880 | bytes 1605632 | tf_op jit(solution)/shard_map/dot_general | solution.py:143
  73.2 0.7 reshape_reshape.3
  (21 shorter events, 0.5 us)
Async XLA Ops:
  12.9 4.0 %copy-start = (f32[256,2048]{1,0:T(8,128)S(1)}, f32[256,2048]{1,0:T(8,128)}, u32[]{:S(2)}) copy-start(f32[256,2048]{1,0:T(8,128)} %shard_map.82) | copy-start | bytes 6291460
  17.3 13.1 %copy-start.1 = (s32[16]{0:T(128)S(1)}, s32[16]{0:T(128)}, u32[]{:S(2)}) copy-start(s32[16]{0:T(128)} %param.11) | copy-start | bytes 196
  17.3 13.1 %copy-start.2 = (s32[16,2]{0,1:T(2,128)S(1)}, s32[16,2]{0,1:T(2,128)}, u32[]{:S(2)}) copy-start(s32[16,2]{0,1:T(2,128)} %param.10) | copy-start | bytes 388
  18.9 31.0 %all-to-all-start = ((bf16[128,16,256]{2,1,0:T(8,128)(2,1)}), bf16[128,16,256]{2,1,0:T(8,128)(2,1)S(1)}, u32[]{:S(2)}, u32[]{:S(2)}) async-start(bf16[128,16,256]{2,1,0:T(8,128)(2,1)} %bitcast.57), calls=%async_computation | async-start | bytes 2097152 | tf_op jit(solution)/shard_map/all_to_all | solution.py:267
  57.2 13.8 %all-to-all-start.1 = ((f32[128,1,256]{2,1,0:T(1,128)}), f32[128,1,256]{2,1,0:T(1,128)S(1)}, u32[]{:S(2)}, u32[]{:S(2)}) async-start(f32[128,1,256]{2,1,0:T(1,128)} %all_to_all.12), calls=%async_computation.1 | async-start | bytes 262144 | tf_op jit(solution)/shard_map/all_to_all | solution.py:296

commit v13 on v12

--- a/solution.py
+++ b/solution.py
@@ -275,14 +275,13 @@
     dst_imag_real = jnp.concatenate([target[:, 1], -target[:, 0]], axis=-1)
 
     def mm(a, b):
-        return jnp.einsum("tbiw,tbjw->tbij", a, b, preferred_element_type=jnp.float32)
+        return jnp.einsum("tbiw,tbjw->tijb", a, b, preferred_element_type=jnp.float32)
 
     real_sum = mm(src_both, dst_real_imag)
     imag_sum = mm(src_both, dst_imag_real)
-    cross = jnp.stack([real_sum, imag_sum], axis=1)
+    cross = jnp.stack([real_sum, imag_sum], axis=3)
     pair_share = BLK * BLK // wide_count
-    cross = cross.reshape(tiles, 2 * group, BLK * BLK // pair_share, pair_share)
-    cross = jnp.transpose(cross, (0, 2, 3, 1))
+    cross = cross.reshape(tiles, BLK * BLK // pair_share, pair_share, 2 * group)
 
     slot_ids = jnp.arange(SLOTS, dtype=jnp.int32)
     owner_ids = jnp.arange(narrow_count, dtype=jnp.int32)

time: 74.1 us -> 74.8 us (level)
  matrix products: 6.09 us -> 7.02 us
    dot_general x1, matrix products: 0.36 us -> 1.28 us  [on_device(): jnp.einsum('nst,twqv->wnsqv', select_all, cross, precision=lax.Precision....]
where the time goes in v13:
time: 74.8 us; the launch traced here: 74.6 us
  waiting for transfers between devices  26.6 us (36%)
  starting transfers between devices  15.4 us (21%)
  Pallas kernels  12.7 us (17%)
  local copies, waits for them, and re-layouts  8.89 us (12%)
  matrix products  7.02 us (9%)
  other arithmetic  3.71 us (5%)
    all_to_all x1, waiting for transfers between devices, on_device(): spectra = lax.all_to_all(whitened, ('wide', 'narrow'), 0, 0, tiled=True)  16.9 us
    pallas_call x1, Pallas kernels, decimate_dft(): pl.pallas_call(functools.partial(fused_kernel, dec_steps=dec_steps, halve...  12.7 us
    all_to_all x1, starting transfers between devices, on_device(): spectra = lax.all_to_all(whitened, ('wide', 'narrow'), 0, 0, tiled=True)  11.5 us
    all_to_all x1, waiting for transfers between devices, on_device(): arrived = lax.all_to_all(send, ('wide', 'narrow'), 0, 0, tiled=True)  9.65 us
    all_to_all x1, starting transfers between devices, on_device(): arrived = lax.all_to_all(send, ('wide', 'narrow'), 0, 0, tiled=True)  3.91 us
    dot_general x1, matrix products, whiten(): jnp.dot(magnitude, smoother(NBINS, SMOOTH), precision=lax.Precision.HIGH)  3.78 us
    cos x2, other arithmetic, trig(): return (jnp.cos(angle), jnp.sin(angle))  2.34 us
    all_to_all x2, local copies, waits for them, and re-layouts, on_device(): arrived = lax.all_to_all(send, ('wide', 'narrow'), 0, 0, tiled=True)  2.2 us
  transfers between devices with their start and end apart: 2, of which 2 were waited for; matrix products, arithmetic and copies ran while one was open for 4% of the time, Pallas kernels for 0%

profile of v13, /device:TPU:1, one launch (start us, length us, event | category | flops | bytes accessed | tf_op | source)
XLA Modules:
  0.0 74.6 jit_solution(7127004450237377611)
XLA Ops:
  0.0 0.2 convert_reduce_fusion
  0.2 12.7 %shard_map.82 = f32[256,2048]{1,0:T(8,128)} custom-call(f32[64]{0:T(128)} %taps_ref.1, bf16[8,32,16384]{2,1,0:T(8,128)(2,1)} %x_ref.1, f32[32,1024]{1,0:T(8,128)} %constant.76.clone.c1_ref, f32[32,1024]{1,0:T(8,128)} %constant.77.clone.s1_ref, f32[128,1024]{1,0:T(8,128)} %constant.78.clone.c2_ref, f32[128,1024]{1,0:T(8,128)} %constant.79.clone.s2_ref), custom_call_target="tpu_custom_call" | custom-call | tf_op jit(solution)/shard_map/pallas_call | solution.py:222
  12.9 3.8 %fusion.47 = (f32[256]{0:T(256)S(1)}, f32[256,1024]{1,0:T(8,128)S(1)}) fusion(f32[1024]{0:T(1024)S(1)} %convert_reduce_fusion, f32[256,2048]{1,0:T(8,128)} %shard_map.82), kind=kOutput, calls=%fused_computation.88 | convolution fusion | flops 1616903936 | bytes 3150848 | tf_op jit(solution)/shard_map/dot_general | solution.py:249
  16.7 0.2 add_divide_fusion
  17.0 0.3 fusion.1
  17.3 0.5 copy.38
  17.9 1.1 %copy.65 = bf16[128,2,8,256]{3,2,1,0:T(8,128)(2,1)} copy(bf16[128,2,8,256]{3,2,0,1:T(8,128)(2,1)S(1)} %bitcast.58) | data formatting | bytes 2097152 | tf_op jit(solution)/shard_map/transpose | solution.py:253
  18.9 11.5 %all-to-all-start = ((bf16[128,16,256]{2,1,0:T(8,128)(2,1)}), bf16[128,16,256]{2,1,0:T(8,128)(2,1)S(1)}, u32[]{:S(2)}, u32[]{:S(2)}) async-start(bf16[128,16,256]{2,1,0:T(8,128)(2,1)} %bitcast.56), calls=%async_computation | async-start | bytes 2097152 | tf_op jit(solution)/shard_map/all_to_all | solution.py:267
  30.6 0.2 reduce_window_sum.11
  30.9 2.1 %fusion.27 = (f32[1024,64]{1,0:T(8,128)S(1)}, f32[1024,64]{1,0:T(8,128)S(1)}) fusion(s32[1024]{0:T(1024)S(1)} %iota_add_fusion), kind=kLoop, calls=%fused_computation.53 | loop fusion | flops 983040 | bytes 528384 | tf_op jit(solution)/shard_map/cos | solution.py:76
  33.0 16.9 %all-to-all-done = bf16[128,16,256]{2,1,0:T(8,128)(2,1)S(1)} async-done(((bf16[128,16,256]{2,1,0:T(8,128)(2,1)}), bf16[128,16,256]{2,1,0:T(8,128)(2,1)S(1)}, u32[]{:S(2)}, u32[]{:S(2)}) %all-to-all-start) | async-done | bytes 1048608 | tf_op jit(solution)/shard_map/all_to_all | solution.py:267
  49.9 0.6 gather_fusion
  50.5 0.1 broadcast_select_fusion
  50.6 0.2 squeeze.20
  50.9 0.2 squeeze.23
  51.3 0.4 convolution_bitcast_fusion.2
  51.6 0.4 convolution_bitcast_fusion.1
  52.0 0.1 pad_maximum_fusion
  52.1 0.8 %copy.44 = f32[16,8,8,2,8]{0,4,3,2,1:T(8,128)S(1)} copy(f32[16,8,8,2,8]{1,2,4,0,3:T(8,128)S(1)} %pad_maximum_fusion) | data formatting | bytes 131072 | tf_op jit(solution)/shard_map/stack | solution.py:282
  52.9 1.3 %convolution_bitcast_fusion = f32[32,4,8,2,16]{0,2,1,4,3:T(8,128)S(1)} fusion(f32[16,32,2,16,1]{0,3,2,1,4:T(8,128)S(1)} %bitcast.59, s32[4,16]{1,0:T(4,128)S(1)} %broadcast_add_fusion, pred[4,16]{1,0:T(4,128)(4,1)S(1)} %get-tuple-element.19), kind=kOutput, calls=%fused_computation.9 | convolution fusion | flops 6292480 | bytes 196928 | tf_op jit(solution)/shard_map/nst,twqv->wnsqv/dot_general | solution.py:293
  54.2 1.5 %copy.46 = f32[32,4,8,2,16]{4,3,2,1,0:T(2,128)S(1)} copy(f32[32,4,8,2,16]{0,2,1,4,3:T(8,128)S(1)} %convolution_bitcast_fusion) | data formatting | bytes 262144 | tf_op jit(solution)/shard_map/nst,twqv->wnsqv/transpose | solution.py:293
  55.7 2.1 %all_to_all.12 = f32[128,1,256]{2,1,0:T(1,128)} reshape(f32[32,4,8,2,16]{4,3,2,1,0:T(2,128)S(1)} %copy.46) | data formatting | bytes 262144 | tf_op jit(solution)/shard_map/all_to_all | solution.py:295
  57.8 3.9 %all-to-all-start.1 = ((f32[128,1,256]{2,1,0:T(1,128)}), f32[128,1,256]{2,1,0:T(1,128)S(1)}, u32[]{:S(2)}, u32[]{:S(2)}) async-start(f32[128,1,256]{2,1,0:T(1,128)} %all_to_all.12), calls=%async_computation.1 | async-start | bytes 262144 | tf_op jit(solution)/shard_map/all_to_all | solution.py:295
  61.7 0.2 fusion.32
  61.9 9.7 %all-to-all-done.1 = f32[128,1,256]{2,1,0:T(1,128)S(1)} async-done(((f32[128,1,256]{2,1,0:T(1,128)}), f32[128,1,256]{2,1,0:T(1,128)S(1)}, u32[]{:S(2)}, u32[]{:S(2)}) %all-to-all-start.1) | async-done | bytes 131104 | tf_op jit(solution)/shard_map/all_to_all | solution.py:295
  71.6 0.1 copy.48
  71.7 0.4 copy.49
  72.2 0.2 copy.50
  72.4 0.2 copy.51
  72.5 0.2 subtract_bitcast_fusion
  72.7 1.2 %fusion.7 = f32[128,64]{1,0:T(8,128)S(1)} fusion(f32[128,1024]{1,0:T(8,128)S(1)} %get-tuple-element.14, f32[128,1024]{1,0:T(8,128)S(1)} %get-tuple-element.13, f32[1024,64]{1,0:T(8,128)S(1)} %get-tuple-element.18, f32[1024,64]{1,0:T(8,128)S(1)} %get-tuple-element.17), kind=kOutput, calls=%fused_computation.17 | convolution fusion | flops 201850880 | bytes 1605632 | tf_op jit(solution)/shard_map/dot_general | solution.py:143
  73.9 0.7 reshape_reshape.3
  (20 shorter events, 0.4 us)
Async XLA Ops:
  12.9 4.0 %copy-start = (f32[256,2048]{1,0:T(8,128)S(1)}, f32[256,2048]{1,0:T(8,128)}, u32[]{:S(2)}) copy-start(f32[256,2048]{1,0:T(8,128)} %shard_map.82) | copy-start | bytes 6291460
  17.3 13.1 %copy-start.1 = (s32[16]{0:T(128)S(1)}, s32[16]{0:T(128)}, u32[]{:S(2)}) copy-start(s32[16]{0:T(128)} %param.11) | copy-start | bytes 196
  17.3 13.1 %copy-start.2 = (s32[16,2]{0,1:T(2,128)S(1)}, s32[16,2]{0,1:T(2,128)}, u32[]{:S(2)}) copy-start(s32[16,2]{0,1:T(2,128)} %param.10) | copy-start | bytes 388
  18.9 31.0 %all-to-all-start = ((bf16[128,16,256]{2,1,0:T(8,128)(2,1)}), bf16[128,16,256]{2,1,0:T(8,128)(2,1)S(1)}, u32[]{:S(2)}, u32[]{:S(2)}) async-start(bf16[128,16,256]{2,1,0:T(8,128)(2,1)} %bitcast.56), calls=%async_computation | async-start | bytes 2097152 | tf_op jit(solution)/shard_map/all_to_all | solution.py:267
  57.8 13.8 %all-to-all-start.1 = ((f32[128,1,256]{2,1,0:T(1,128)}), f32[128,1,256]{2,1,0:T(1,128)S(1)}, u32[]{:S(2)}, u32[]{:S(2)}) async-start(f32[128,1,256]{2,1,0:T(1,128)} %all_to_all.12), calls=%async_computation.1 | async-start | bytes 262144 | tf_op jit(solution)/shard_map/all_to_all | solution.py:295

commit v14 on v12

--- a/solution.py
+++ b/solution.py
@@ -140,7 +140,7 @@
     v = xr * sa[None] + xi * ca[None]
     uv = jnp.concatenate([u, v], axis=2).reshape(pairs * (lag_count // split), 2 * bin_count)
     table = jnp.concatenate([cb, -sb], axis=0) * weight
-    out = jnp.dot(uv, table, precision=lax.Precision.HIGHEST)
+    out = jnp.dot(uv, table, precision=lax.Precision.HIGH)
     return out.reshape(pairs, lag_count)
 
 

time: 74.1 us -> 73.6 us (level)
  no operation moved by 1% of the time
where the time goes in v14:
time: 73.6 us; the launch traced here: 73.4 us
  waiting for transfers between devices  26.6 us (36%)
  starting transfers between devices  15.4 us (21%)
  Pallas kernels  12.7 us (17%)
  local copies, waits for them, and re-layouts  9.16 us (12%)
  matrix products  5.59 us (8%)
  other arithmetic  3.71 us (5%)
    all_to_all x1, waiting for transfers between devices, on_device(): spectra = lax.all_to_all(whitened, ('wide', 'narrow'), 0, 0, tiled=True)  16.9 us
    pallas_call x1, Pallas kernels, decimate_dft(): pl.pallas_call(functools.partial(fused_kernel, dec_steps=dec_steps, halve...  12.7 us
    all_to_all x1, starting transfers between devices, on_device(): spectra = lax.all_to_all(whitened, ('wide', 'narrow'), 0, 0, tiled=True)  11.5 us
    all_to_all x1, waiting for transfers between devices, on_device(): arrived = lax.all_to_all(send, ('wide', 'narrow'), 0, 0, tiled=True)  9.65 us
    all_to_all x1, starting transfers between devices, on_device(): arrived = lax.all_to_all(send, ('wide', 'narrow'), 0, 0, tiled=True)  3.9 us
    dot_general x1, matrix products, whiten(): jnp.dot(magnitude, smoother(NBINS, SMOOTH), precision=lax.Precision.HIGH)  3.78 us
    cos x2, other arithmetic, trig(): return (jnp.cos(angle), jnp.sin(angle))  2.34 us
    all_to_all x2, local copies, waits for them, and re-layouts, on_device(): arrived = lax.all_to_all(send, ('wide', 'narrow'), 0, 0, tiled=True)  2.2 us
  transfers between devices with their start and end apart: 2, of which 2 were waited for; matrix products, arithmetic and copies ran while one was open for 4% of the time, Pallas kernels for 0%

profile of v14, /device:TPU:1, one launch (start us, length us, event | category | flops | bytes accessed | tf_op | source)
XLA Modules:
  0.0 73.4 jit_solution(9058481876178096902)
XLA Ops:
  0.0 0.2 convert_reduce_fusion
  0.2 12.7 %shard_map.82 = f32[256,2048]{1,0:T(8,128)} custom-call(f32[64]{0:T(128)} %taps_ref.1, bf16[8,32,16384]{2,1,0:T(8,128)(2,1)} %x_ref.1, f32[32,1024]{1,0:T(8,128)} %constant.76.clone.c1_ref, f32[32,1024]{1,0:T(8,128)} %constant.77.clone.s1_ref, f32[128,1024]{1,0:T(8,128)} %constant.78.clone.c2_ref, f32[128,1024]{1,0:T(8,128)} %constant.79.clone.s2_ref), custom_call_target="tpu_custom_call" | custom-call | tf_op jit(solution)/shard_map/pallas_call | solution.py:222
  12.9 3.8 %fusion.47 = (f32[256]{0:T(256)S(1)}, f32[256,1024]{1,0:T(8,128)S(1)}) fusion(f32[1024]{0:T(1024)S(1)} %convert_reduce_fusion, f32[256,2048]{1,0:T(8,128)} %shard_map.82), kind=kOutput, calls=%fused_computation.88 | convolution fusion | flops 1616903936 | bytes 3150848 | tf_op jit(solution)/shard_map/dot_general | solution.py:249
  16.7 0.2 add_divide_fusion
  17.0 0.3 fusion.1
  17.3 0.5 copy.38
  17.9 1.1 %copy.61 = bf16[128,2,8,256]{3,2,1,0:T(8,128)(2,1)} copy(bf16[128,2,8,256]{3,2,0,1:T(8,128)(2,1)S(1)} %bitcast.59) | data formatting | bytes 2097152 | tf_op jit(solution)/shard_map/transpose | solution.py:253
  18.9 11.5 %all-to-all-start = ((bf16[128,16,256]{2,1,0:T(8,128)(2,1)}), bf16[128,16,256]{2,1,0:T(8,128)(2,1)S(1)}, u32[]{:S(2)}, u32[]{:S(2)}) async-start(bf16[128,16,256]{2,1,0:T(8,128)(2,1)} %bitcast.57), calls=%async_computation | async-start | bytes 2097152 | tf_op jit(solution)/shard_map/all_to_all | solution.py:267
  30.6 0.2 reduce_window_sum.11
  30.9 2.1 %fusion.27 = (f32[1024,64]{1,0:T(8,128)S(1)}, f32[1024,64]{1,0:T(8,128)S(1)}) fusion(s32[1024]{0:T(1024)S(1)} %iota_add_fusion), kind=kLoop, calls=%fused_computation.53 | loop fusion | flops 983040 | bytes 528384 | tf_op jit(solution)/shard_map/cos | solution.py:76
  33.0 16.9 %all-to-all-done = bf16[128,16,256]{2,1,0:T(8,128)(2,1)S(1)} async-done(((bf16[128,16,256]{2,1,0:T(8,128)(2,1)}), bf16[128,16,256]{2,1,0:T(8,128)(2,1)S(1)}, u32[]{:S(2)}, u32[]{:S(2)}) %all-to-all-start) | async-done | bytes 1048608 | tf_op jit(solution)/shard_map/all_to_all | solution.py:267
  49.9 0.6 gather_fusion
  50.5 0.1 broadcast_select_fusion
  50.6 0.2 squeeze.23
  50.9 0.2 squeeze.20
  51.3 0.4 convolution_bitcast_fusion.2
  51.6 0.4 convolution_bitcast_fusion.1
  52.1 0.7 copy.44
  52.9 0.3 copy.45
  53.2 0.4 convolution_bitcast_fusion
  53.5 1.5 %copy.46 = f32[32,4,8,2,16]{4,3,2,1,0:T(2,128)S(1)} copy(f32[32,4,8,2,16]{0,2,1,4,3:T(8,128)S(1)} %convolution_bitcast_fusion) | data formatting | bytes 262144 | tf_op jit(solution)/shard_map/nst,twqv->wnsqv/transpose | solution.py:294
  55.1 2.1 %all_to_all.12 = f32[128,1,256]{2,1,0:T(1,128)} reshape(f32[32,4,8,2,16]{4,3,2,1,0:T(2,128)S(1)} %copy.46) | data formatting | bytes 262144 | tf_op jit(solution)/shard_map/all_to_all | solution.py:296
  57.2 3.9 %all-to-all-start.1 = ((f32[128,1,256]{2,1,0:T(1,128)}), f32[128,1,256]{2,1,0:T(1,128)S(1)}, u32[]{:S(2)}, u32[]{:S(2)}) async-start(f32[128,1,256]{2,1,0:T(1,128)} %all_to_all.12), calls=%async_computation.1 | async-start | bytes 262144 | tf_op jit(solution)/shard_map/all_to_all | solution.py:296
  61.1 0.2 fusion.32
  61.3 9.7 %all-to-all-done.1 = f32[128,1,256]{2,1,0:T(1,128)S(1)} async-done(((f32[128,1,256]{2,1,0:T(1,128)}), f32[128,1,256]{2,1,0:T(1,128)S(1)}, u32[]{:S(2)}, u32[]{:S(2)}) %all-to-all-start.1) | async-done | bytes 131104 | tf_op jit(solution)/shard_map/all_to_all | solution.py:296
  70.9 0.1 copy.48
  71.0 0.4 copy.49
  71.5 0.2 copy.50
  71.7 0.2 copy.51
  71.9 0.2 subtract_bitcast_fusion
  72.0 0.7 fusion.7
  72.7 0.7 reshape_reshape.3
  (21 shorter events, 0.5 us)
Async XLA Ops:
  12.9 4.0 %copy-start = (f32[256,2048]{1,0:T(8,128)S(1)}, f32[256,2048]{1,0:T(8,128)}, u32[]{:S(2)}) copy-start(f32[256,2048]{1,0:T(8,128)} %shard_map.82) | copy-start | bytes 6291460
  17.3 13.1 %copy-start.1 = (s32[16]{0:T(128)S(1)}, s32[16]{0:T(128)}, u32[]{:S(2)}) copy-start(s32[16]{0:T(128)} %param.11) | copy-start | bytes 196
  17.3 13.1 %copy-start.2 = (s32[16,2]{0,1:T(2,128)S(1)}, s32[16,2]{0,1:T(2,128)}, u32[]{:S(2)}) copy-start(s32[16,2]{0,1:T(2,128)} %param.10) | copy-start | bytes 388
  18.9 31.0 %all-to-all-start = ((bf16[128,16,256]{2,1,0:T(8,128)(2,1)}), bf16[128,16,256]{2,1,0:T(8,128)(2,1)S(1)}, u32[]{:S(2)}, u32[]{:S(2)}) async-start(bf16[128,16,256]{2,1,0:T(8,128)(2,1)} %bitcast.57), calls=%async_computation | async-start | bytes 2097152 | tf_op jit(solution)/shard_map/all_to_all | solution.py:267
  57.2 13.8 %all-to-all-start.1 = ((f32[128,1,256]{2,1,0:T(1,128)}), f32[128,1,256]{2,1,0:T(1,128)S(1)}, u32[]{:S(2)}, u32[]{:S(2)}) async-start(f32[128,1,256]{2,1,0:T(1,128)} %all_to_all.12), calls=%async_computation.1 | async-start | bytes 262144 | tf_op jit(solution)/shard_map/all_to_all | solution.py:296

commit v15 on v14

--- a/solution.py
+++ b/solution.py
@@ -291,7 +291,7 @@
     select_all = (owned_all[:, None, :] & (rank_all[:, None, :] == slot_ids[None, :, None])).astype(
         jnp.float32
     )
-    send = jnp.einsum("nst,twqv->wnsqv", select_all, cross, precision=lax.Precision.HIGHEST)
+    send = jnp.einsum("nst,twqv->wnsqv", select_all, cross, precision=lax.Precision.HIGH)
     send = send.reshape(devices, SLOTS * pair_share * 2 * group)
     arrived = lax.all_to_all(send, ("wide", "narrow"), 0, 0, tiled=True)
     arrived = arrived.reshape(devices, SLOTS * pair_share, 2, group)

time: 73.6 us -> 73.6 us (level)
  no operation moved by 1% of the time
where the time goes in v15:
time: 73.6 us; the launch traced here: 73.4 us
  waiting for transfers between devices  26.6 us (36%)
  starting transfers between devices  15.4 us (21%)
  Pallas kernels  12.7 us (17%)
  local copies, waits for them, and re-layouts  9.16 us (12%)
  matrix products  5.51 us (7%)
  other arithmetic  3.71 us (5%)
    all_to_all x1, waiting for transfers between devices, on_device(): spectra = lax.all_to_all(whitened, ('wide', 'narrow'), 0, 0, tiled=True)  16.9 us
    pallas_call x1, Pallas kernels, decimate_dft(): pl.pallas_call(functools.partial(fused_kernel, dec_steps=dec_steps, halve...  12.7 us
    all_to_all x1, starting transfers between devices, on_device(): spectra = lax.all_to_all(whitened, ('wide', 'narrow'), 0, 0, tiled=True)  11.5 us
    all_to_all x1, waiting for transfers between devices, on_device(): arrived = lax.all_to_all(send, ('wide', 'narrow'), 0, 0, tiled=True)  9.65 us
    all_to_all x1, starting transfers between devices, on_device(): arrived = lax.all_to_all(send, ('wide', 'narrow'), 0, 0, tiled=True)  3.91 us
    dot_general x1, matrix products, whiten(): jnp.dot(magnitude, smoother(NBINS, SMOOTH), precision=lax.Precision.HIGH)  3.78 us
    cos x2, other arithmetic, trig(): return (jnp.cos(angle), jnp.sin(angle))  2.34 us
    all_to_all x2, local copies, waits for them, and re-layouts, on_device(): arrived = lax.all_to_all(send, ('wide', 'narrow'), 0, 0, tiled=True)  2.2 us
  transfers between devices with their start and end apart: 2, of which 2 were waited for; matrix products, arithmetic and copies ran while one was open for 4% of the time, Pallas kernels for 0%

profile of v15, /device:TPU:1, one launch (start us, length us, event | category | flops | bytes accessed | tf_op | source)
XLA Modules:
  0.0 73.4 jit_solution(7251629668098612087)
XLA Ops:
  0.0 0.2 convert_reduce_fusion
  0.2 12.7 %shard_map.82 = f32[256,2048]{1,0:T(8,128)} custom-call(f32[64]{0:T(128)} %taps_ref.1, bf16[8,32,16384]{2,1,0:T(8,128)(2,1)} %x_ref.1, f32[32,1024]{1,0:T(8,128)} %constant.76.clone.c1_ref, f32[32,1024]{1,0:T(8,128)} %constant.77.clone.s1_ref, f32[128,1024]{1,0:T(8,128)} %constant.78.clone.c2_ref, f32[128,1024]{1,0:T(8,128)} %constant.79.clone.s2_ref), custom_call_target="tpu_custom_call" | custom-call | tf_op jit(solution)/shard_map/pallas_call | solution.py:222
  12.9 3.8 %fusion.47 = (f32[256]{0:T(256)S(1)}, f32[256,1024]{1,0:T(8,128)S(1)}) fusion(f32[1024]{0:T(1024)S(1)} %convert_reduce_fusion, f32[256,2048]{1,0:T(8,128)} %shard_map.82), kind=kOutput, calls=%fused_computation.88 | convolution fusion | flops 1616903936 | bytes 3150848 | tf_op jit(solution)/shard_map/dot_general | solution.py:249
  16.7 0.2 add_divide_fusion
  17.0 0.3 fusion.1
  17.3 0.5 copy.38
  17.9 1.1 %copy.61 = bf16[128,2,8,256]{3,2,1,0:T(8,128)(2,1)} copy(bf16[128,2,8,256]{3,2,0,1:T(8,128)(2,1)S(1)} %bitcast.59) | data formatting | bytes 2097152 | tf_op jit(solution)/shard_map/transpose | solution.py:253
  18.9 11.5 %all-to-all-start = ((bf16[128,16,256]{2,1,0:T(8,128)(2,1)}), bf16[128,16,256]{2,1,0:T(8,128)(2,1)S(1)}, u32[]{:S(2)}, u32[]{:S(2)}) async-start(bf16[128,16,256]{2,1,0:T(8,128)(2,1)} %bitcast.57), calls=%async_computation | async-start | bytes 2097152 | tf_op jit(solution)/shard_map/all_to_all | solution.py:267
  30.6 0.2 reduce_window_sum.11
  30.9 2.1 %fusion.27 = (f32[1024,64]{1,0:T(8,128)S(1)}, f32[1024,64]{1,0:T(8,128)S(1)}) fusion(s32[1024]{0:T(1024)S(1)} %iota_add_fusion), kind=kLoop, calls=%fused_computation.53 | loop fusion | flops 983040 | bytes 528384 | tf_op jit(solution)/shard_map/cos | solution.py:76
  33.0 16.9 %all-to-all-done = bf16[128,16,256]{2,1,0:T(8,128)(2,1)S(1)} async-done(((bf16[128,16,256]{2,1,0:T(8,128)(2,1)}), bf16[128,16,256]{2,1,0:T(8,128)(2,1)S(1)}, u32[]{:S(2)}, u32[]{:S(2)}) %all-to-all-start) | async-done | bytes 1048608 | tf_op jit(solution)/shard_map/all_to_all | solution.py:267
  49.9 0.6 gather_fusion
  50.5 0.1 broadcast_select_fusion
  50.6 0.2 squeeze.23
  50.9 0.2 squeeze.20
  51.3 0.4 convolution_bitcast_fusion.2
  51.6 0.4 convolution_bitcast_fusion.1
  52.1 0.7 copy.44
  52.9 0.3 copy.45
  53.2 0.3 convolution_bitcast_fusion
  53.5 1.5 %copy.46 = f32[32,4,8,2,16]{4,3,2,1,0:T(2,128)S(1)} copy(f32[32,4,8,2,16]{0,2,1,4,3:T(8,128)S(1)} %convolution_bitcast_fusion) | data formatting | bytes 262144 | tf_op jit(solution)/shard_map/nst,twqv->wnsqv/transpose | solution.py:294
  55.0 2.1 %all_to_all.12 = f32[128,1,256]{2,1,0:T(1,128)} reshape(f32[32,4,8,2,16]{4,3,2,1,0:T(2,128)S(1)} %copy.46) | data formatting | bytes 262144 | tf_op jit(solution)/shard_map/all_to_all | solution.py:296
  57.1 3.9 %all-to-all-start.1 = ((f32[128,1,256]{2,1,0:T(1,128)}), f32[128,1,256]{2,1,0:T(1,128)S(1)}, u32[]{:S(2)}, u32[]{:S(2)}) async-start(f32[128,1,256]{2,1,0:T(1,128)} %all_to_all.12), calls=%async_computation.1 | async-start | bytes 262144 | tf_op jit(solution)/shard_map/all_to_all | solution.py:296
  61.0 0.2 fusion.32
  61.2 9.7 %all-to-all-done.1 = f32[128,1,256]{2,1,0:T(1,128)S(1)} async-done(((f32[128,1,256]{2,1,0:T(1,128)}), f32[128,1,256]{2,1,0:T(1,128)S(1)}, u32[]{:S(2)}, u32[]{:S(2)}) %all-to-all-start.1) | async-done | bytes 131104 | tf_op jit(solution)/shard_map/all_to_all | solution.py:296
  70.9 0.1 copy.48
  71.0 0.4 copy.49
  71.5 0.2 copy.50
  71.6 0.2 copy.51
  71.8 0.2 subtract_bitcast_fusion
  72.0 0.7 fusion.7
  72.7 0.7 reshape_reshape.3
  (21 shorter events, 0.5 us)
Async XLA Ops:
  12.9 4.0 %copy-start = (f32[256,2048]{1,0:T(8,128)S(1)}, f32[256,2048]{1,0:T(8,128)}, u32[]{:S(2)}) copy-start(f32[256,2048]{1,0:T(8,128)} %shard_map.82) | copy-start | bytes 6291460
  17.3 13.1 %copy-start.1 = (s32[16]{0:T(128)S(1)}, s32[16]{0:T(128)}, u32[]{:S(2)}) copy-start(s32[16]{0:T(128)} %param.11) | copy-start | bytes 196
  17.3 13.1 %copy-start.2 = (s32[16,2]{0,1:T(2,128)S(1)}, s32[16,2]{0,1:T(2,128)}, u32[]{:S(2)}) copy-start(s32[16,2]{0,1:T(2,128)} %param.10) | copy-start | bytes 388
  18.9 31.0 %all-to-all-start = ((bf16[128,16,256]{2,1,0:T(8,128)(2,1)}), bf16[128,16,256]{2,1,0:T(8,128)(2,1)S(1)}, u32[]{:S(2)}, u32[]{:S(2)}) async-start(bf16[128,16,256]{2,1,0:T(8,128)(2,1)} %bitcast.57), calls=%async_computation | async-start | bytes 2097152 | tf_op jit(solution)/shard_map/all_to_all | solution.py:267
  57.1 13.8 %all-to-all-start.1 = ((f32[128,1,256]{2,1,0:T(1,128)}), f32[128,1,256]{2,1,0:T(1,128)S(1)}, u32[]{:S(2)}, u32[]{:S(2)}) async-start(f32[128,1,256]{2,1,0:T(1,128)} %all_to_all.12), calls=%async_computation.1 | async-start | bytes 262144 | tf_op jit(solution)/shard_map/all_to_all | solution.py:296

commit v16 on v14

--- a/solution.py
+++ b/solution.py
@@ -200,7 +200,7 @@
         out_ref[...] = jnp.dot(dec_ref[...], tab_ref[...], preferred_element_type=jnp.float32)
 
 
-def decimate_dft(samples, filter_taps, chunk=8192, block_cols=512):
+def decimate_dft(samples, filter_taps, chunk=8192, block_cols=1024):
     channels, windows, row_length = samples.shape
     block_size = min(128, row_length // DECIM)
     rows = channels * windows

time: 73.6 us -> 73.7 us (level)
  no operation moved by 1% of the time
where the time goes in v16:
time: 73.7 us; the launch traced here: 73.5 us
  waiting for transfers between devices  26.6 us (36%)
  starting transfers between devices  15.4 us (21%)
  Pallas kernels  12.8 us (17%)
  local copies, waits for them, and re-layouts  9.16 us (12%)
  matrix products  5.59 us (8%)
  other arithmetic  3.71 us (5%)
    all_to_all x1, waiting for transfers between devices, on_device(): spectra = lax.all_to_all(whitened, ('wide', 'narrow'), 0, 0, tiled=True)  16.9 us
    pallas_call x1, Pallas kernels, decimate_dft(): pl.pallas_call(functools.partial(fused_kernel, dec_steps=dec_steps, halve...  12.8 us
    all_to_all x1, starting transfers between devices, on_device(): spectra = lax.all_to_all(whitened, ('wide', 'narrow'), 0, 0, tiled=True)  11.5 us
    all_to_all x1, waiting for transfers between devices, on_device(): arrived = lax.all_to_all(send, ('wide', 'narrow'), 0, 0, tiled=True)  9.65 us
    all_to_all x1, starting transfers between devices, on_device(): arrived = lax.all_to_all(send, ('wide', 'narrow'), 0, 0, tiled=True)  3.9 us
    dot_general x1, matrix products, whiten(): jnp.dot(magnitude, smoother(NBINS, SMOOTH), precision=lax.Precision.HIGH)  3.78 us
    cos x2, other arithmetic, trig(): return (jnp.cos(angle), jnp.sin(angle))  2.34 us
    all_to_all x2, local copies, waits for them, and re-layouts, on_device(): arrived = lax.all_to_all(send, ('wide', 'narrow'), 0, 0, tiled=True)  2.2 us
  transfers between devices with their start and end apart: 2, of which 2 were waited for; matrix products, arithmetic and copies ran while one was open for 4% of the time, Pallas kernels for 0%

profile of v16, /device:TPU:1, one launch (start us, length us, event | category | flops | bytes accessed | tf_op | source)
XLA Modules:
  0.0 73.5 jit_solution(937223375767602212)
XLA Ops:
  0.0 0.2 convert_reduce_fusion
  0.2 12.8 %shard_map.82 = f32[256,2048]{1,0:T(8,128)} custom-call(f32[64]{0:T(128)} %taps_ref.1, bf16[8,32,16384]{2,1,0:T(8,128)(2,1)} %x_ref.1, f32[32,1024]{1,0:T(8,128)} %constant.76.clone.c1_ref, f32[32,1024]{1,0:T(8,128)} %constant.77.clone.s1_ref, f32[128,1024]{1,0:T(8,128)} %constant.78.clone.c2_ref, f32[128,1024]{1,0:T(8,128)} %constant.79.clone.s2_ref), custom_call_target="tpu_custom_call" | custom-call | tf_op jit(solution)/shard_map/pallas_call | solution.py:222
  13.0 3.8 %fusion.47 = (f32[256]{0:T(256)S(1)}, f32[256,1024]{1,0:T(8,128)S(1)}) fusion(f32[1024]{0:T(1024)S(1)} %convert_reduce_fusion, f32[256,2048]{1,0:T(8,128)} %shard_map.82), kind=kOutput, calls=%fused_computation.88 | convolution fusion | flops 1616903936 | bytes 3150848 | tf_op jit(solution)/shard_map/dot_general | solution.py:249
  16.8 0.2 add_divide_fusion
  17.0 0.3 fusion.1
  17.4 0.5 copy.38
  17.9 1.1 %copy.61 = bf16[128,2,8,256]{3,2,1,0:T(8,128)(2,1)} copy(bf16[128,2,8,256]{3,2,0,1:T(8,128)(2,1)S(1)} %bitcast.59) | data formatting | bytes 2097152 | tf_op jit(solution)/shard_map/transpose | solution.py:253
  19.0 11.5 %all-to-all-start = ((bf16[128,16,256]{2,1,0:T(8,128)(2,1)}), bf16[128,16,256]{2,1,0:T(8,128)(2,1)S(1)}, u32[]{:S(2)}, u32[]{:S(2)}) async-start(bf16[128,16,256]{2,1,0:T(8,128)(2,1)} %bitcast.57), calls=%async_computation | async-start | bytes 2097152 | tf_op jit(solution)/shard_map/all_to_all | solution.py:267
  30.7 0.2 reduce_window_sum.11
  30.9 2.1 %fusion.27 = (f32[1024,64]{1,0:T(8,128)S(1)}, f32[1024,64]{1,0:T(8,128)S(1)}) fusion(s32[1024]{0:T(1024)S(1)} %iota_add_fusion), kind=kLoop, calls=%fused_computation.53 | loop fusion | flops 983040 | bytes 528384 | tf_op jit(solution)/shard_map/cos | solution.py:76
  33.0 16.9 %all-to-all-done = bf16[128,16,256]{2,1,0:T(8,128)(2,1)S(1)} async-done(((bf16[128,16,256]{2,1,0:T(8,128)(2,1)}), bf16[128,16,256]{2,1,0:T(8,128)(2,1)S(1)}, u32[]{:S(2)}, u32[]{:S(2)}) %all-to-all-start) | async-done | bytes 1048608 | tf_op jit(solution)/shard_map/all_to_all | solution.py:267
  50.0 0.6 gather_fusion
  50.6 0.1 broadcast_select_fusion
  50.7 0.2 squeeze.23
  50.9 0.2 squeeze.20
  51.3 0.4 convolution_bitcast_fusion.2
  51.7 0.4 convolution_bitcast_fusion.1
  52.2 0.7 copy.44
  52.9 0.3 copy.45
  53.2 0.4 convolution_bitcast_fusion
  53.6 1.5 %copy.46 = f32[32,4,8,2,16]{4,3,2,1,0:T(2,128)S(1)} copy(f32[32,4,8,2,16]{0,2,1,4,3:T(8,128)S(1)} %convolution_bitcast_fusion) | data formatting | bytes 262144 | tf_op jit(solution)/shard_map/nst,twqv->wnsqv/transpose | solution.py:294
  55.1 2.1 %all_to_all.12 = f32[128,1,256]{2,1,0:T(1,128)} reshape(f32[32,4,8,2,16]{4,3,2,1,0:T(2,128)S(1)} %copy.46) | data formatting | bytes 262144 | tf_op jit(solution)/shard_map/all_to_all | solution.py:296
  57.2 3.9 %all-to-all-start.1 = ((f32[128,1,256]{2,1,0:T(1,128)}), f32[128,1,256]{2,1,0:T(1,128)S(1)}, u32[]{:S(2)}, u32[]{:S(2)}) async-start(f32[128,1,256]{2,1,0:T(1,128)} %all_to_all.12), calls=%async_computation.1 | async-start | bytes 262144 | tf_op jit(solution)/shard_map/all_to_all | solution.py:296
  61.1 0.2 fusion.32
  61.3 9.7 %all-to-all-done.1 = f32[128,1,256]{2,1,0:T(1,128)S(1)} async-done(((f32[128,1,256]{2,1,0:T(1,128)}), f32[128,1,256]{2,1,0:T(1,128)S(1)}, u32[]{:S(2)}, u32[]{:S(2)}) %all-to-all-start.1) | async-done | bytes 131104 | tf_op jit(solution)/shard_map/all_to_all | solution.py:296
  71.0 0.1 copy.48
  71.1 0.4 copy.49
  71.6 0.2 copy.50
  71.8 0.2 copy.51
  71.9 0.2 subtract_bitcast_fusion
  72.1 0.7 fusion.7
  72.8 0.7 reshape_reshape.3
  (21 shorter events, 0.5 us)
Async XLA Ops:
  13.0 4.0 %copy-start = (f32[256,2048]{1,0:T(8,128)S(1)}, f32[256,2048]{1,0:T(8,128)}, u32[]{:S(2)}) copy-start(f32[256,2048]{1,0:T(8,128)} %shard_map.82) | copy-start | bytes 6291460
  17.4 13.1 %copy-start.1 = (s32[16]{0:T(128)S(1)}, s32[16]{0:T(128)}, u32[]{:S(2)}) copy-start(s32[16]{0:T(128)} %param.11) | copy-start | bytes 196
  17.4 13.1 %copy-start.2 = (s32[16,2]{0,1:T(2,128)S(1)}, s32[16,2]{0,1:T(2,128)}, u32[]{:S(2)}) copy-start(s32[16,2]{0,1:T(2,128)} %param.10) | copy-start | bytes 388
  19.0 31.0 %all-to-all-start = ((bf16[128,16,256]{2,1,0:T(8,128)(2,1)}), bf16[128,16,256]{2,1,0:T(8,128)(2,1)S(1)}, u32[]{:S(2)}, u32[]{:S(2)}) async-start(bf16[128,16,256]{2,1,0:T(8,128)(2,1)} %bitcast.57), calls=%async_computation | async-start | bytes 2097152 | tf_op jit(solution)/shard_map/all_to_all | solution.py:267
  57.2 13.8 %all-to-all-start.1 = ((f32[128,1,256]{2,1,0:T(1,128)}), f32[128,1,256]{2,1,0:T(1,128)S(1)}, u32[]{:S(2)}, u32[]{:S(2)}) async-start(f32[128,1,256]{2,1,0:T(1,128)} %all_to_all.12), calls=%async_computation.1 | async-start | bytes 262144 | tf_op jit(solution)/shard_map/all_to_all | solution.py:296
